TPU v7x, 512 devices: a whole 4x8x8 slice. The times are simulated.
512 devices in a mesh: row: 8 (over x, y_lo), col: 8 (over y_hi, core), smp: 8 (over z).
Axes of the slice: x: 4, y: 8 (y_hi: 4, y_lo: 2; y = y_hi * 2 + y_lo), z: 8, core: 2. Of those that a mesh axis runs over, the one named last changes fastest.
Arguments:
- single: bfloat16 [1024, 768], P('row'), may hold values from -0.59765625 to 0.59765625
- pair_features: bfloat16 [1024, 1024, 128], P('row', ('col', 'smp')), may hold values from -6 to 6
- coords: float32 [3, 8192], replicated, may hold values from -6 to 6
- token_centre_atom: int32 [1024], P('row'), may hold values from 0 to 8191
- chain_label: int32 [1024], P('row'), may hold values from 0 to 7, never falling along the last dimension, each value on 1 to 256 neighbouring positions
- padding_key_mask: int32 [1024], P('row'), may hold values 0 or 1
- angles: float32 [8, 3], P('smp'), may hold values from -3.140625 to 3.140625
- sample_noise_level: float32 [8], P('smp'), may hold values from 0.05 to 10
- centre_noise: float32 [8, 3, 1024], P('smp', None, 'row'), may hold values from -6 to 6
- embedding_weight: float32 [4, 768], replicated, may hold values from -1.5 to 1.5
- pair_bias_weight: bfloat16 [128, 4, 16], replicated, may hold values from -1 to 1
- same_chain_offset: float32 [4, 16], replicated, may hold values from -300 to 300
- query_key_value_gate_weight: bfloat16 [4, 4, 768, 768], P(None, None, 'col'), may hold values from -0.21875 to 0.21875
- attention_output_weight: bfloat16 [4, 768, 768], P(None, 'col'), may hold values from -1.25 to 1.25
- position_update_weight: bfloat16 [3, 768], replicated, may hold values from -0.21875 to 0.21875
Outputs:
- tokens_out: bfloat16 [8, 1024, 768], P('smp', 'row')
- denoised: float32 [8, 3, 1024], P('smp', None, 'row')
All inputs are finite; a program needn't handle non-finite values. No bound on the sum of `padding_key_mask` on one device may be relied on, other than what follows from the above.
Results may differ from a plain program's by a relative error of at most 0.024.
Values may be sent and summed in bfloat16 or wider, within the bound.
No kernel may reach another device: no remote copies, remote signals or barrier semaphores. Data moves between devices by JAX's collectives and lax.ppermute only.
A program may use at most 64 MiB of HBM per device.

v0:
```python
import jax
import jax.numpy as jnp
from jax import lax
from jax.sharding import PartitionSpec as P

EPSILON = 1e-05
MASKED = -1000000000.0
LOWEST = -1e30


def layer_norm(inputs):
    average = jnp.mean(inputs, axis=-1, keepdims=True)
    centred = inputs - average
    spread = jnp.mean(centred * centred, axis=-1, keepdims=True)
    return centred * lax.rsqrt(spread + EPSILON)


def rotation_rows(angles):
    cos_a = jnp.cos(angles[:, 0])
    sin_a = jnp.sin(angles[:, 0])
    cos_b = jnp.cos(angles[:, 1])
    sin_b = jnp.sin(angles[:, 1])
    cos_c = jnp.cos(angles[:, 2])
    sin_c = jnp.sin(angles[:, 2])
    first = jnp.stack(
        [
            cos_a * cos_b,
            cos_a * sin_b * sin_c - sin_a * cos_c,
            cos_a * sin_b * cos_c + sin_a * sin_c,
        ],
        axis=-1,
    )
    second = jnp.stack(
        [
            sin_a * cos_b,
            sin_a * sin_b * sin_c + cos_a * cos_c,
            sin_a * sin_b * cos_c - cos_a * sin_c,
        ],
        axis=-1,
    )
    third = jnp.stack([-sin_b, cos_b * sin_c, cos_b * cos_c], axis=-1)
    return jnp.stack([first, second, third], axis=1)


def noisy_centres(coords, token_centre_atom, angles, sample_noise_level, centre_noise):
    centre = jnp.take(coords, token_centre_atom, axis=1)
    rotation = rotation_rows(angles)
    turned = rotation[:, :, 0, None] * centre[0][None, None, :]
    turned = turned + rotation[:, :, 1, None] * centre[1][None, None, :]
    turned = turned + rotation[:, :, 2, None] * centre[2][None, None, :]
    return turned + sample_noise_level[:, None, None] * centre_noise


def embed_tokens(single, noisy, sample_noise_level, embedding_weight):
    scaled = noisy / jnp.sqrt(sample_noise_level * sample_noise_level + 1.0)[:, None, None]
    log_level = 0.25 * jnp.log(sample_noise_level)
    hidden_activity = single.astype(jnp.float32)[None] + scaled[:, 0, :, None] * embedding_weight[0]
    hidden_activity = hidden_activity + scaled[:, 1, :, None] * embedding_weight[1]
    hidden_activity = hidden_activity + scaled[:, 2, :, None] * embedding_weight[2]
    hidden_activity = hidden_activity + log_level[:, None, None] * embedding_weight[3]
    return hidden_activity.astype(jnp.bfloat16)


def relay_bias(local_bias):
    blocks, total_heads, row_count, keys_dev = local_bias.shape
    col_count = lax.axis_size("col")
    copies = lax.axis_size("smp")
    group_members = total_heads // col_count
    spread = jnp.broadcast_to(
        local_bias.reshape(blocks, col_count, 1, group_members, row_count, 1, keys_dev),
        (blocks, col_count, copies, group_members, row_count, 1, keys_dev),
    )
    spread = spread.reshape(blocks, col_count * copies * group_members, row_count, 1, keys_dev)
    relayed = lax.all_to_all(spread, ("col", "smp"), split_axis=1, concat_axis=3, tiled=True)
    return relayed.reshape(blocks, group_members, row_count, -1)


def build_absorber(
    query_vectors,
    per_block_bias,
    chain_offset,
    query_chain_labels,
    gathered_chain_ids,
    gathered_key_mask,
    input_scaling,
):
    samples, row_count, group_members, head_size = query_vectors.shape

    def absorb(running, kv_piece, key_start):
        key_count = kv_piece.shape[0]
        key_rows = kv_piece[:, :, 0].reshape(key_count, samples, group_members, head_size)
        value_rows = kv_piece[:, :, 1].reshape(key_count, samples, group_members, head_size)
        attention_logits = (
            jnp.einsum(
                "sqhd,kshd->shqk", query_vectors, key_rows, preferred_element_type=jnp.float32
            )
            * input_scaling
        )
        bias_section = per_block_bias.astype(jnp.float32)
        chain_match = (query_chain_labels[:, None] == gathered_chain_ids[None, :]).astype(
            jnp.float32
        )
        attention_logits = (
            attention_logits
            + bias_section[None]
            + chain_offset[None, :, None, None] * chain_match[None, None]
        )
        attention_logits = jnp.where(
            gathered_key_mask[None, None, None, :] > 0, attention_logits, MASKED
        )
        old_max, old_sum, old_acc = running
        new_max = jnp.maximum(old_max, jnp.max(attention_logits, axis=-1))
        unscaled = jnp.exp(attention_logits - new_max[..., None])
        new_sum = jnp.sum(unscaled, axis=-1)
        new_acc = jnp.einsum(
            "shqk,kshd->shqd",
            unscaled.astype(jnp.bfloat16),
            value_rows,
            preferred_element_type=jnp.float32,
        )
        return (new_max, new_sum, new_acc)

    return absorb


def body(
    single,
    pair_features,
    coords,
    token_centre_atom,
    chain_label,
    padding_key_mask,
    angles,
    sample_noise_level,
    centre_noise,
    embedding_weight,
    pair_bias_weight,
    same_chain_offset,
    query_key_value_gate_weight,
    attention_output_weight,
    position_update_weight,
):
    noisy = noisy_centres(coords, token_centre_atom, angles, sample_noise_level, centre_noise)
    hidden_activity = embed_tokens(single, noisy, sample_noise_level, embedding_weight)
    pair_normed = layer_norm(pair_features.astype(jnp.float32)).astype(jnp.bfloat16)
    local_bias = jnp.einsum(
        "ikc,cbh->bhik", pair_normed, pair_bias_weight, preferred_element_type=jnp.float32
    ).astype(jnp.bfloat16)
    gathered_pair_bias = relay_bias(local_bias)
    gathered_chain_ids, gathered_key_mask = (
        lax.all_gather(chain_label, "row", axis=0, tiled=True),
        lax.all_gather(padding_key_mask, "row", axis=0, tiled=True),
    )
    samples, row_count, model_width = hidden_activity.shape
    group_members = gathered_pair_bias.shape[1]
    head_size = query_key_value_gate_weight.shape[2] // group_members
    group_offset = lax.axis_index("col") * group_members
    input_scaling = head_size ** (-0.5)
    for block_index in range(query_key_value_gate_weight.shape[0]):
        normed = layer_norm(hidden_activity.astype(jnp.float32)).astype(jnp.bfloat16)
        front = jnp.einsum(
            "snd,fed->fsne",
            normed,
            query_key_value_gate_weight[block_index, 0:2],
            preferred_element_type=jnp.float32,
        )
        key_value = jnp.einsum(
            "snd,fed->nsfe",
            normed,
            query_key_value_gate_weight[block_index, 2:4],
            preferred_element_type=jnp.float32,
        ).astype(jnp.bfloat16)
        query_vectors = (
            front[0].astype(jnp.bfloat16).reshape(samples, row_count, group_members, head_size)
        )
        chain_offset = lax.dynamic_slice_in_dim(
            same_chain_offset[block_index], group_offset, group_members, 0
        )
        absorb = build_absorber(
            query_vectors,
            gathered_pair_bias[block_index],
            chain_offset,
            chain_label,
            gathered_chain_ids,
            gathered_key_mask,
            input_scaling,
        )
        start_state = (
            jnp.full((samples, group_members, row_count), LOWEST, jnp.float32),
            jnp.zeros((samples, group_members, row_count), jnp.float32),
            jnp.zeros((samples, group_members, row_count, head_size), jnp.float32),
        )
        final_max, final_sum, final_acc = absorb(
            start_state, lax.all_gather(key_value, "row", axis=0, tiled=True), jnp.int32(0)
        )
        attended = final_acc / final_sum[..., None]
        attended = jnp.transpose(attended, (0, 2, 1, 3)).reshape(
            samples, row_count, group_members * head_size
        )
        gated_output = (jax.nn.sigmoid(front[1]) * attended).astype(jnp.bfloat16)
        partial_out = jnp.einsum(
            "kxp,pj->kxj",
            gated_output,
            attention_output_weight[block_index],
            preferred_element_type=jnp.float32,
        )
        summed = lax.psum(partial_out.astype(jnp.bfloat16), "col").astype(jnp.float32)
        hidden_activity = (hidden_activity.astype(jnp.float32) + summed).astype(jnp.bfloat16)
    final_normed = layer_norm(hidden_activity.astype(jnp.float32)).astype(jnp.bfloat16)
    update = jnp.einsum(
        "snd,cd->scn", final_normed, position_update_weight, preferred_element_type=jnp.float32
    )
    spread_sq = 1.0 + sample_noise_level * sample_noise_level
    denoised = (
        noisy / spread_sq[:, None, None]
        + (sample_noise_level / jnp.sqrt(spread_sq))[:, None, None] * update
    )
    return (hidden_activity, denoised)


def solution(mesh):
    return jax.shard_map(
        body,
        mesh=mesh,
        in_specs=(
            P("row", None),
            P("row", ("col", "smp"), None),
            P(),
            P("row"),
            P("row"),
            P("row"),
            P("smp", None),
            P("smp"),
            P("smp", None, "row"),
            P(),
            P(),
            P(),
            P(None, None, "col", None),
            P(None, "col", None),
            P(),
        ),
        out_specs=(P("smp", "row", None), P("smp", None, "row")),
        check_vma=False,
    )
```

profile of v0, /device:TPU:19, one launch (start us, length us, event | category | flops | bytes accessed | tf_op | source)
XLA Modules:
  0.0 548.1 jit_solution(17188569693350493762)
XLA Ops:
  7.2 1.4 convert_reduce_fusion
  8.6 1.7 fusion.36
  10.3 1.6 fusion.50
  12.4 1.9 broadcast_in_dim.47
  14.3 16.9 %all-to-all-start = ((bf16[4,128,128,1,16]{2,4,3,0,1:T(8,128)(2,1)}), bf16[4,128,128,1,16]{2,4,3,0,1:T(8,128)(2,1)S(1)}, u32[]{:S(2)}, u32[]{:S(2)}) async-start(bf16[4,128,128,1,16]{2,4,3,0,1:T(8,128)(2,1)} %bitcast.262), calls=%async_computation | async-start | bytes 4194304 | tf_op jit(solution)/shard_map/all_to_all | solution.py:74
  36.9 2.6 copy.35
  39.5 2.8 gather_fusion
  43.7 1.3 convolution_bitcast_fusion.3
  45.0 39.0 %all-gather.1 = s32[8,1,128]{2,1,0:T(1,128)S(1)} all-gather(s32[1,1,128]{2,1,0:T(1,128)S(1)} %bitcast.290), channel_id=1, replica_groups=mesh['row'=8,'col'=8,'smp'=8] {'row'}, dimensions={0}, use_global_device_ids=true | all-gather | bytes 4608 | tf_op jit(solution)/shard_map/all_gather | solution.py:151
  84.0 11.5 %all-gather = s32[8,1,128]{2,1,0:T(1,128)S(1)} all-gather(s32[1,1,128]{2,1,0:T(1,128)S(1)} %bitcast.291), channel_id=1, replica_groups=mesh['row'=8,'col'=8,'smp'=8] {'row'}, dimensions={0}, use_global_device_ids=true | all-gather | bytes 4608 | tf_op jit(solution)/shard_map/all_gather | solution.py:152
  95.6 1.3 fusion.22
  96.8 22.6 %all_gather.19 = bf16[1024,1,2,96]{0,3,2,1:T(8,128)(2,1)S(1)} all-gather(bf16[128,1,2,96]{0,3,2,1:T(8,128)(2,1)S(1)} %fusion.22), channel_id=1, replica_groups=mesh['row'=8,'col'=8,'smp'=8] {'row'}, dimensions={0}, use_global_device_ids=true | all-gather | bytes 442368 | tf_op jit(solution)/shard_map/all_gather | solution.py:194
  120.0 1.9 slice_convert_fusion
  121.9 1.3 copy.42
  123.3 1.7 fusion.150
  125.7 1.8 fusion.14
  127.6 1.3 copy.43
  128.9 1.4 copy.44
  130.3 86.6 %all-reduce.5.cloned.1.call-done = bf16[1,128,768]{2,1,0:T(8,128)(2,1)} async-done(((bf16[1,128,768]{2,1,0:T(8,128)(2,1)}), bf16[1,128,768]{2,1,0:T(8,128)(2,1)}) %all-reduce.5.cloned.1.call-update) | async-done | bytes 196624 | tf_op jit(solution)/shard_map/psum | solution.py:207
  218.1 1.3 fusion.23
  220.7 20.5 %all_gather.21 = bf16[1024,1,2,96]{0,3,2,1:T(8,128)(2,1)S(1)} all-gather(bf16[128,1,2,96]{0,3,2,1:T(8,128)(2,1)S(1)} %fusion.23), channel_id=1, replica_groups=mesh['row'=8,'col'=8,'smp'=8] {'row'}, dimensions={0}, use_global_device_ids=true | all-gather | bytes 442368 | tf_op jit(solution)/shard_map/all_gather | solution.py:194
  242.5 1.8 fusion.15
  244.5 1.3 copy.45
  245.8 1.3 copy.46
  247.1 77.9 %all-reduce.7.cloned.1.call-done = bf16[1,128,768]{2,1,0:T(8,128)(2,1)} async-done(((bf16[1,128,768]{2,1,0:T(8,128)(2,1)}), bf16[1,128,768]{2,1,0:T(8,128)(2,1)}) %all-reduce.7.cloned.1.call-update) | async-done | bytes 196624 | tf_op jit(solution)/shard_map/psum | solution.py:207
  326.3 1.3 fusion.24
  327.6 1.3 convolution_bitcast_fusion.1
  328.9 20.5 %all_gather.22 = bf16[1024,1,2,96]{0,3,2,1:T(8,128)(2,1)S(1)} all-gather(bf16[128,1,2,96]{0,3,2,1:T(8,128)(2,1)S(1)} %fusion.24), channel_id=1, replica_groups=mesh['row'=8,'col'=8,'smp'=8] {'row'}, dimensions={0}, use_global_device_ids=true | all-gather | bytes 442368 | tf_op jit(solution)/shard_map/all_gather | solution.py:194
  352.3 79.9 %all-reduce.9.cloned.1.call-done = bf16[1,128,768]{2,1,0:T(8,128)(2,1)} async-done(((bf16[1,128,768]{2,1,0:T(8,128)(2,1)}), bf16[1,128,768]{2,1,0:T(8,128)(2,1)}) %all-reduce.9.cloned.1.call-update) | async-done | bytes 196624 | tf_op jit(solution)/shard_map/psum | solution.py:207
  433.5 1.3 fusion.25
  436.1 20.5 %all_gather.23 = bf16[1024,1,2,96]{0,3,2,1:T(8,128)(2,1)S(1)} all-gather(bf16[128,1,2,96]{0,3,2,1:T(8,128)(2,1)S(1)} %fusion.25), channel_id=1, replica_groups=mesh['row'=8,'col'=8,'smp'=8] {'row'}, dimensions={0}, use_global_device_ids=true | all-gather | bytes 442368 | tf_op jit(solution)/shard_map/all_gather | solution.py:194
  458.8 80.6 %all-reduce.11.cloned.1.call-done = bf16[1,128,768]{2,1,0:T(8,128)(2,1)} async-done(((bf16[1,128,768]{2,1,0:T(8,128)(2,1)}), bf16[1,128,768]{2,1,0:T(8,128)(2,1)}) %all-reduce.11.cloned.1.call-update) | async-done | bytes 196624 | tf_op jit(solution)/shard_map/psum | solution.py:207
  (118 shorter events, 18.7 us)
Async XLA Ops:
  7.2 4.8 copy-start
  14.3 17.0 %copy-start.8 = (f32[1,3]{1,0:T(1,128)S(1)}, f32[1,3]{1,0:T(1,128)}, u32[]{:S(2)}) copy-start(f32[1,3]{1,0:T(1,128)} %param.21) | copy-start | bytes 40
  14.3 17.6 %copy-start.14 = (s32[128]{0:T(128)S(1)}, s32[128]{0:T(128)}, u32[]{:S(2)}) copy-start(s32[128]{0:T(128)} %param.18) | copy-start | bytes 1540
  14.3 22.5 %copy-start.6 = (f32[3,8192]{1,0:T(4,128)S(1)}, f32[3,8192]{1,0:T(4,128)}, u32[]{:S(2)}) copy-start(f32[3,8192]{1,0:T(4,128)} %param.17) | copy-start | bytes 294916
  14.3 105.3 %all-to-all-start = ((bf16[4,128,128,1,16]{2,4,3,0,1:T(8,128)(2,1)}), bf16[4,128,128,1,16]{2,4,3,0,1:T(8,128)(2,1)S(1)}, u32[]{:S(2)}, u32[]{:S(2)}) async-start(bf16[4,128,128,1,16]{2,4,3,0,1:T(8,128)(2,1)} %bitcast.262), calls=%async_computation | async-start | bytes 4194304 | tf_op jit(solution)/shard_map/all_to_all | solution.py:74
  31.3 11.5 %copy-start.7 = (f32[4,768]{1,0:T(4,128)S(1)}, f32[4,768]{1,0:T(4,128)}, u32[]{:S(2)}) copy-start(f32[4,768]{1,0:T(4,128)} %param.24) | copy-start | bytes 36868
  31.3 185.6 %all-reduce.5.cloned.1.call-start = ((), (), s32[]{:S(2)}) async-start(), calls=%async_computation.1 | async-start | bytes 393216 | tf_op jit(solution)/shard_map/psum | solution.py:207
  36.8 6.2 %copy-start.11 = (f32[1,3,128]{2,0,1:T(1,128)S(1)}, f32[1,3,128]{2,0,1:T(1,128)}, u32[]{:S(2)}) copy-start(f32[1,3,128]{2,0,1:T(1,128)} %param.23) | copy-start | bytes 4612
  36.9 6.3 %copy-start.5 = (bf16[128,768]{1,0:T(8,128)(2,1)S(1)}, bf16[128,768]{1,0:T(8,128)(2,1)}, u32[]{:S(2)}) copy-start(bf16[128,768]{1,0:T(8,128)(2,1)} %param.15) | copy-start | bytes 589828
  36.9 8.1 %copy-start.9 = (s32[128]{0:T(128)S(1)}, s32[128]{0:T(128)}, u32[]{:S(2)}) copy-start(s32[128]{0:T(128)} %param.19) | copy-start | bytes 1540
  36.9 47.1 %copy-start.12 = (s32[128]{0:T(128)S(1)}, s32[128]{0:T(128)}, u32[]{:S(2)}) copy-start(s32[128]{0:T(128)} %param.20) | copy-start | bytes 1540
  36.9 58.6 %copy-start.10 = (f32[4,16]{1,0:T(4,128)S(1)}, f32[4,16]{1,0:T(4,128)}, u32[]{:S(2)}) copy-start(f32[4,16]{1,0:T(4,128)} %param.26) | copy-start | bytes 772
  127.5 197.5 %all-reduce.7.cloned.1.call-start = ((), (), s32[]{:S(2)}) async-start(), calls=%async_computation.2 | async-start | bytes 393216 | tf_op jit(solution)/shard_map/psum | solution.py:207
  130.3 111.0 %copy-start.1 = (f32[2,128,1024]{2,1,0:T(8,128)S(1)}, f32[2,128,1024]{2,1,0:T(8,128)}, u32[]{:S(2)}) copy-start(f32[2,128,1024]{2,1,0:T(8,128)} %copy.44) | copy-start | bytes 3145732
  244.3 187.9 %all-reduce.9.cloned.1.call-start = ((), (), s32[]{:S(2)}) async-start(), calls=%async_computation.3 | async-start | bytes 393216 | tf_op jit(solution)/shard_map/psum | solution.py:207
  247.1 102.4 %copy-start.2 = (f32[2,128,1024]{2,1,0:T(8,128)S(1)}, f32[2,128,1024]{2,1,0:T(8,128)}, u32[]{:S(2)}) copy-start(f32[2,128,1024]{2,1,0:T(8,128)} %copy.46) | copy-start | bytes 3145732
  349.5 1.2 copy-start.4
  351.7 187.7 %all-reduce.11.cloned.1.call-start = ((), (), s32[]{:S(2)}) async-start(), calls=%async_computation.4 | async-start | bytes 393216 | tf_op jit(solution)/shard_map/psum | solution.py:207
  457.1 83.6 %copy-start.13 = (bf16[3,768]{1,0:T(4,128)(2,1)S(1)}, bf16[3,768]{1,0:T(4,128)(2,1)}, u32[]{:S(2)}) copy-start(bf16[3,768]{1,0:T(4,128)(2,1)} %param.29) | copy-start | bytes 13828
  540.5 1.1 copy-start.3
Sparse Core Ops, SparseCore 0:
  127.7 89.1 all-reduce.4
  244.4 80.5 all-reduce.6
  351.8 80.4 all-reduce.8
  458.9 80.4 all-reduce.10
where the time goes:
time: 549 us; the launch traced here: 548 us
  waiting for transfers between devices  325 us (59%)
  blocking collectives  135 us (25%)
  matrix products  20.9 us (4%)
  between operations  19.3 us (4%)
  starting transfers between devices  17.3 us (3%)
  local copies, waits for them, and re-layouts  16.9 us (3%)
  other arithmetic  14 us (3%)
    psum x4, waiting for transfers between devices, body(): lax.psum(partial_out.astype(jnp.bfloat16), 'col').astype(jnp.float32)  325 us
    all_gather x4, blocking collectives, body(): lax.all_gather(key_value, 'row', axis=0, tiled=True)  84.1 us
    all_gather x1, blocking collectives, body(): lax.all_gather(chain_label, 'row', axis=0, tiled=True)  39 us
    all_to_all x1, starting transfers between devices, relay_bias(): lax.all_to_all(spread, ('col', 'smp'), split_axis=1, concat_axis=3, tiled...  16.9 us
    all_gather x1, blocking collectives, body(): lax.all_gather(padding_key_mask, 'row', axis=0, tiled=True)  11.5 us
  transfers between devices with their start and end apart: 5, of which 4 were waited for; matrix products, arithmetic and copies ran while one was open for 3% of the time, Pallas kernels for 0%

commit v1 on v0

--- a/solution.py
+++ b/solution.py
@@ -121,6 +121,24 @@
         return (new_max, new_sum, new_acc)
 
     return absorb
+
+
+def gather_by_exchange(piece, axis_name, axis):
+    count = lax.axis_size(axis_name)
+    shape = piece.shape
+    spread = jnp.broadcast_to(
+        jnp.expand_dims(piece, axis), shape[:axis] + (count,) + shape[axis:]
+    )
+    joined = lax.all_to_all(spread, axis_name, axis, axis, tiled=True)
+    return joined.reshape(shape[:axis] + (count * shape[axis],) + shape[axis + 1 :])
+
+
+def scatter_sum_rows(partial, axis_name):
+    samples, row_count, model_width = partial.shape
+    count = lax.axis_size(axis_name)
+    pieces = partial.reshape(samples, count, row_count // count, model_width)
+    arrived = lax.all_to_all(pieces, axis_name, 1, 1, tiled=True)
+    return jnp.sum(arrived.astype(jnp.float32), axis=1)
 
 
 def body(
@@ -142,22 +160,25 @@
 ):
     noisy = noisy_centres(coords, token_centre_atom, angles, sample_noise_level, centre_noise)
     hidden_activity = embed_tokens(single, noisy, sample_noise_level, embedding_weight)
+    key_marks = gather_by_exchange(jnp.stack([chain_label, padding_key_mask]), "row", 1)
+    gathered_chain_ids, gathered_key_mask = key_marks[0], key_marks[1]
     pair_normed = layer_norm(pair_features.astype(jnp.float32)).astype(jnp.bfloat16)
     local_bias = jnp.einsum(
         "ikc,cbh->bhik", pair_normed, pair_bias_weight, preferred_element_type=jnp.float32
     ).astype(jnp.bfloat16)
     gathered_pair_bias = relay_bias(local_bias)
-    gathered_chain_ids, gathered_key_mask = (
-        lax.all_gather(chain_label, "row", axis=0, tiled=True),
-        lax.all_gather(padding_key_mask, "row", axis=0, tiled=True),
-    )
     samples, row_count, model_width = hidden_activity.shape
+    col_count = lax.axis_size("col")
+    own_rows = row_count // col_count
+    own_start = lax.axis_index("col") * own_rows
+    own_hidden = lax.dynamic_slice_in_dim(hidden_activity, own_start, own_rows, 1)
+    normed = layer_norm(hidden_activity.astype(jnp.float32)).astype(jnp.bfloat16)
     group_members = gathered_pair_bias.shape[1]
     head_size = query_key_value_gate_weight.shape[2] // group_members
     group_offset = lax.axis_index("col") * group_members
     input_scaling = head_size ** (-0.5)
-    for block_index in range(query_key_value_gate_weight.shape[0]):
-        normed = layer_norm(hidden_activity.astype(jnp.float32)).astype(jnp.bfloat16)
+    block_count = query_key_value_gate_weight.shape[0]
+    for block_index in range(block_count):
         front = jnp.einsum(
             "snd,fed->fsne",
             normed,
@@ -191,7 +212,7 @@
             jnp.zeros((samples, group_members, row_count, head_size), jnp.float32),
         )
         final_max, final_sum, final_acc = absorb(
-            start_state, lax.all_gather(key_value, "row", axis=0, tiled=True), jnp.int32(0)
+            start_state, gather_by_exchange(key_value, "row", 0), jnp.int32(0)
         )
         attended = final_acc / final_sum[..., None]
         attended = jnp.transpose(attended, (0, 2, 1, 3)).reshape(
@@ -203,9 +224,13 @@
             gated_output,
             attention_output_weight[block_index],
             preferred_element_type=jnp.float32,
-        )
-        summed = lax.psum(partial_out.astype(jnp.bfloat16), "col").astype(jnp.float32)
-        hidden_activity = (hidden_activity.astype(jnp.float32) + summed).astype(jnp.bfloat16)
+        ).astype(jnp.bfloat16)
+        summed = scatter_sum_rows(partial_out, "col")
+        own_hidden = (own_hidden.astype(jnp.float32) + summed).astype(jnp.bfloat16)
+        if block_index + 1 < block_count:
+            own_normed = layer_norm(own_hidden.astype(jnp.float32)).astype(jnp.bfloat16)
+            normed = gather_by_exchange(own_normed, "col", 1)
+    hidden_activity = gather_by_exchange(own_hidden, "col", 1)
     final_normed = layer_norm(hidden_activity.astype(jnp.float32)).astype(jnp.bfloat16)
     update = jnp.einsum(
         "snd,cd->scn", final_normed, position_update_weight, preferred_element_type=jnp.float32

time: 549 us -> 283 us (0.52)
  the two profiles are of different devices: /device:TPU:19 before, /device:TPU:8 now
where the time goes in v1:
time: 283 us; the launch traced here: 282 us
  waiting for transfers between devices  85 us (30%)
  blocking collectives  80 us (28%)
  starting transfers between devices  56.4 us (20%)
  local copies, waits for them, and re-layouts  24.2 us (9%)
  matrix products  20.3 us (7%)
  other arithmetic  9.57 us (3%)
  between operations  6.32 us (2%)
    all_to_all x1, waiting for transfers between devices, relay_bias(): lax.all_to_all(spread, ('col', 'smp'), split_axis=1, concat_axis=3, tiled...  47.4 us
    all_to_all x3, blocking collectives, scatter_sum_rows(): arrived = lax.all_to_all(pieces, axis_name, 1, 1, tiled=True)  40.9 us
    all_to_all x3, blocking collectives, gather_by_exchange(): joined = lax.all_to_all(spread, axis_name, axis, axis, tiled=True)  39.1 us
    all_to_all x6, starting transfers between devices, gather_by_exchange(): joined = lax.all_to_all(spread, axis_name, axis, axis, tiled=True)  35.7 us
    all_to_all x6, waiting for transfers between devices, gather_by_exchange(): joined = lax.all_to_all(spread, axis_name, axis, axis, tiled=True)  27.2 us
    all_to_all x1, starting transfers between devices, relay_bias(): lax.all_to_all(spread, ('col', 'smp'), split_axis=1, concat_axis=3, tiled...  12.6 us
    all_to_all x1, waiting for transfers between devices, scatter_sum_rows(): arrived = lax.all_to_all(pieces, axis_name, 1, 1, tiled=True)  10.3 us
    all_to_all x1, starting transfers between devices, scatter_sum_rows(): arrived = lax.all_to_all(pieces, axis_name, 1, 1, tiled=True)  8.1 us
  transfers between devices with their start and end apart: 8, of which 7 were waited for; matrix products, arithmetic and copies ran while one was open for 9% of the time, Pallas kernels for 0%

profile of v1, /device:TPU:8, one launch (start us, length us, event | category | flops | bytes accessed | tf_op | source)
XLA Modules:
  0.0 281.8 jit_solution(3463227946874302716)
XLA Ops:
  1.9 9.1 %all-to-all-start = ((s32[2,8,128]{2,0,1:T(2,128)}), s32[2,8,128]{2,0,1:T(2,128)S(1)}, u32[]{:S(2)}, u32[]{:S(2)}) async-start(s32[2,8,128]{2,0,1:T(2,128)} %broadcast_in_dim.63), calls=%async_computation | async-start | bytes 16384 | tf_op jit(solution)/shard_map/all_to_all | solution.py:132
  11.0 1.4 fusion.123
  19.2 3.5 %copy.53 = f32[3,8192]{0,1:T(8,128)} copy(f32[3,8192]{1,0:T(4,128)} %param.17) | data formatting | bytes 196608 | tf_op args[2]
  22.7 2.8 %gather_fusion = f32[128,3]{1,0:T(8,128)S(1)} fusion(f32[3,8192]{0,1:T(8,128)} %copy.53, s32[1024]{0:T(1024)S(1)} %pad_clamp_fusion), kind=kCustom, calls=%fused_computation | custom fusion | bytes 3584 | tf_op jit(solution)/shard_map/jit(_take)/gather | solution.py:46
  29.5 5.7 %all-to-all-start.1 = ((bf16[8,128,1,2,96]{1,4,3,2,0:T(8,128)(2,1)}), bf16[8,128,1,2,96]{1,4,3,2,0:T(8,128)(2,1)S(1)}, u32[]{:S(2)}, u32[]{:S(2)}) async-start(bf16[8,128,1,2,96]{1,4,3,2,0:T(8,128)(2,1)} %broadcast_in_dim.65), calls=%async_computation.1 | async-start | bytes 786432 | tf_op jit(solution)/shard_map/all_to_all | solution.py:132
  36.4 5.7 %all-to-all-done.1 = bf16[8,128,1,2,96]{1,4,3,2,0:T(8,128)(2,1)S(1)} async-done(((bf16[8,128,1,2,96]{1,4,3,2,0:T(8,128)(2,1)}), bf16[8,128,1,2,96]{1,4,3,2,0:T(8,128)(2,1)S(1)}, u32[]{:S(2)}, u32[]{:S(2)}) %all-to-all-start.1) | async-done | bytes 393248 | tf_op jit(solution)/shard_map/all_to_all | solution.py:132
  42.1 1.9 broadcast_in_dim.67
  44.0 12.6 %all-to-all-start.2 = ((bf16[4,128,128,1,16]{2,4,3,0,1:T(8,128)(2,1)}), bf16[4,128,128,1,16]{2,4,3,0,1:T(8,128)(2,1)S(1)}, u32[]{:S(2)}, u32[]{:S(2)}) async-start(bf16[4,128,128,1,16]{2,4,3,0,1:T(8,128)(2,1)} %bitcast.260), calls=%async_computation.2 | async-start | bytes 4194304 | tf_op jit(solution)/shard_map/all_to_all | solution.py:74
  58.3 47.4 %all-to-all-done.2 = bf16[4,128,128,1,16]{2,4,3,0,1:T(8,128)(2,1)S(1)} async-done(((bf16[4,128,128,1,16]{2,4,3,0,1:T(8,128)(2,1)}), bf16[4,128,128,1,16]{2,4,3,0,1:T(8,128)(2,1)S(1)}, u32[]{:S(2)}, u32[]{:S(2)}) %all-to-all-start.2) | async-done | bytes 2097184 | tf_op jit(solution)/shard_map/all_to_all | solution.py:74
  106.1 1.9 slice_convert_fusion
  108.0 1.3 copy.61
  109.3 1.7 fusion.124
  111.7 1.8 convolution_convert_fusion.4
  113.6 8.1 %all-to-all-start.3 = ((bf16[1,8,16,768]{3,2,0,1:T(8,128)(2,1)}), bf16[1,8,16,768]{3,2,0,1:T(8,128)(2,1)S(1)}, u32[]{:S(2)}, u32[]{:S(2)}) async-start(bf16[1,8,16,768]{3,2,0,1:T(8,128)(2,1)} %bitcast.55), calls=%async_computation.3 | async-start | bytes 393216 | tf_op jit(solution)/shard_map/all_to_all | solution.py:140
  121.7 10.3 %all-to-all-done.3 = bf16[1,8,16,768]{3,2,0,1:T(8,128)(2,1)S(1)} async-done(((bf16[1,8,16,768]{3,2,0,1:T(8,128)(2,1)}), bf16[1,8,16,768]{3,2,0,1:T(8,128)(2,1)S(1)}, u32[]{:S(2)}, u32[]{:S(2)}) %all-to-all-start.3) | async-done | bytes 196640 | tf_op jit(solution)/shard_map/all_to_all | solution.py:140
  132.4 12.7 %all_to_all.80 = bf16[1,8,16,768]{3,2,0,1:T(8,128)(2,1)S(1)} all-to-all(bf16[1,8,16,768]{3,2,0,1:T(8,128)(2,1)S(1)} %broadcast_in_dim.70), channel_id=1, replica_groups=mesh['row'=8,'col'=8,'smp'=8] {'col'}, dimensions={1} | all-to-all | bytes 393216 | tf_op jit(solution)/shard_map/all_to_all | solution.py:132
  147.2 8.3 %all-to-all-start.5 = ((bf16[8,128,1,2,96]{1,4,3,2,0:T(8,128)(2,1)}), bf16[8,128,1,2,96]{1,4,3,2,0:T(8,128)(2,1)S(1)}, u32[]{:S(2)}, u32[]{:S(2)}) async-start(bf16[8,128,1,2,96]{1,4,3,2,0:T(8,128)(2,1)} %broadcast_in_dim.71), calls=%async_computation.5 | async-start | bytes 786432 | tf_op jit(solution)/shard_map/all_to_all | solution.py:132
  156.8 1.4 copy.65
  159.5 2.8 %all-to-all-done.5 = bf16[8,128,1,2,96]{1,4,3,2,0:T(8,128)(2,1)S(1)} async-done(((bf16[8,128,1,2,96]{1,4,3,2,0:T(8,128)(2,1)}), bf16[8,128,1,2,96]{1,4,3,2,0:T(8,128)(2,1)S(1)}, u32[]{:S(2)}, u32[]{:S(2)}) %all-to-all-start.5) | async-done | bytes 393248 | tf_op jit(solution)/shard_map/all_to_all | solution.py:132
  164.8 13.6 %all_to_all.81 = bf16[1,8,16,768]{3,2,0,1:T(8,128)(2,1)S(1)} all-to-all(bf16[1,8,16,768]{3,2,0,1:T(8,128)(2,1)S(1)} %bitcast.272), channel_id=1, replica_groups=mesh['row'=8,'col'=8,'smp'=8] {'col'}, dimensions={1} | all-to-all | bytes 393216 | tf_op jit(solution)/shard_map/all_to_all | solution.py:140
  178.9 13.2 %all_to_all.82 = bf16[1,8,16,768]{3,2,0,1:T(8,128)(2,1)S(1)} all-to-all(bf16[1,8,16,768]{3,2,0,1:T(8,128)(2,1)S(1)} %broadcast_in_dim.72), channel_id=1, replica_groups=mesh['row'=8,'col'=8,'smp'=8] {'col'}, dimensions={1} | all-to-all | bytes 393216 | tf_op jit(solution)/shard_map/all_to_all | solution.py:132
  194.1 4.6 %all-to-all-start.8 = ((bf16[8,128,1,2,96]{1,4,3,2,0:T(8,128)(2,1)}), bf16[8,128,1,2,96]{1,4,3,2,0:T(8,128)(2,1)S(1)}, u32[]{:S(2)}, u32[]{:S(2)}) async-start(bf16[8,128,1,2,96]{1,4,3,2,0:T(8,128)(2,1)} %broadcast_in_dim.73), calls=%async_computation.8 | async-start | bytes 786432 | tf_op jit(solution)/shard_map/all_to_all | solution.py:132
  198.8 1.3 copy.68
  200.1 1.3 copy.69
  202.7 2.8 all-to-all-done.8
  208.0 13.6 %all_to_all.83 = bf16[1,8,16,768]{3,2,0,1:T(8,128)(2,1)S(1)} all-to-all(bf16[1,8,16,768]{3,2,0,1:T(8,128)(2,1)S(1)} %bitcast.273), channel_id=1, replica_groups=mesh['row'=8,'col'=8,'smp'=8] {'col'}, dimensions={1} | all-to-all | bytes 393216 | tf_op jit(solution)/shard_map/all_to_all | solution.py:140
  222.1 13.2 %all_to_all.84 = bf16[1,8,16,768]{3,2,0,1:T(8,128)(2,1)S(1)} all-to-all(bf16[1,8,16,768]{3,2,0,1:T(8,128)(2,1)S(1)} %broadcast_in_dim.74), channel_id=1, replica_groups=mesh['row'=8,'col'=8,'smp'=8] {'col'}, dimensions={1} | all-to-all | bytes 393216 | tf_op jit(solution)/shard_map/all_to_all | solution.py:132
  237.3 4.6 %all-to-all-start.11 = ((bf16[8,128,1,2,96]{1,4,3,2,0:T(8,128)(2,1)}), bf16[8,128,1,2,96]{1,4,3,2,0:T(8,128)(2,1)S(1)}, u32[]{:S(2)}, u32[]{:S(2)}) async-start(bf16[8,128,1,2,96]{1,4,3,2,0:T(8,128)(2,1)} %broadcast_in_dim.75), calls=%async_computation.11 | async-start | bytes 786432 | tf_op jit(solution)/shard_map/all_to_all | solution.py:132
  243.6 5.2 %all-to-all-done.11 = bf16[8,128,1,2,96]{1,4,3,2,0:T(8,128)(2,1)S(1)} async-done(((bf16[8,128,1,2,96]{1,4,3,2,0:T(8,128)(2,1)}), bf16[8,128,1,2,96]{1,4,3,2,0:T(8,128)(2,1)S(1)}, u32[]{:S(2)}, u32[]{:S(2)}) %all-to-all-start.11) | async-done | bytes 393248 | tf_op jit(solution)/shard_map/all_to_all | solution.py:132
  251.2 13.6 %all_to_all.85 = bf16[1,8,16,768]{3,2,0,1:T(8,128)(2,1)S(1)} all-to-all(bf16[1,8,16,768]{3,2,0,1:T(8,128)(2,1)S(1)} %bitcast.274), channel_id=1, replica_groups=mesh['row'=8,'col'=8,'smp'=8] {'col'}, dimensions={1} | all-to-all | bytes 393216 | tf_op jit(solution)/shard_map/all_to_all | solution.py:140
  265.6 3.4 %all-to-all-start.13 = ((bf16[1,8,16,768]{3,2,0,1:T(8,128)(2,1)}), bf16[1,8,16,768]{3,2,0,1:T(8,128)(2,1)S(1)}, u32[]{:S(2)}, u32[]{:S(2)}) async-start(bf16[1,8,16,768]{3,2,0,1:T(8,128)(2,1)} %broadcast_in_dim.76), calls=%async_computation.13 | async-start | bytes 393216 | tf_op jit(solution)/shard_map/all_to_all | solution.py:132
  269.0 10.7 %all-to-all-done.13 = bf16[1,8,16,768]{3,2,0,1:T(8,128)(2,1)S(1)} async-done(((bf16[1,8,16,768]{3,2,0,1:T(8,128)(2,1)}), bf16[1,8,16,768]{3,2,0,1:T(8,128)(2,1)S(1)}, u32[]{:S(2)}, u32[]{:S(2)}) %all-to-all-start.13) | async-done | bytes 196640 | tf_op jit(solution)/shard_map/all_to_all | solution.py:132
  (136 shorter events, 33.7 us)
Async XLA Ops:
  0.6 35.3 %copy-start = (bf16[128,4,16]{0,2,1:T(8,128)(2,1)S(1)}, bf16[128,4,16]{0,2,1:T(8,128)(2,1)}, u32[]{:S(2)}) copy-start(bf16[128,4,16]{0,2,1:T(8,128)(2,1)} %param.25) | copy-start | bytes 49156
  1.9 26.8 %all-to-all-start = ((s32[2,8,128]{2,0,1:T(2,128)}), s32[2,8,128]{2,0,1:T(2,128)S(1)}, u32[]{:S(2)}, u32[]{:S(2)}) async-start(s32[2,8,128]{2,0,1:T(2,128)} %broadcast_in_dim.63), calls=%async_computation | async-start | bytes 16384 | tf_op jit(solution)/shard_map/all_to_all | solution.py:132
  18.8 7.0 %copy-start.9 = (f32[1,3,128]{2,0,1:T(1,128)S(1)}, f32[1,3,128]{2,0,1:T(1,128)}, u32[]{:S(2)}) copy-start(f32[1,3,128]{2,0,1:T(1,128)} %param.23) | copy-start | bytes 4612
  19.1 6.8 %copy-start.5 = (f32[4,768]{1,0:T(4,128)S(1)}, f32[4,768]{1,0:T(4,128)}, u32[]{:S(2)}) copy-start(f32[4,768]{1,0:T(4,128)} %param.24) | copy-start | bytes 36868
  19.1 6.8 %copy-start.4 = (bf16[128,768]{1,0:T(8,128)(2,1)S(1)}, bf16[128,768]{1,0:T(8,128)(2,1)}, u32[]{:S(2)}) copy-start(bf16[128,768]{1,0:T(8,128)(2,1)} %param.15) | copy-start | bytes 589828
  19.1 7.3 %copy-start.1 = (bf16[128,16,128]{2,1,0:T(8,128)(2,1)S(1)}, bf16[128,16,128]{2,1,0:T(8,128)(2,1)}, u32[]{:S(2)}) copy-start(bf16[128,16,128]{2,1,0:T(8,128)(2,1)} %param.16) | copy-start | bytes 1572868
  29.5 12.6 %all-to-all-start.1 = ((bf16[8,128,1,2,96]{1,4,3,2,0:T(8,128)(2,1)}), bf16[8,128,1,2,96]{1,4,3,2,0:T(8,128)(2,1)S(1)}, u32[]{:S(2)}, u32[]{:S(2)}) async-start(bf16[8,128,1,2,96]{1,4,3,2,0:T(8,128)(2,1)} %broadcast_in_dim.65), calls=%async_computation.1 | async-start | bytes 786432 | tf_op jit(solution)/shard_map/all_to_all | solution.py:132
  44.0 13.9 %copy-start.8 = (f32[4,16]{1,0:T(4,128)S(1)}, f32[4,16]{1,0:T(4,128)}, u32[]{:S(2)}) copy-start(f32[4,16]{1,0:T(4,128)} %param.26) | copy-start | bytes 772
  44.0 14.1 %copy-start.7 = (s32[128]{0:T(128)S(1)}, s32[128]{0:T(128)}, u32[]{:S(2)}) copy-start(s32[128]{0:T(128)} %param.19) | copy-start | bytes 1540
  44.0 61.7 %all-to-all-start.2 = ((bf16[4,128,128,1,16]{2,4,3,0,1:T(8,128)(2,1)}), bf16[4,128,128,1,16]{2,4,3,0,1:T(8,128)(2,1)S(1)}, u32[]{:S(2)}, u32[]{:S(2)}) async-start(bf16[4,128,128,1,16]{2,4,3,0,1:T(8,128)(2,1)} %bitcast.260), calls=%async_computation.2 | async-start | bytes 4194304 | tf_op jit(solution)/shard_map/all_to_all | solution.py:74
  113.6 18.4 %all-to-all-start.3 = ((bf16[1,8,16,768]{3,2,0,1:T(8,128)(2,1)}), bf16[1,8,16,768]{3,2,0,1:T(8,128)(2,1)S(1)}, u32[]{:S(2)}, u32[]{:S(2)}) async-start(bf16[1,8,16,768]{3,2,0,1:T(8,128)(2,1)} %bitcast.55), calls=%async_computation.3 | async-start | bytes 393216 | tf_op jit(solution)/shard_map/all_to_all | solution.py:140
  147.2 15.2 %all-to-all-start.5 = ((bf16[8,128,1,2,96]{1,4,3,2,0:T(8,128)(2,1)}), bf16[8,128,1,2,96]{1,4,3,2,0:T(8,128)(2,1)S(1)}, u32[]{:S(2)}, u32[]{:S(2)}) async-start(bf16[8,128,1,2,96]{1,4,3,2,0:T(8,128)(2,1)} %broadcast_in_dim.71), calls=%async_computation.5 | async-start | bytes 786432 | tf_op jit(solution)/shard_map/all_to_all | solution.py:132
  158.2 4.3 %copy-start.2 = (f32[2,128,1024]{2,1,0:T(8,128)S(1)}, f32[2,128,1024]{2,1,0:T(8,128)}, u32[]{:S(2)}) copy-start(f32[2,128,1024]{2,1,0:T(8,128)} %copy.65) | copy-start | bytes 3145732
  194.1 11.4 %all-to-all-start.8 = ((bf16[8,128,1,2,96]{1,4,3,2,0:T(8,128)(2,1)}), bf16[8,128,1,2,96]{1,4,3,2,0:T(8,128)(2,1)S(1)}, u32[]{:S(2)}, u32[]{:S(2)}) async-start(bf16[8,128,1,2,96]{1,4,3,2,0:T(8,128)(2,1)} %broadcast_in_dim.73), calls=%async_computation.8 | async-start | bytes 786432 | tf_op jit(solution)/shard_map/all_to_all | solution.py:132
  201.4 4.2 %copy-start.3 = (f32[2,128,1024]{2,1,0:T(8,128)S(1)}, f32[2,128,1024]{2,1,0:T(8,128)}, u32[]{:S(2)}) copy-start(f32[2,128,1024]{2,1,0:T(8,128)} %copy.69) | copy-start | bytes 3145732
  237.3 11.4 %all-to-all-start.11 = ((bf16[8,128,1,2,96]{1,4,3,2,0:T(8,128)(2,1)}), bf16[8,128,1,2,96]{1,4,3,2,0:T(8,128)(2,1)S(1)}, u32[]{:S(2)}, u32[]{:S(2)}) async-start(bf16[8,128,1,2,96]{1,4,3,2,0:T(8,128)(2,1)} %broadcast_in_dim.75), calls=%async_computation.11 | async-start | bytes 786432 | tf_op jit(solution)/shard_map/all_to_all | solution.py:132
  249.4 31.0 %copy-start.6 = (bf16[3,768]{1,0:T(4,128)(2,1)S(1)}, bf16[3,768]{1,0:T(4,128)(2,1)}, u32[]{:S(2)}) copy-start(bf16[3,768]{1,0:T(4,128)(2,1)} %param.29) | copy-start | bytes 13828
  265.6 14.2 %all-to-all-start.13 = ((bf16[1,8,16,768]{3,2,0,1:T(8,128)(2,1)}), bf16[1,8,16,768]{3,2,0,1:T(8,128)(2,1)S(1)}, u32[]{:S(2)}, u32[]{:S(2)}) async-start(bf16[1,8,16,768]{3,2,0,1:T(8,128)(2,1)} %broadcast_in_dim.76), calls=%async_computation.13 | async-start | bytes 393216 | tf_op jit(solution)/shard_map/all_to_all | solution.py:132

commit v2 on v1

--- a/solution.py
+++ b/solution.py
@@ -191,6 +191,10 @@
             query_key_value_gate_weight[block_index, 2:4],
             preferred_element_type=jnp.float32,
         ).astype(jnp.bfloat16)
+        if block_index == 0:
+            key_value, gathered_pair_bias = lax.optimization_barrier(
+                (key_value, gathered_pair_bias)
+            )
         query_vectors = (
             front[0].astype(jnp.bfloat16).reshape(samples, row_count, group_members, head_size)
         )

time: 283 us -> 270 us (0.954)
  starting transfers between devices: 56.4 us -> 50.3 us
  local copies, waits for them, and re-layouts: 24.2 us -> 18.4 us
    all_to_all x1, waiting for transfers between devices: 47.4 us -> 39.3 us  [relay_bias(): lax.all_to_all(spread, ('col', 'smp'), split_axis=1, concat_axis=3, tiled...]
    all_to_all x6, starting transfers between devices: 35.7 us -> 28.5 us  [gather_by_exchange(): joined = lax.all_to_all(spread, axis_name, axis, axis, tiled=True)]
    convert_element_type x8 -> x0, local copies, waits for them, and re-layouts: 7.1 us -> none  [absorb(): bias_section = per_block_bias.astype(jnp.float32)]
    all_to_all x6, waiting for transfers between devices: 27.2 us -> 34.1 us  [gather_by_exchange(): joined = lax.all_to_all(spread, axis_name, axis, axis, tiled=True)]
    dot_general x4, matrix products: 5.27 us -> 1.63 us  [body(): jnp.einsum('kxp,pj->kxj', gated_output, attention_output_weight[block_ind...]
    all_to_all x1, starting transfers between devices: 12.6 us -> 15.8 us  [relay_bias(): lax.all_to_all(spread, ('col', 'smp'), split_axis=1, concat_axis=3, tiled...]
    dot_general x4, matrix products: 3.21 us -> 6.3 us  [absorb(): jnp.einsum('sqhd,kshd->shqk', query_vectors, key_rows, preferred_element_...]
  transfers between devices with their start and end apart: 8 -> 8, of which waited for: 7 -> 8; matrix products, arithmetic and copies ran while one was open for 9% -> 6% of each run, Pallas kernels for 0% -> 0%
where the time goes in v2:
time: 270 us; the launch traced here: 268 us
  waiting for transfers between devices  84.7 us (31%)
  blocking collectives  80.1 us (30%)
  starting transfers between devices  50.3 us (19%)
  matrix products  19.6 us (7%)
  local copies, waits for them, and re-layouts  18.4 us (7%)
  other arithmetic  8.87 us (3%)
  between operations  6.23 us (2%)
    all_to_all x3, blocking collectives, scatter_sum_rows(): arrived = lax.all_to_all(pieces, axis_name, 1, 1, tiled=True)  40.9 us
    all_to_all x1, waiting for transfers between devices, relay_bias(): lax.all_to_all(spread, ('col', 'smp'), split_axis=1, concat_axis=3, tiled...  39.3 us
    all_to_all x3, blocking collectives, gather_by_exchange(): joined = lax.all_to_all(spread, axis_name, axis, axis, tiled=True)  39.2 us
    all_to_all x6, waiting for transfers between devices, gather_by_exchange(): joined = lax.all_to_all(spread, axis_name, axis, axis, tiled=True)  34.1 us
    all_to_all x6, starting transfers between devices, gather_by_exchange(): joined = lax.all_to_all(spread, axis_name, axis, axis, tiled=True)  28.5 us
    all_to_all x1, starting transfers between devices, relay_bias(): lax.all_to_all(spread, ('col', 'smp'), split_axis=1, concat_axis=3, tiled...  15.8 us
    all_to_all x1, waiting for transfers between devices, scatter_sum_rows(): arrived = lax.all_to_all(pieces, axis_name, 1, 1, tiled=True)  11.3 us
    dot_general x4, matrix products, absorb(): jnp.einsum('sqhd,kshd->shqk', query_vectors, key_rows, preferred_element_...  6.3 us
  transfers between devices with their start and end apart: 8, of which 8 were waited for; matrix products, arithmetic and copies ran while one was open for 6% of the time, Pallas kernels for 0%

profile of v2, /device:TPU:8, one launch (start us, length us, event | category | flops | bytes accessed | tf_op | source)
XLA Modules:
  0.0 268.2 jit_solution(2940311782049883961)
XLA Ops:
  2.1 1.7 fusion.29
  3.8 1.6 fusion.43
  5.9 1.9 broadcast_in_dim.68
  7.8 15.8 %all-to-all-start.1 = ((bf16[4,128,128,1,16]{2,4,3,0,1:T(8,128)(2,1)}), bf16[4,128,128,1,16]{2,4,3,0,1:T(8,128)(2,1)S(1)}, u32[]{:S(2)}, u32[]{:S(2)}) async-start(bf16[4,128,128,1,16]{2,4,3,0,1:T(8,128)(2,1)} %bitcast.283), calls=%async_computation.1 | async-start | bytes 4194304 | tf_op jit(solution)/shard_map/all_to_all | solution.py:74
  29.2 2.6 copy.47
  31.8 2.8 %gather_fusion = f32[128,3]{1,0:T(8,128)S(1)} fusion(f32[3,8192]{0,1:T(8,128)} %copy.47, s32[1024]{0:T(1024)S(1)} %pad_clamp_fusion), kind=kCustom, calls=%fused_computation | custom fusion | bytes 3584 | tf_op jit(solution)/shard_map/jit(_take)/gather | solution.py:46
  37.3 39.3 %all-to-all-done.1 = bf16[4,128,128,1,16]{2,4,3,0,1:T(8,128)(2,1)S(1)} async-done(((bf16[4,128,128,1,16]{2,4,3,0,1:T(8,128)(2,1)}), bf16[4,128,128,1,16]{2,4,3,0,1:T(8,128)(2,1)S(1)}, u32[]{:S(2)}, u32[]{:S(2)}) %all-to-all-start.1) | async-done | bytes 2097184 | tf_op jit(solution)/shard_map/all_to_all | solution.py:74
  77.2 6.0 %all-to-all-start = ((s32[2,8,128]{2,0,1:T(2,128)}), s32[2,8,128]{2,0,1:T(2,128)S(1)}, u32[]{:S(2)}, u32[]{:S(2)}) async-start(s32[2,8,128]{2,0,1:T(2,128)} %broadcast_in_dim.65), calls=%async_computation | async-start | bytes 16384 | tf_op jit(solution)/shard_map/all_to_all | solution.py:132
  85.3 2.7 %all-to-all-done = s32[2,8,128]{2,0,1:T(2,128)S(1)} async-done(((s32[2,8,128]{2,0,1:T(2,128)}), s32[2,8,128]{2,0,1:T(2,128)S(1)}, u32[]{:S(2)}, u32[]{:S(2)}) %all-to-all-start) | async-done | bytes 8224 | tf_op jit(solution)/shard_map/all_to_all | solution.py:132
  88.8 4.8 %all-to-all-start.2 = ((bf16[8,128,1,2,96]{1,4,3,2,0:T(8,128)(2,1)}), bf16[8,128,1,2,96]{1,4,3,2,0:T(8,128)(2,1)S(1)}, u32[]{:S(2)}, u32[]{:S(2)}) async-start(bf16[8,128,1,2,96]{1,4,3,2,0:T(8,128)(2,1)} %broadcast_in_dim.71), calls=%async_computation.2 | async-start | bytes 786432 | tf_op jit(solution)/shard_map/all_to_all | solution.py:132
  93.8 2.7 %copy.55 = bf16[4,2,128,1024]{3,2,1,0:T(8,128)(2,1)} copy(bf16[4,2,128,1024]{2,3,1,0:T(8,128)(2,1)S(1)} %bitcast.284) | data formatting | bytes 4194304 | tf_op jit(solution)/shard_map/optimization_barrier | solution.py:195
  96.5 4.0 %all-to-all-done.2 = bf16[8,128,1,2,96]{1,4,3,2,0:T(8,128)(2,1)S(1)} async-done(((bf16[8,128,1,2,96]{1,4,3,2,0:T(8,128)(2,1)}), bf16[8,128,1,2,96]{1,4,3,2,0:T(8,128)(2,1)S(1)}, u32[]{:S(2)}, u32[]{:S(2)}) %all-to-all-start.2) | async-done | bytes 393248 | tf_op jit(solution)/shard_map/all_to_all | solution.py:132
  100.6 1.6 fusion.125
  103.9 6.0 %all-to-all-start.3 = ((bf16[1,8,16,768]{3,2,0,1:T(8,128)(2,1)}), bf16[1,8,16,768]{3,2,0,1:T(8,128)(2,1)S(1)}, u32[]{:S(2)}, u32[]{:S(2)}) async-start(bf16[1,8,16,768]{3,2,0,1:T(8,128)(2,1)} %bitcast.60), calls=%async_computation.3 | async-start | bytes 393216 | tf_op jit(solution)/shard_map/all_to_all | solution.py:140
  109.8 11.3 %all-to-all-done.3 = bf16[1,8,16,768]{3,2,0,1:T(8,128)(2,1)S(1)} async-done(((bf16[1,8,16,768]{3,2,0,1:T(8,128)(2,1)}), bf16[1,8,16,768]{3,2,0,1:T(8,128)(2,1)S(1)}, u32[]{:S(2)}, u32[]{:S(2)}) %all-to-all-start.3) | async-done | bytes 196640 | tf_op jit(solution)/shard_map/all_to_all | solution.py:140
  121.6 13.3 %all_to_all.80 = bf16[1,8,16,768]{3,2,0,1:T(8,128)(2,1)S(1)} all-to-all(bf16[1,8,16,768]{3,2,0,1:T(8,128)(2,1)S(1)} %broadcast_in_dim.73), channel_id=1, replica_groups=mesh['row'=8,'col'=8,'smp'=8] {'col'}, dimensions={1} | all-to-all | bytes 393216 | tf_op jit(solution)/shard_map/all_to_all | solution.py:132
  136.9 4.6 %all-to-all-start.5 = ((bf16[8,128,1,2,96]{1,4,3,2,0:T(8,128)(2,1)}), bf16[8,128,1,2,96]{1,4,3,2,0:T(8,128)(2,1)S(1)}, u32[]{:S(2)}, u32[]{:S(2)}) async-start(bf16[8,128,1,2,96]{1,4,3,2,0:T(8,128)(2,1)} %broadcast_in_dim.74), calls=%async_computation.5 | async-start | bytes 786432 | tf_op jit(solution)/shard_map/all_to_all | solution.py:132
  142.8 5.6 %all-to-all-done.5 = bf16[8,128,1,2,96]{1,4,3,2,0:T(8,128)(2,1)S(1)} async-done(((bf16[8,128,1,2,96]{1,4,3,2,0:T(8,128)(2,1)}), bf16[8,128,1,2,96]{1,4,3,2,0:T(8,128)(2,1)S(1)}, u32[]{:S(2)}, u32[]{:S(2)}) %all-to-all-start.5) | async-done | bytes 393248 | tf_op jit(solution)/shard_map/all_to_all | solution.py:132
  148.5 1.6 fusion.126
  151.0 13.6 %all_to_all.81 = bf16[1,8,16,768]{3,2,0,1:T(8,128)(2,1)S(1)} all-to-all(bf16[1,8,16,768]{3,2,0,1:T(8,128)(2,1)S(1)} %bitcast.293), channel_id=1, replica_groups=mesh['row'=8,'col'=8,'smp'=8] {'col'}, dimensions={1} | all-to-all | bytes 393216 | tf_op jit(solution)/shard_map/all_to_all | solution.py:140
  165.1 12.7 %all_to_all.82 = bf16[1,8,16,768]{3,2,0,1:T(8,128)(2,1)S(1)} all-to-all(bf16[1,8,16,768]{3,2,0,1:T(8,128)(2,1)S(1)} %broadcast_in_dim.75), channel_id=1, replica_groups=mesh['row'=8,'col'=8,'smp'=8] {'col'}, dimensions={1} | all-to-all | bytes 393216 | tf_op jit(solution)/shard_map/all_to_all | solution.py:132
  179.7 5.1 %all-to-all-start.8 = ((bf16[8,128,1,2,96]{1,4,3,2,0:T(8,128)(2,1)}), bf16[8,128,1,2,96]{1,4,3,2,0:T(8,128)(2,1)S(1)}, u32[]{:S(2)}, u32[]{:S(2)}) async-start(bf16[8,128,1,2,96]{1,4,3,2,0:T(8,128)(2,1)} %broadcast_in_dim.76), calls=%async_computation.8 | async-start | bytes 786432 | tf_op jit(solution)/shard_map/all_to_all | solution.py:132
  186.2 5.5 %all-to-all-done.8 = bf16[8,128,1,2,96]{1,4,3,2,0:T(8,128)(2,1)S(1)} async-done(((bf16[8,128,1,2,96]{1,4,3,2,0:T(8,128)(2,1)}), bf16[8,128,1,2,96]{1,4,3,2,0:T(8,128)(2,1)S(1)}, u32[]{:S(2)}, u32[]{:S(2)}) %all-to-all-start.8) | async-done | bytes 393248 | tf_op jit(solution)/shard_map/all_to_all | solution.py:132
  191.8 1.6 fusion.127
  194.3 13.6 %all_to_all.83 = bf16[1,8,16,768]{3,2,0,1:T(8,128)(2,1)S(1)} all-to-all(bf16[1,8,16,768]{3,2,0,1:T(8,128)(2,1)S(1)} %bitcast.294), channel_id=1, replica_groups=mesh['row'=8,'col'=8,'smp'=8] {'col'}, dimensions={1} | all-to-all | bytes 393216 | tf_op jit(solution)/shard_map/all_to_all | solution.py:140
  208.4 13.2 %all_to_all.84 = bf16[1,8,16,768]{3,2,0,1:T(8,128)(2,1)S(1)} all-to-all(bf16[1,8,16,768]{3,2,0,1:T(8,128)(2,1)S(1)} %broadcast_in_dim.77), channel_id=1, replica_groups=mesh['row'=8,'col'=8,'smp'=8] {'col'}, dimensions={1} | all-to-all | bytes 393216 | tf_op jit(solution)/shard_map/all_to_all | solution.py:132
  223.6 4.6 %all-to-all-start.11 = ((bf16[8,128,1,2,96]{1,4,3,2,0:T(8,128)(2,1)}), bf16[8,128,1,2,96]{1,4,3,2,0:T(8,128)(2,1)S(1)}, u32[]{:S(2)}, u32[]{:S(2)}) async-start(bf16[8,128,1,2,96]{1,4,3,2,0:T(8,128)(2,1)} %broadcast_in_dim.78), calls=%async_computation.11 | async-start | bytes 786432 | tf_op jit(solution)/shard_map/all_to_all | solution.py:132
  229.5 5.6 %all-to-all-done.11 = bf16[8,128,1,2,96]{1,4,3,2,0:T(8,128)(2,1)S(1)} async-done(((bf16[8,128,1,2,96]{1,4,3,2,0:T(8,128)(2,1)}), bf16[8,128,1,2,96]{1,4,3,2,0:T(8,128)(2,1)S(1)}, u32[]{:S(2)}, u32[]{:S(2)}) %all-to-all-start.11) | async-done | bytes 393248 | tf_op jit(solution)/shard_map/all_to_all | solution.py:132
  235.2 1.6 fusion.128
  237.7 13.6 %all_to_all.85 = bf16[1,8,16,768]{3,2,0,1:T(8,128)(2,1)S(1)} all-to-all(bf16[1,8,16,768]{3,2,0,1:T(8,128)(2,1)S(1)} %bitcast.295), channel_id=1, replica_groups=mesh['row'=8,'col'=8,'smp'=8] {'col'}, dimensions={1} | all-to-all | bytes 393216 | tf_op jit(solution)/shard_map/all_to_all | solution.py:140
  252.0 3.4 %all-to-all-start.13 = ((bf16[1,8,16,768]{3,2,0,1:T(8,128)(2,1)}), bf16[1,8,16,768]{3,2,0,1:T(8,128)(2,1)S(1)}, u32[]{:S(2)}, u32[]{:S(2)}) async-start(bf16[1,8,16,768]{3,2,0,1:T(8,128)(2,1)} %broadcast_in_dim.79), calls=%async_computation.13 | async-start | bytes 393216 | tf_op jit(solution)/shard_map/all_to_all | solution.py:132
  255.5 10.7 %all-to-all-done.13 = bf16[1,8,16,768]{3,2,0,1:T(8,128)(2,1)S(1)} async-done(((bf16[1,8,16,768]{3,2,0,1:T(8,128)(2,1)}), bf16[1,8,16,768]{3,2,0,1:T(8,128)(2,1)S(1)}, u32[]{:S(2)}, u32[]{:S(2)}) %all-to-all-start.13) | async-done | bytes 196640 | tf_op jit(solution)/shard_map/all_to_all | solution.py:132
  (137 shorter events, 27.2 us)
Async XLA Ops:
  0.6 4.8 %copy-start = (bf16[128,4,16]{0,2,1:T(8,128)(2,1)S(1)}, bf16[128,4,16]{0,2,1:T(8,128)(2,1)}, u32[]{:S(2)}) copy-start(bf16[128,4,16]{0,2,1:T(8,128)(2,1)} %param.25) | copy-start | bytes 49156
  7.8 15.8 %copy-start.8 = (f32[1,3]{1,0:T(1,128)S(1)}, f32[1,3]{1,0:T(1,128)}, u32[]{:S(2)}) copy-start(f32[1,3]{1,0:T(1,128)} %param.21) | copy-start | bytes 40
  7.8 21.4 %copy-start.5 = (f32[3,8192]{1,0:T(4,128)S(1)}, f32[3,8192]{1,0:T(4,128)}, u32[]{:S(2)}) copy-start(f32[3,8192]{1,0:T(4,128)} %param.17) | copy-start | bytes 294916
  7.8 68.8 %all-to-all-start.1 = ((bf16[4,128,128,1,16]{2,4,3,0,1:T(8,128)(2,1)}), bf16[4,128,128,1,16]{2,4,3,0,1:T(8,128)(2,1)S(1)}, u32[]{:S(2)}, u32[]{:S(2)}) async-start(bf16[4,128,128,1,16]{2,4,3,0,1:T(8,128)(2,1)} %bitcast.283), calls=%async_computation.1 | async-start | bytes 4194304 | tf_op jit(solution)/shard_map/all_to_all | solution.py:74
  23.6 8.2 %copy-start.13 = (s32[128]{0:T(128)S(1)}, s32[128]{0:T(128)}, u32[]{:S(2)}) copy-start(s32[128]{0:T(128)} %param.18) | copy-start | bytes 1540
  23.6 11.1 %copy-start.9 = (s32[128]{0:T(128)S(1)}, s32[128]{0:T(128)}, u32[]{:S(2)}) copy-start(s32[128]{0:T(128)} %param.19) | copy-start | bytes 1540
  23.6 11.1 %copy-start.12 = (s32[128]{0:T(128)S(1)}, s32[128]{0:T(128)}, u32[]{:S(2)}) copy-start(s32[128]{0:T(128)} %param.20) | copy-start | bytes 1540
  23.6 11.4 %copy-start.6 = (f32[4,768]{1,0:T(4,128)S(1)}, f32[4,768]{1,0:T(4,128)}, u32[]{:S(2)}) copy-start(f32[4,768]{1,0:T(4,128)} %param.24) | copy-start | bytes 36868
  29.2 6.2 %copy-start.11 = (f32[1,3,128]{2,0,1:T(1,128)S(1)}, f32[1,3,128]{2,0,1:T(1,128)}, u32[]{:S(2)}) copy-start(f32[1,3,128]{2,0,1:T(1,128)} %param.23) | copy-start | bytes 4612
  29.2 6.3 %copy-start.4 = (bf16[128,768]{1,0:T(8,128)(2,1)S(1)}, bf16[128,768]{1,0:T(8,128)(2,1)}, u32[]{:S(2)}) copy-start(bf16[128,768]{1,0:T(8,128)(2,1)} %param.15) | copy-start | bytes 589828
  29.2 8.1 %copy-start.10 = (f32[4,16]{1,0:T(4,128)S(1)}, f32[4,16]{1,0:T(4,128)}, u32[]{:S(2)}) copy-start(f32[4,16]{1,0:T(4,128)} %param.26) | copy-start | bytes 772
  77.2 10.8 %all-to-all-start = ((s32[2,8,128]{2,0,1:T(2,128)}), s32[2,8,128]{2,0,1:T(2,128)S(1)}, u32[]{:S(2)}, u32[]{:S(2)}) async-start(s32[2,8,128]{2,0,1:T(2,128)} %broadcast_in_dim.65), calls=%async_computation | async-start | bytes 16384 | tf_op jit(solution)/shard_map/all_to_all | solution.py:132
  88.8 11.7 %all-to-all-start.2 = ((bf16[8,128,1,2,96]{1,4,3,2,0:T(8,128)(2,1)}), bf16[8,128,1,2,96]{1,4,3,2,0:T(8,128)(2,1)S(1)}, u32[]{:S(2)}, u32[]{:S(2)}) async-start(bf16[8,128,1,2,96]{1,4,3,2,0:T(8,128)(2,1)} %broadcast_in_dim.71), calls=%async_computation.2 | async-start | bytes 786432 | tf_op jit(solution)/shard_map/all_to_all | solution.py:132
  93.8 6.8 %copy-start.3 = (f32[128,1024]{1,0:T(8,128)}, f32[128,1024]{1,0:T(8,128)S(1)}, u32[]{:S(2)}) copy-start(f32[128,1024]{1,0:T(8,128)S(1)} %compare_convert_fusion) | copy-start | bytes 1572868
  100.6 2.3 copy-start.2
  103.9 17.2 %all-to-all-start.3 = ((bf16[1,8,16,768]{3,2,0,1:T(8,128)(2,1)}), bf16[1,8,16,768]{3,2,0,1:T(8,128)(2,1)S(1)}, u32[]{:S(2)}, u32[]{:S(2)}) async-start(bf16[1,8,16,768]{3,2,0,1:T(8,128)(2,1)} %bitcast.60), calls=%async_computation.3 | async-start | bytes 393216 | tf_op jit(solution)/shard_map/all_to_all | solution.py:140
  121.5 26.9 %copy-start.1 = (bf16[4,2,128,1024]{3,2,1,0:T(8,128)(2,1)S(1)}, bf16[4,2,128,1024]{3,2,1,0:T(8,128)(2,1)}, u32[]{:S(2)}) copy-start(bf16[4,2,128,1024]{3,2,1,0:T(8,128)(2,1)} %copy.55) | copy-start | bytes 6291460
  136.9 11.5 %all-to-all-start.5 = ((bf16[8,128,1,2,96]{1,4,3,2,0:T(8,128)(2,1)}), bf16[8,128,1,2,96]{1,4,3,2,0:T(8,128)(2,1)S(1)}, u32[]{:S(2)}, u32[]{:S(2)}) async-start(bf16[8,128,1,2,96]{1,4,3,2,0:T(8,128)(2,1)} %broadcast_in_dim.74), calls=%async_computation.5 | async-start | bytes 786432 | tf_op jit(solution)/shard_map/all_to_all | solution.py:132
  179.7 12.0 %all-to-all-start.8 = ((bf16[8,128,1,2,96]{1,4,3,2,0:T(8,128)(2,1)}), bf16[8,128,1,2,96]{1,4,3,2,0:T(8,128)(2,1)S(1)}, u32[]{:S(2)}, u32[]{:S(2)}) async-start(bf16[8,128,1,2,96]{1,4,3,2,0:T(8,128)(2,1)} %broadcast_in_dim.76), calls=%async_computation.8 | async-start | bytes 786432 | tf_op jit(solution)/shard_map/all_to_all | solution.py:132
  223.6 11.4 %all-to-all-start.11 = ((bf16[8,128,1,2,96]{1,4,3,2,0:T(8,128)(2,1)}), bf16[8,128,1,2,96]{1,4,3,2,0:T(8,128)(2,1)S(1)}, u32[]{:S(2)}, u32[]{:S(2)}) async-start(bf16[8,128,1,2,96]{1,4,3,2,0:T(8,128)(2,1)} %broadcast_in_dim.78), calls=%async_computation.11 | async-start | bytes 786432 | tf_op jit(solution)/shard_map/all_to_all | solution.py:132
  236.7 30.0 %copy-start.7 = (bf16[3,768]{1,0:T(4,128)(2,1)S(1)}, bf16[3,768]{1,0:T(4,128)(2,1)}, u32[]{:S(2)}) copy-start(bf16[3,768]{1,0:T(4,128)(2,1)} %param.29) | copy-start | bytes 13828
  252.0 14.2 %all-to-all-start.13 = ((bf16[1,8,16,768]{3,2,0,1:T(8,128)(2,1)}), bf16[1,8,16,768]{3,2,0,1:T(8,128)(2,1)S(1)}, u32[]{:S(2)}, u32[]{:S(2)}) async-start(bf16[1,8,16,768]{3,2,0,1:T(8,128)(2,1)} %broadcast_in_dim.79), calls=%async_computation.13 | async-start | bytes 393216 | tf_op jit(solution)/shard_map/all_to_all | solution.py:132

commit v3 on v2

--- a/solution.py
+++ b/solution.py
@@ -161,12 +161,13 @@
     noisy = noisy_centres(coords, token_centre_atom, angles, sample_noise_level, centre_noise)
     hidden_activity = embed_tokens(single, noisy, sample_noise_level, embedding_weight)
     key_marks = gather_by_exchange(jnp.stack([chain_label, padding_key_mask]), "row", 1)
-    gathered_chain_ids, gathered_key_mask = key_marks[0], key_marks[1]
     pair_normed = layer_norm(pair_features.astype(jnp.float32)).astype(jnp.bfloat16)
     local_bias = jnp.einsum(
         "ikc,cbh->bhik", pair_normed, pair_bias_weight, preferred_element_type=jnp.float32
     ).astype(jnp.bfloat16)
+    local_bias, key_marks = lax.optimization_barrier((local_bias, key_marks))
     gathered_pair_bias = relay_bias(local_bias)
+    gathered_chain_ids, gathered_key_mask = key_marks[0], key_marks[1]
     samples, row_count, model_width = hidden_activity.shape
     col_count = lax.axis_size("col")
     own_rows = row_count // col_count

time: 270 us -> 269 us (level)
  waiting for transfers between devices: 84.7 us -> 79.5 us
    all_to_all x6, starting transfers between devices: 28.5 us -> 35.9 us  [gather_by_exchange(): joined = lax.all_to_all(spread, axis_name, axis, axis, tiled=True)]
    all_to_all x1, waiting for transfers between devices: 39.3 us -> 35.3 us  [relay_bias(): lax.all_to_all(spread, ('col', 'smp'), split_axis=1, concat_axis=3, tiled...]
    all_to_all x1, starting transfers between devices: 15.8 us -> 12.5 us  [relay_bias(): lax.all_to_all(spread, ('col', 'smp'), split_axis=1, concat_axis=3, tiled...]
  transfers between devices with their start and end apart: 8 -> 8, of which waited for: 8 -> 7; matrix products, arithmetic and copies ran while one was open for 6% -> 8% of each run, Pallas kernels for 0% -> 0%
where the time goes in v3:
time: 269 us; the launch traced here: 267 us
  blocking collectives  80.7 us (30%)
  waiting for transfers between devices  79.5 us (30%)
  starting transfers between devices  52.9 us (20%)
  matrix products  19.6 us (7%)
  local copies, waits for them, and re-layouts  18.4 us (7%)
  other arithmetic  9.56 us (4%)
  between operations  6.23 us (2%)
    all_to_all x3, blocking collectives, scatter_sum_rows(): arrived = lax.all_to_all(pieces, axis_name, 1, 1, tiled=True)  40.9 us
    all_to_all x3, blocking collectives, gather_by_exchange(): joined = lax.all_to_all(spread, axis_name, axis, axis, tiled=True)  39.8 us
    all_to_all x6, starting transfers between devices, gather_by_exchange(): joined = lax.all_to_all(spread, axis_name, axis, axis, tiled=True)  35.9 us
    all_to_all x1, waiting for transfers between devices, relay_bias(): lax.all_to_all(spread, ('col', 'smp'), split_axis=1, concat_axis=3, tiled...  35.3 us
    all_to_all x6, waiting for transfers between devices, gather_by_exchange(): joined = lax.all_to_all(spread, axis_name, axis, axis, tiled=True)  33 us
    all_to_all x1, starting transfers between devices, relay_bias(): lax.all_to_all(spread, ('col', 'smp'), split_axis=1, concat_axis=3, tiled...  12.5 us
    all_to_all x1, waiting for transfers between devices, scatter_sum_rows(): arrived = lax.all_to_all(pieces, axis_name, 1, 1, tiled=True)  11.2 us
    dot_general x4, matrix products, absorb(): jnp.einsum('sqhd,kshd->shqk', query_vectors, key_rows, preferred_element_...  6.3 us
  transfers between devices with their start and end apart: 8, of which 7 were waited for; matrix products, arithmetic and copies ran while one was open for 8% of the time, Pallas kernels for 0%

profile of v3, /device:TPU:8, one launch (start us, length us, event | category | flops | bytes accessed | tf_op | source)
XLA Modules:
  0.0 266.9 jit_solution(6403234262256293473)
XLA Ops:
  1.9 9.1 %all-to-all-start = ((s32[2,8,128]{2,0,1:T(2,128)}), s32[2,8,128]{2,0,1:T(2,128)S(1)}, u32[]{:S(2)}, u32[]{:S(2)}) async-start(s32[2,8,128]{2,0,1:T(2,128)} %broadcast_in_dim.65), calls=%async_computation | async-start | bytes 16384 | tf_op jit(solution)/shard_map/all_to_all | solution.py:132
  11.0 1.4 convert_reduce_fusion
  12.4 1.7 fusion.30
  14.1 1.6 fusion.44
  16.3 1.9 broadcast_in_dim.68
  18.1 12.5 %all-to-all-start.1 = ((bf16[4,128,128,1,16]{2,4,3,0,1:T(8,128)(2,1)}), bf16[4,128,128,1,16]{2,4,3,0,1:T(8,128)(2,1)S(1)}, u32[]{:S(2)}, u32[]{:S(2)}) async-start(bf16[4,128,128,1,16]{2,4,3,0,1:T(8,128)(2,1)} %bitcast.281), calls=%async_computation.1 | async-start | bytes 4194304 | tf_op jit(solution)/shard_map/all_to_all | solution.py:74
  36.2 2.6 copy.47
  38.9 2.8 %gather_fusion = f32[128,3]{1,0:T(8,128)S(1)} fusion(f32[3,8192]{0,1:T(8,128)} %copy.47, s32[1024]{0:T(1024)S(1)} %pad_clamp_fusion), kind=kCustom, calls=%fused_computation | custom fusion | bytes 3584 | tf_op jit(solution)/shard_map/jit(_take)/gather | solution.py:46
  45.6 35.3 %all-to-all-done.1 = bf16[4,128,128,1,16]{2,4,3,0,1:T(8,128)(2,1)S(1)} async-done(((bf16[4,128,128,1,16]{2,4,3,0,1:T(8,128)(2,1)}), bf16[4,128,128,1,16]{2,4,3,0,1:T(8,128)(2,1)S(1)}, u32[]{:S(2)}, u32[]{:S(2)}) %all-to-all-start.1) | async-done | bytes 2097184 | tf_op jit(solution)/shard_map/all_to_all | solution.py:74
  82.5 9.7 %all-to-all-start.2 = ((bf16[8,128,1,2,96]{1,4,3,2,0:T(8,128)(2,1)}), bf16[8,128,1,2,96]{1,4,3,2,0:T(8,128)(2,1)S(1)}, u32[]{:S(2)}, u32[]{:S(2)}) async-start(bf16[8,128,1,2,96]{1,4,3,2,0:T(8,128)(2,1)} %broadcast_in_dim.71), calls=%async_computation.2 | async-start | bytes 786432 | tf_op jit(solution)/shard_map/all_to_all | solution.py:132
  92.5 2.7 %copy.54 = bf16[4,2,128,1024]{3,2,1,0:T(8,128)(2,1)} copy(bf16[4,2,128,1024]{2,3,1,0:T(8,128)(2,1)S(1)} %bitcast.282) | data formatting | bytes 4194304 | tf_op jit(solution)/shard_map/optimization_barrier | solution.py:196
  95.2 5.5 %all-to-all-done.2 = bf16[8,128,1,2,96]{1,4,3,2,0:T(8,128)(2,1)S(1)} async-done(((bf16[8,128,1,2,96]{1,4,3,2,0:T(8,128)(2,1)}), bf16[8,128,1,2,96]{1,4,3,2,0:T(8,128)(2,1)S(1)}, u32[]{:S(2)}, u32[]{:S(2)}) %all-to-all-start.2) | async-done | bytes 393248 | tf_op jit(solution)/shard_map/all_to_all | solution.py:132
  100.9 1.6 fusion.125
  104.1 4.5 %all-to-all-start.3 = ((bf16[1,8,16,768]{3,2,0,1:T(8,128)(2,1)}), bf16[1,8,16,768]{3,2,0,1:T(8,128)(2,1)S(1)}, u32[]{:S(2)}, u32[]{:S(2)}) async-start(bf16[1,8,16,768]{3,2,0,1:T(8,128)(2,1)} %bitcast.60), calls=%async_computation.3 | async-start | bytes 393216 | tf_op jit(solution)/shard_map/all_to_all | solution.py:140
  108.6 11.2 %all-to-all-done.3 = bf16[1,8,16,768]{3,2,0,1:T(8,128)(2,1)S(1)} async-done(((bf16[1,8,16,768]{3,2,0,1:T(8,128)(2,1)}), bf16[1,8,16,768]{3,2,0,1:T(8,128)(2,1)S(1)}, u32[]{:S(2)}, u32[]{:S(2)}) %all-to-all-start.3) | async-done | bytes 196640 | tf_op jit(solution)/shard_map/all_to_all | solution.py:140
  120.3 13.4 %all_to_all.80 = bf16[1,8,16,768]{3,2,0,1:T(8,128)(2,1)S(1)} all-to-all(bf16[1,8,16,768]{3,2,0,1:T(8,128)(2,1)S(1)} %broadcast_in_dim.73), channel_id=1, replica_groups=mesh['row'=8,'col'=8,'smp'=8] {'col'}, dimensions={1} | all-to-all | bytes 393216 | tf_op jit(solution)/shard_map/all_to_all | solution.py:132
  135.7 4.6 %all-to-all-start.5 = ((bf16[8,128,1,2,96]{1,4,3,2,0:T(8,128)(2,1)}), bf16[8,128,1,2,96]{1,4,3,2,0:T(8,128)(2,1)S(1)}, u32[]{:S(2)}, u32[]{:S(2)}) async-start(bf16[8,128,1,2,96]{1,4,3,2,0:T(8,128)(2,1)} %broadcast_in_dim.74), calls=%async_computation.5 | async-start | bytes 786432 | tf_op jit(solution)/shard_map/all_to_all | solution.py:132
  141.5 5.6 %all-to-all-done.5 = bf16[8,128,1,2,96]{1,4,3,2,0:T(8,128)(2,1)S(1)} async-done(((bf16[8,128,1,2,96]{1,4,3,2,0:T(8,128)(2,1)}), bf16[8,128,1,2,96]{1,4,3,2,0:T(8,128)(2,1)S(1)}, u32[]{:S(2)}, u32[]{:S(2)}) %all-to-all-start.5) | async-done | bytes 393248 | tf_op jit(solution)/shard_map/all_to_all | solution.py:132
  147.2 1.6 fusion.126
  149.7 13.6 %all_to_all.81 = bf16[1,8,16,768]{3,2,0,1:T(8,128)(2,1)S(1)} all-to-all(bf16[1,8,16,768]{3,2,0,1:T(8,128)(2,1)S(1)} %bitcast.291), channel_id=1, replica_groups=mesh['row'=8,'col'=8,'smp'=8] {'col'}, dimensions={1} | all-to-all | bytes 393216 | tf_op jit(solution)/shard_map/all_to_all | solution.py:140
  163.8 13.2 %all_to_all.82 = bf16[1,8,16,768]{3,2,0,1:T(8,128)(2,1)S(1)} all-to-all(bf16[1,8,16,768]{3,2,0,1:T(8,128)(2,1)S(1)} %broadcast_in_dim.75), channel_id=1, replica_groups=mesh['row'=8,'col'=8,'smp'=8] {'col'}, dimensions={1} | all-to-all | bytes 393216 | tf_op jit(solution)/shard_map/all_to_all | solution.py:132
  179.0 4.6 %all-to-all-start.8 = ((bf16[8,128,1,2,96]{1,4,3,2,0:T(8,128)(2,1)}), bf16[8,128,1,2,96]{1,4,3,2,0:T(8,128)(2,1)S(1)}, u32[]{:S(2)}, u32[]{:S(2)}) async-start(bf16[8,128,1,2,96]{1,4,3,2,0:T(8,128)(2,1)} %broadcast_in_dim.76), calls=%async_computation.8 | async-start | bytes 786432 | tf_op jit(solution)/shard_map/all_to_all | solution.py:132
  184.9 5.5 %all-to-all-done.8 = bf16[8,128,1,2,96]{1,4,3,2,0:T(8,128)(2,1)S(1)} async-done(((bf16[8,128,1,2,96]{1,4,3,2,0:T(8,128)(2,1)}), bf16[8,128,1,2,96]{1,4,3,2,0:T(8,128)(2,1)S(1)}, u32[]{:S(2)}, u32[]{:S(2)}) %all-to-all-start.8) | async-done | bytes 393248 | tf_op jit(solution)/shard_map/all_to_all | solution.py:132
  190.5 1.6 fusion.127
  193.0 13.6 %all_to_all.83 = bf16[1,8,16,768]{3,2,0,1:T(8,128)(2,1)S(1)} all-to-all(bf16[1,8,16,768]{3,2,0,1:T(8,128)(2,1)S(1)} %bitcast.292), channel_id=1, replica_groups=mesh['row'=8,'col'=8,'smp'=8] {'col'}, dimensions={1} | all-to-all | bytes 393216 | tf_op jit(solution)/shard_map/all_to_all | solution.py:140
  207.1 13.2 %all_to_all.84 = bf16[1,8,16,768]{3,2,0,1:T(8,128)(2,1)S(1)} all-to-all(bf16[1,8,16,768]{3,2,0,1:T(8,128)(2,1)S(1)} %broadcast_in_dim.77), channel_id=1, replica_groups=mesh['row'=8,'col'=8,'smp'=8] {'col'}, dimensions={1} | all-to-all | bytes 393216 | tf_op jit(solution)/shard_map/all_to_all | solution.py:132
  222.3 4.6 %all-to-all-start.11 = ((bf16[8,128,1,2,96]{1,4,3,2,0:T(8,128)(2,1)}), bf16[8,128,1,2,96]{1,4,3,2,0:T(8,128)(2,1)S(1)}, u32[]{:S(2)}, u32[]{:S(2)}) async-start(bf16[8,128,1,2,96]{1,4,3,2,0:T(8,128)(2,1)} %broadcast_in_dim.78), calls=%async_computation.11 | async-start | bytes 786432 | tf_op jit(solution)/shard_map/all_to_all | solution.py:132
  228.2 5.6 %all-to-all-done.11 = bf16[8,128,1,2,96]{1,4,3,2,0:T(8,128)(2,1)S(1)} async-done(((bf16[8,128,1,2,96]{1,4,3,2,0:T(8,128)(2,1)}), bf16[8,128,1,2,96]{1,4,3,2,0:T(8,128)(2,1)S(1)}, u32[]{:S(2)}, u32[]{:S(2)}) %all-to-all-start.11) | async-done | bytes 393248 | tf_op jit(solution)/shard_map/all_to_all | solution.py:132
  233.9 1.6 fusion.128
  236.4 13.6 %all_to_all.85 = bf16[1,8,16,768]{3,2,0,1:T(8,128)(2,1)S(1)} all-to-all(bf16[1,8,16,768]{3,2,0,1:T(8,128)(2,1)S(1)} %bitcast.293), channel_id=1, replica_groups=mesh['row'=8,'col'=8,'smp'=8] {'col'}, dimensions={1} | all-to-all | bytes 393216 | tf_op jit(solution)/shard_map/all_to_all | solution.py:140
  250.7 3.4 %all-to-all-start.13 = ((bf16[1,8,16,768]{3,2,0,1:T(8,128)(2,1)}), bf16[1,8,16,768]{3,2,0,1:T(8,128)(2,1)S(1)}, u32[]{:S(2)}, u32[]{:S(2)}) async-start(bf16[1,8,16,768]{3,2,0,1:T(8,128)(2,1)} %broadcast_in_dim.79), calls=%async_computation.13 | async-start | bytes 393216 | tf_op jit(solution)/shard_map/all_to_all | solution.py:132
  254.2 10.7 %all-to-all-done.13 = bf16[1,8,16,768]{3,2,0,1:T(8,128)(2,1)S(1)} async-done(((bf16[1,8,16,768]{3,2,0,1:T(8,128)(2,1)}), bf16[1,8,16,768]{3,2,0,1:T(8,128)(2,1)S(1)}, u32[]{:S(2)}, u32[]{:S(2)}) %all-to-all-start.13) | async-done | bytes 196640 | tf_op jit(solution)/shard_map/all_to_all | solution.py:132
  (135 shorter events, 26.5 us)
Async XLA Ops:
  0.6 15.1 %copy-start = (bf16[128,4,16]{0,2,1:T(8,128)(2,1)S(1)}, bf16[128,4,16]{0,2,1:T(8,128)(2,1)}, u32[]{:S(2)}) copy-start(bf16[128,4,16]{0,2,1:T(8,128)(2,1)} %param.25) | copy-start | bytes 49156
  1.9 14.1 %all-to-all-start = ((s32[2,8,128]{2,0,1:T(2,128)}), s32[2,8,128]{2,0,1:T(2,128)S(1)}, u32[]{:S(2)}, u32[]{:S(2)}) async-start(s32[2,8,128]{2,0,1:T(2,128)} %broadcast_in_dim.65), calls=%async_computation | async-start | bytes 16384 | tf_op jit(solution)/shard_map/all_to_all | solution.py:132
  18.1 12.5 %copy-start.8 = (f32[1,3]{1,0:T(1,128)S(1)}, f32[1,3]{1,0:T(1,128)}, u32[]{:S(2)}) copy-start(f32[1,3]{1,0:T(1,128)} %param.21) | copy-start | bytes 40
  18.1 18.0 %copy-start.5 = (f32[3,8192]{1,0:T(4,128)S(1)}, f32[3,8192]{1,0:T(4,128)}, u32[]{:S(2)}) copy-start(f32[3,8192]{1,0:T(4,128)} %param.17) | copy-start | bytes 294916
  18.1 62.8 %all-to-all-start.1 = ((bf16[4,128,128,1,16]{2,4,3,0,1:T(8,128)(2,1)}), bf16[4,128,128,1,16]{2,4,3,0,1:T(8,128)(2,1)S(1)}, u32[]{:S(2)}, u32[]{:S(2)}) async-start(bf16[4,128,128,1,16]{2,4,3,0,1:T(8,128)(2,1)} %bitcast.281), calls=%async_computation.1 | async-start | bytes 4194304 | tf_op jit(solution)/shard_map/all_to_all | solution.py:74
  30.7 8.2 %copy-start.12 = (s32[128]{0:T(128)S(1)}, s32[128]{0:T(128)}, u32[]{:S(2)}) copy-start(s32[128]{0:T(128)} %param.18) | copy-start | bytes 1540
  30.7 11.4 %copy-start.6 = (f32[4,768]{1,0:T(4,128)S(1)}, f32[4,768]{1,0:T(4,128)}, u32[]{:S(2)}) copy-start(f32[4,768]{1,0:T(4,128)} %param.24) | copy-start | bytes 36868
  36.2 6.2 %copy-start.11 = (f32[1,3,128]{2,0,1:T(1,128)S(1)}, f32[1,3,128]{2,0,1:T(1,128)}, u32[]{:S(2)}) copy-start(f32[1,3,128]{2,0,1:T(1,128)} %param.23) | copy-start | bytes 4612
  36.2 6.3 %copy-start.4 = (bf16[128,768]{1,0:T(8,128)(2,1)S(1)}, bf16[128,768]{1,0:T(8,128)(2,1)}, u32[]{:S(2)}) copy-start(bf16[128,768]{1,0:T(8,128)(2,1)} %param.15) | copy-start | bytes 589828
  38.8 6.8 %copy-start.10 = (f32[4,16]{1,0:T(4,128)S(1)}, f32[4,16]{1,0:T(4,128)}, u32[]{:S(2)}) copy-start(f32[4,16]{1,0:T(4,128)} %param.26) | copy-start | bytes 772
  81.3 11.1 %copy-start.9 = (s32[128]{0:T(128)S(1)}, s32[128]{0:T(128)}, u32[]{:S(2)}) copy-start(s32[128]{0:T(128)} %param.19) | copy-start | bytes 1540
  82.5 18.3 %all-to-all-start.2 = ((bf16[8,128,1,2,96]{1,4,3,2,0:T(8,128)(2,1)}), bf16[8,128,1,2,96]{1,4,3,2,0:T(8,128)(2,1)S(1)}, u32[]{:S(2)}, u32[]{:S(2)}) async-start(bf16[8,128,1,2,96]{1,4,3,2,0:T(8,128)(2,1)} %broadcast_in_dim.71), calls=%async_computation.2 | async-start | bytes 786432 | tf_op jit(solution)/shard_map/all_to_all | solution.py:132
  92.5 8.4 %copy-start.3 = (f32[128,1024]{1,0:T(8,128)}, f32[128,1024]{1,0:T(8,128)S(1)}, u32[]{:S(2)}) copy-start(f32[128,1024]{1,0:T(8,128)S(1)} %compare_convert_fusion) | copy-start | bytes 1572868
  100.9 2.3 copy-start.2
  104.1 15.7 %all-to-all-start.3 = ((bf16[1,8,16,768]{3,2,0,1:T(8,128)(2,1)}), bf16[1,8,16,768]{3,2,0,1:T(8,128)(2,1)S(1)}, u32[]{:S(2)}, u32[]{:S(2)}) async-start(bf16[1,8,16,768]{3,2,0,1:T(8,128)(2,1)} %bitcast.60), calls=%async_computation.3 | async-start | bytes 393216 | tf_op jit(solution)/shard_map/all_to_all | solution.py:140
  120.3 26.9 %copy-start.1 = (bf16[4,2,128,1024]{3,2,1,0:T(8,128)(2,1)S(1)}, bf16[4,2,128,1024]{3,2,1,0:T(8,128)(2,1)}, u32[]{:S(2)}) copy-start(bf16[4,2,128,1024]{3,2,1,0:T(8,128)(2,1)} %copy.54) | copy-start | bytes 6291460
  135.7 11.4 %all-to-all-start.5 = ((bf16[8,128,1,2,96]{1,4,3,2,0:T(8,128)(2,1)}), bf16[8,128,1,2,96]{1,4,3,2,0:T(8,128)(2,1)S(1)}, u32[]{:S(2)}, u32[]{:S(2)}) async-start(bf16[8,128,1,2,96]{1,4,3,2,0:T(8,128)(2,1)} %broadcast_in_dim.74), calls=%async_computation.5 | async-start | bytes 786432 | tf_op jit(solution)/shard_map/all_to_all | solution.py:132
  179.0 11.4 %all-to-all-start.8 = ((bf16[8,128,1,2,96]{1,4,3,2,0:T(8,128)(2,1)}), bf16[8,128,1,2,96]{1,4,3,2,0:T(8,128)(2,1)S(1)}, u32[]{:S(2)}, u32[]{:S(2)}) async-start(bf16[8,128,1,2,96]{1,4,3,2,0:T(8,128)(2,1)} %broadcast_in_dim.76), calls=%async_computation.8 | async-start | bytes 786432 | tf_op jit(solution)/shard_map/all_to_all | solution.py:132
  222.3 11.4 %all-to-all-start.11 = ((bf16[8,128,1,2,96]{1,4,3,2,0:T(8,128)(2,1)}), bf16[8,128,1,2,96]{1,4,3,2,0:T(8,128)(2,1)S(1)}, u32[]{:S(2)}, u32[]{:S(2)}) async-start(bf16[8,128,1,2,96]{1,4,3,2,0:T(8,128)(2,1)} %broadcast_in_dim.78), calls=%async_computation.11 | async-start | bytes 786432 | tf_op jit(solution)/shard_map/all_to_all | solution.py:132
  235.4 30.0 %copy-start.7 = (bf16[3,768]{1,0:T(4,128)(2,1)S(1)}, bf16[3,768]{1,0:T(4,128)(2,1)}, u32[]{:S(2)}) copy-start(bf16[3,768]{1,0:T(4,128)(2,1)} %param.29) | copy-start | bytes 13828
  250.7 14.2 %all-to-all-start.13 = ((bf16[1,8,16,768]{3,2,0,1:T(8,128)(2,1)}), bf16[1,8,16,768]{3,2,0,1:T(8,128)(2,1)S(1)}, u32[]{:S(2)}, u32[]{:S(2)}) async-start(bf16[1,8,16,768]{3,2,0,1:T(8,128)(2,1)} %broadcast_in_dim.79), calls=%async_computation.13 | async-start | bytes 393216 | tf_op jit(solution)/shard_map/all_to_all | solution.py:132

commit v4 on v2

--- a/solution.py
+++ b/solution.py
@@ -160,8 +160,6 @@
 ):
     noisy = noisy_centres(coords, token_centre_atom, angles, sample_noise_level, centre_noise)
     hidden_activity = embed_tokens(single, noisy, sample_noise_level, embedding_weight)
-    key_marks = gather_by_exchange(jnp.stack([chain_label, padding_key_mask]), "row", 1)
-    gathered_chain_ids, gathered_key_mask = key_marks[0], key_marks[1]
     pair_normed = layer_norm(pair_features.astype(jnp.float32)).astype(jnp.bfloat16)
     local_bias = jnp.einsum(
         "ikc,cbh->bhik", pair_normed, pair_bias_weight, preferred_element_type=jnp.float32
@@ -192,9 +190,18 @@
             preferred_element_type=jnp.float32,
         ).astype(jnp.bfloat16)
         if block_index == 0:
+            key_marks = jnp.stack([chain_label, padding_key_mask], axis=-1).astype(jnp.bfloat16)
+            key_marks = jnp.broadcast_to(key_marks[:, None, None, :], (row_count, samples, 1, 2))
+            key_marks = jnp.pad(key_marks, ((0, 0), (0, 0), (0, 0), (0, head_size * group_members - 2)))
+            key_value = jnp.concatenate([key_value, key_marks], axis=2)
             key_value, gathered_pair_bias = lax.optimization_barrier(
                 (key_value, gathered_pair_bias)
             )
+        gathered_key_value = gather_by_exchange(key_value, "row", 0)
+        if block_index == 0:
+            gathered_marks = gathered_key_value[:, 0, 2, 0:2].astype(jnp.int32)
+            gathered_chain_ids, gathered_key_mask = gathered_marks[:, 0], gathered_marks[:, 1]
+            gathered_key_value = gathered_key_value[:, :, 0:2]
         query_vectors = (
             front[0].astype(jnp.bfloat16).reshape(samples, row_count, group_members, head_size)
         )
@@ -216,7 +223,7 @@
             jnp.zeros((samples, group_members, row_count, head_size), jnp.float32),
         )
         final_max, final_sum, final_acc = absorb(
-            start_state, gather_by_exchange(key_value, "row", 0), jnp.int32(0)
+            start_state, gathered_key_value, jnp.int32(0)
         )
         attended = final_acc / final_sum[..., None]
         attended = jnp.transpose(attended, (0, 2, 1, 3)).reshape(

time: 270 us -> 263 us (0.974)
  starting transfers between devices: 50.3 us -> 44.2 us
    all_to_all x6 -> x5, starting transfers between devices: 28.5 us -> 23.7 us  [gather_by_exchange(): joined = lax.all_to_all(spread, axis_name, axis, axis, tiled=True)]
    all_to_all x6 -> x5, waiting for transfers between devices: 34.1 us -> 33.4 us  [gather_by_exchange(): joined = lax.all_to_all(spread, axis_name, axis, axis, tiled=True)]
  transfers between devices with their start and end apart: 8 -> 7, of which waited for: 8 -> 7; matrix products, arithmetic and copies ran while one was open for 6% -> 6% of each run, Pallas kernels for 0% -> 0%
where the time goes in v4:
time: 263 us; the launch traced here: 261 us
  waiting for transfers between devices  83.9 us (32%)
  blocking collectives  80 us (30%)
  starting transfers between devices  44.2 us (17%)
  matrix products  19.6 us (7%)
  local copies, waits for them, and re-layouts  18 us (7%)
  other arithmetic  8.91 us (3%)
  between operations  6.24 us (2%)
    all_to_all x3, blocking collectives, scatter_sum_rows(): arrived = lax.all_to_all(pieces, axis_name, 1, 1, tiled=True)  40.9 us
    all_to_all x1, waiting for transfers between devices, relay_bias(): lax.all_to_all(spread, ('col', 'smp'), split_axis=1, concat_axis=3, tiled...  39.3 us
    all_to_all x3, blocking collectives, gather_by_exchange(): joined = lax.all_to_all(spread, axis_name, axis, axis, tiled=True)  39.1 us
    all_to_all x5, waiting for transfers between devices, gather_by_exchange(): joined = lax.all_to_all(spread, axis_name, axis, axis, tiled=True)  33.4 us
    all_to_all x5, starting transfers between devices, gather_by_exchange(): joined = lax.all_to_all(spread, axis_name, axis, axis, tiled=True)  23.7 us
    all_to_all x1, starting transfers between devices, relay_bias(): lax.all_to_all(spread, ('col', 'smp'), split_axis=1, concat_axis=3, tiled...  15.8 us
    all_to_all x1, waiting for transfers between devices, scatter_sum_rows(): arrived = lax.all_to_all(pieces, axis_name, 1, 1, tiled=True)  11.2 us
    dot_general x4, matrix products, absorb(): jnp.einsum('sqhd,kshd->shqk', query_vectors, key_rows, preferred_element_...  6.31 us
  transfers between devices with their start and end apart: 7, of which 7 were waited for; matrix products, arithmetic and copies ran while one was open for 6% of the time, Pallas kernels for 0%

profile of v4, /device:TPU:8, one launch (start us, length us, event | category | flops | bytes accessed | tf_op | source)
XLA Modules:
  0.0 260.9 jit_solution(12155091558489768783)
XLA Ops:
  0.6 1.4 convert_reduce_fusion
  2.1 1.7 fusion.29
  3.8 1.6 fusion.43
  5.9 1.9 broadcast_in_dim.64
  7.8 15.8 %all-to-all-start = ((bf16[4,128,128,1,16]{2,4,3,0,1:T(8,128)(2,1)}), bf16[4,128,128,1,16]{2,4,3,0,1:T(8,128)(2,1)S(1)}, u32[]{:S(2)}, u32[]{:S(2)}) async-start(bf16[4,128,128,1,16]{2,4,3,0,1:T(8,128)(2,1)} %bitcast.287), calls=%async_computation | async-start | bytes 4194304 | tf_op jit(solution)/shard_map/all_to_all | solution.py:74
  29.2 2.6 %copy.47 = f32[3,8192]{0,1:T(8,128)} copy(f32[3,8192]{1,0:T(4,128)S(1)} %copy-done.3) | data formatting | bytes 196608 | tf_op args[2]
  31.8 2.8 %gather_fusion = f32[128,3]{1,0:T(8,128)S(1)} fusion(f32[3,8192]{0,1:T(8,128)} %copy.47, s32[1024]{0:T(1024)S(1)} %pad_clamp_fusion), kind=kCustom, calls=%fused_computation | custom fusion | bytes 3584 | tf_op jit(solution)/shard_map/jit(_take)/gather | solution.py:46
  36.0 1.3 fusion.18
  37.3 39.3 %all-to-all-done = bf16[4,128,128,1,16]{2,4,3,0,1:T(8,128)(2,1)S(1)} async-done(((bf16[4,128,128,1,16]{2,4,3,0,1:T(8,128)(2,1)}), bf16[4,128,128,1,16]{2,4,3,0,1:T(8,128)(2,1)S(1)}, u32[]{:S(2)}, u32[]{:S(2)}) %all-to-all-start) | async-done | bytes 2097184 | tf_op jit(solution)/shard_map/all_to_all | solution.py:74
  78.3 6.0 %all-to-all-start.1 = ((bf16[8,128,1,3,96]{1,4,3,2,0:T(8,128)(2,1)}), bf16[8,128,1,3,96]{1,4,3,2,0:T(8,128)(2,1)S(1)}, u32[]{:S(2)}, u32[]{:S(2)}) async-start(bf16[8,128,1,3,96]{1,4,3,2,0:T(8,128)(2,1)} %broadcast_in_dim.67), calls=%async_computation.1 | async-start | bytes 1179648 | tf_op jit(solution)/shard_map/all_to_all | solution.py:132
  85.7 2.7 %copy.54 = bf16[4,2,128,1024]{3,2,1,0:T(8,128)(2,1)} copy(bf16[4,2,128,1024]{2,3,1,0:T(8,128)(2,1)S(1)} %bitcast.288) | data formatting | bytes 4194304 | tf_op jit(solution)/shard_map/optimization_barrier | solution.py:197
  88.4 6.0 %all-to-all-done.1 = bf16[8,128,1,3,96]{1,4,3,2,0:T(8,128)(2,1)S(1)} async-done(((bf16[8,128,1,3,96]{1,4,3,2,0:T(8,128)(2,1)}), bf16[8,128,1,3,96]{1,4,3,2,0:T(8,128)(2,1)S(1)}, u32[]{:S(2)}, u32[]{:S(2)}) %all-to-all-start.1) | async-done | bytes 589856 | tf_op jit(solution)/shard_map/all_to_all | solution.py:132
  94.7 1.6 fusion.128
  98.0 4.7 %all-to-all-start.2 = ((bf16[1,8,16,768]{3,2,0,1:T(8,128)(2,1)}), bf16[1,8,16,768]{3,2,0,1:T(8,128)(2,1)S(1)}, u32[]{:S(2)}, u32[]{:S(2)}) async-start(bf16[1,8,16,768]{3,2,0,1:T(8,128)(2,1)} %bitcast.61), calls=%async_computation.2 | async-start | bytes 393216 | tf_op jit(solution)/shard_map/all_to_all | solution.py:140
  102.6 11.2 %all-to-all-done.2 = bf16[1,8,16,768]{3,2,0,1:T(8,128)(2,1)S(1)} async-done(((bf16[1,8,16,768]{3,2,0,1:T(8,128)(2,1)}), bf16[1,8,16,768]{3,2,0,1:T(8,128)(2,1)S(1)}, u32[]{:S(2)}, u32[]{:S(2)}) %all-to-all-start.2) | async-done | bytes 196640 | tf_op jit(solution)/shard_map/all_to_all | solution.py:140
  114.3 13.2 %all_to_all.75 = bf16[1,8,16,768]{3,2,0,1:T(8,128)(2,1)S(1)} all-to-all(bf16[1,8,16,768]{3,2,0,1:T(8,128)(2,1)S(1)} %broadcast_in_dim.70), channel_id=1, replica_groups=mesh['row'=8,'col'=8,'smp'=8] {'col'}, dimensions={1} | all-to-all | bytes 393216 | tf_op jit(solution)/shard_map/all_to_all | solution.py:132
  129.6 4.6 %all-to-all-start.4 = ((bf16[8,128,1,2,96]{1,4,3,2,0:T(8,128)(2,1)}), bf16[8,128,1,2,96]{1,4,3,2,0:T(8,128)(2,1)S(1)}, u32[]{:S(2)}, u32[]{:S(2)}) async-start(bf16[8,128,1,2,96]{1,4,3,2,0:T(8,128)(2,1)} %broadcast_in_dim.71), calls=%async_computation.4 | async-start | bytes 786432 | tf_op jit(solution)/shard_map/all_to_all | solution.py:132
  135.4 5.6 %all-to-all-done.4 = bf16[8,128,1,2,96]{1,4,3,2,0:T(8,128)(2,1)S(1)} async-done(((bf16[8,128,1,2,96]{1,4,3,2,0:T(8,128)(2,1)}), bf16[8,128,1,2,96]{1,4,3,2,0:T(8,128)(2,1)S(1)}, u32[]{:S(2)}, u32[]{:S(2)}) %all-to-all-start.4) | async-done | bytes 393248 | tf_op jit(solution)/shard_map/all_to_all | solution.py:132
  141.1 1.6 fusion.129
  143.6 13.6 %all_to_all.76 = bf16[1,8,16,768]{3,2,0,1:T(8,128)(2,1)S(1)} all-to-all(bf16[1,8,16,768]{3,2,0,1:T(8,128)(2,1)S(1)} %bitcast.297), channel_id=1, replica_groups=mesh['row'=8,'col'=8,'smp'=8] {'col'}, dimensions={1} | all-to-all | bytes 393216 | tf_op jit(solution)/shard_map/all_to_all | solution.py:140
  157.7 13.2 %all_to_all.77 = bf16[1,8,16,768]{3,2,0,1:T(8,128)(2,1)S(1)} all-to-all(bf16[1,8,16,768]{3,2,0,1:T(8,128)(2,1)S(1)} %broadcast_in_dim.72), channel_id=1, replica_groups=mesh['row'=8,'col'=8,'smp'=8] {'col'}, dimensions={1} | all-to-all | bytes 393216 | tf_op jit(solution)/shard_map/all_to_all | solution.py:132
  172.9 4.6 %all-to-all-start.7 = ((bf16[8,128,1,2,96]{1,4,3,2,0:T(8,128)(2,1)}), bf16[8,128,1,2,96]{1,4,3,2,0:T(8,128)(2,1)S(1)}, u32[]{:S(2)}, u32[]{:S(2)}) async-start(bf16[8,128,1,2,96]{1,4,3,2,0:T(8,128)(2,1)} %broadcast_in_dim.73), calls=%async_computation.7 | async-start | bytes 786432 | tf_op jit(solution)/shard_map/all_to_all | solution.py:132
  178.8 5.5 %all-to-all-done.7 = bf16[8,128,1,2,96]{1,4,3,2,0:T(8,128)(2,1)S(1)} async-done(((bf16[8,128,1,2,96]{1,4,3,2,0:T(8,128)(2,1)}), bf16[8,128,1,2,96]{1,4,3,2,0:T(8,128)(2,1)S(1)}, u32[]{:S(2)}, u32[]{:S(2)}) %all-to-all-start.7) | async-done | bytes 393248 | tf_op jit(solution)/shard_map/all_to_all | solution.py:132
  184.4 1.6 fusion.130
  187.0 13.6 %all_to_all.78 = bf16[1,8,16,768]{3,2,0,1:T(8,128)(2,1)S(1)} all-to-all(bf16[1,8,16,768]{3,2,0,1:T(8,128)(2,1)S(1)} %bitcast.298), channel_id=1, replica_groups=mesh['row'=8,'col'=8,'smp'=8] {'col'}, dimensions={1} | all-to-all | bytes 393216 | tf_op jit(solution)/shard_map/all_to_all | solution.py:140
  201.0 12.7 %all_to_all.79 = bf16[1,8,16,768]{3,2,0,1:T(8,128)(2,1)S(1)} all-to-all(bf16[1,8,16,768]{3,2,0,1:T(8,128)(2,1)S(1)} %broadcast_in_dim.74), channel_id=1, replica_groups=mesh['row'=8,'col'=8,'smp'=8] {'col'}, dimensions={1} | all-to-all | bytes 393216 | tf_op jit(solution)/shard_map/all_to_all | solution.py:132
  215.7 5.1 %all-to-all-start.10 = ((bf16[8,128,1,2,96]{1,4,3,2,0:T(8,128)(2,1)}), bf16[8,128,1,2,96]{1,4,3,2,0:T(8,128)(2,1)S(1)}, u32[]{:S(2)}, u32[]{:S(2)}) async-start(bf16[8,128,1,2,96]{1,4,3,2,0:T(8,128)(2,1)} %broadcast_in_dim.75), calls=%async_computation.10 | async-start | bytes 786432 | tf_op jit(solution)/shard_map/all_to_all | solution.py:132
  222.1 5.6 %all-to-all-done.10 = bf16[8,128,1,2,96]{1,4,3,2,0:T(8,128)(2,1)S(1)} async-done(((bf16[8,128,1,2,96]{1,4,3,2,0:T(8,128)(2,1)}), bf16[8,128,1,2,96]{1,4,3,2,0:T(8,128)(2,1)S(1)}, u32[]{:S(2)}, u32[]{:S(2)}) %all-to-all-start.10) | async-done | bytes 393248 | tf_op jit(solution)/shard_map/all_to_all | solution.py:132
  227.8 1.6 fusion.131
  230.3 13.6 %all_to_all.80 = bf16[1,8,16,768]{3,2,0,1:T(8,128)(2,1)S(1)} all-to-all(bf16[1,8,16,768]{3,2,0,1:T(8,128)(2,1)S(1)} %bitcast.299), channel_id=1, replica_groups=mesh['row'=8,'col'=8,'smp'=8] {'col'}, dimensions={1} | all-to-all | bytes 393216 | tf_op jit(solution)/shard_map/all_to_all | solution.py:140
  244.7 3.4 %all-to-all-start.12 = ((bf16[1,8,16,768]{3,2,0,1:T(8,128)(2,1)}), bf16[1,8,16,768]{3,2,0,1:T(8,128)(2,1)S(1)}, u32[]{:S(2)}, u32[]{:S(2)}) async-start(bf16[1,8,16,768]{3,2,0,1:T(8,128)(2,1)} %broadcast_in_dim.76), calls=%async_computation.12 | async-start | bytes 393216 | tf_op jit(solution)/shard_map/all_to_all | solution.py:132
  248.1 10.7 %all-to-all-done.12 = bf16[1,8,16,768]{3,2,0,1:T(8,128)(2,1)S(1)} async-done(((bf16[1,8,16,768]{3,2,0,1:T(8,128)(2,1)}), bf16[1,8,16,768]{3,2,0,1:T(8,128)(2,1)S(1)}, u32[]{:S(2)}, u32[]{:S(2)}) %all-to-all-start.12) | async-done | bytes 196640 | tf_op jit(solution)/shard_map/all_to_all | solution.py:132
  (133 shorter events, 24.2 us)
Async XLA Ops:
  0.6 4.8 %copy-start = (bf16[128,4,16]{0,2,1:T(8,128)(2,1)S(1)}, bf16[128,4,16]{0,2,1:T(8,128)(2,1)}, u32[]{:S(2)}) copy-start(bf16[128,4,16]{0,2,1:T(8,128)(2,1)} %param.25) | copy-start | bytes 49156
  7.8 15.8 %copy-start.6 = (f32[1,3]{1,0:T(1,128)S(1)}, f32[1,3]{1,0:T(1,128)}, u32[]{:S(2)}) copy-start(f32[1,3]{1,0:T(1,128)} %param.21) | copy-start | bytes 40
  7.8 21.4 %copy-start.3 = (f32[3,8192]{1,0:T(4,128)S(1)}, f32[3,8192]{1,0:T(4,128)}, u32[]{:S(2)}) copy-start(f32[3,8192]{1,0:T(4,128)} %param.17) | copy-start | bytes 294916
  7.8 68.8 %all-to-all-start = ((bf16[4,128,128,1,16]{2,4,3,0,1:T(8,128)(2,1)}), bf16[4,128,128,1,16]{2,4,3,0,1:T(8,128)(2,1)S(1)}, u32[]{:S(2)}, u32[]{:S(2)}) async-start(bf16[4,128,128,1,16]{2,4,3,0,1:T(8,128)(2,1)} %bitcast.287), calls=%async_computation | async-start | bytes 4194304 | tf_op jit(solution)/shard_map/all_to_all | solution.py:74
  23.6 8.2 %copy-start.11 = (s32[128]{0:T(128)S(1)}, s32[128]{0:T(128)}, u32[]{:S(2)}) copy-start(s32[128]{0:T(128)} %param.18) | copy-start | bytes 1540
  23.6 11.4 %copy-start.7 = (s32[128]{0:T(128)S(1)}, s32[128]{0:T(128)}, u32[]{:S(2)}) copy-start(s32[128]{0:T(128)} %param.19) | copy-start | bytes 1540
  23.6 11.4 %copy-start.10 = (s32[128]{0:T(128)S(1)}, s32[128]{0:T(128)}, u32[]{:S(2)}) copy-start(s32[128]{0:T(128)} %param.20) | copy-start | bytes 1540
  23.6 11.4 %copy-start.4 = (f32[4,768]{1,0:T(4,128)S(1)}, f32[4,768]{1,0:T(4,128)}, u32[]{:S(2)}) copy-start(f32[4,768]{1,0:T(4,128)} %param.24) | copy-start | bytes 36868
  29.2 6.3 %copy-start.9 = (f32[1,3,128]{2,0,1:T(1,128)S(1)}, f32[1,3,128]{2,0,1:T(1,128)}, u32[]{:S(2)}) copy-start(f32[1,3,128]{2,0,1:T(1,128)} %param.23) | copy-start | bytes 4612
  29.2 6.3 %copy-start.2 = (bf16[128,768]{1,0:T(8,128)(2,1)S(1)}, bf16[128,768]{1,0:T(8,128)(2,1)}, u32[]{:S(2)}) copy-start(bf16[128,768]{1,0:T(8,128)(2,1)} %param.15) | copy-start | bytes 589828
  77.3 8.2 %copy-start.8 = (f32[4,16]{1,0:T(4,128)S(1)}, f32[4,16]{1,0:T(4,128)}, u32[]{:S(2)}) copy-start(f32[4,16]{1,0:T(4,128)} %param.26) | copy-start | bytes 772
  78.3 16.2 %all-to-all-start.1 = ((bf16[8,128,1,3,96]{1,4,3,2,0:T(8,128)(2,1)}), bf16[8,128,1,3,96]{1,4,3,2,0:T(8,128)(2,1)S(1)}, u32[]{:S(2)}, u32[]{:S(2)}) async-start(bf16[8,128,1,3,96]{1,4,3,2,0:T(8,128)(2,1)} %broadcast_in_dim.67), calls=%async_computation.1 | async-start | bytes 1179648 | tf_op jit(solution)/shard_map/all_to_all | solution.py:132
  94.7 2.3 copy-start.1
  98.0 15.9 %all-to-all-start.2 = ((bf16[1,8,16,768]{3,2,0,1:T(8,128)(2,1)}), bf16[1,8,16,768]{3,2,0,1:T(8,128)(2,1)S(1)}, u32[]{:S(2)}, u32[]{:S(2)}) async-start(bf16[1,8,16,768]{3,2,0,1:T(8,128)(2,1)} %bitcast.61), calls=%async_computation.2 | async-start | bytes 393216 | tf_op jit(solution)/shard_map/all_to_all | solution.py:140
  129.6 11.4 %all-to-all-start.4 = ((bf16[8,128,1,2,96]{1,4,3,2,0:T(8,128)(2,1)}), bf16[8,128,1,2,96]{1,4,3,2,0:T(8,128)(2,1)S(1)}, u32[]{:S(2)}, u32[]{:S(2)}) async-start(bf16[8,128,1,2,96]{1,4,3,2,0:T(8,128)(2,1)} %broadcast_in_dim.71), calls=%async_computation.4 | async-start | bytes 786432 | tf_op jit(solution)/shard_map/all_to_all | solution.py:132
  172.9 11.4 %all-to-all-start.7 = ((bf16[8,128,1,2,96]{1,4,3,2,0:T(8,128)(2,1)}), bf16[8,128,1,2,96]{1,4,3,2,0:T(8,128)(2,1)S(1)}, u32[]{:S(2)}, u32[]{:S(2)}) async-start(bf16[8,128,1,2,96]{1,4,3,2,0:T(8,128)(2,1)} %broadcast_in_dim.73), calls=%async_computation.7 | async-start | bytes 786432 | tf_op jit(solution)/shard_map/all_to_all | solution.py:132
  215.7 12.0 %all-to-all-start.10 = ((bf16[8,128,1,2,96]{1,4,3,2,0:T(8,128)(2,1)}), bf16[8,128,1,2,96]{1,4,3,2,0:T(8,128)(2,1)S(1)}, u32[]{:S(2)}, u32[]{:S(2)}) async-start(bf16[8,128,1,2,96]{1,4,3,2,0:T(8,128)(2,1)} %broadcast_in_dim.75), calls=%async_computation.10 | async-start | bytes 786432 | tf_op jit(solution)/shard_map/all_to_all | solution.py:132
  229.4 30.0 %copy-start.5 = (bf16[3,768]{1,0:T(4,128)(2,1)S(1)}, bf16[3,768]{1,0:T(4,128)(2,1)}, u32[]{:S(2)}) copy-start(bf16[3,768]{1,0:T(4,128)(2,1)} %param.29) | copy-start | bytes 13828
  244.7 14.2 %all-to-all-start.12 = ((bf16[1,8,16,768]{3,2,0,1:T(8,128)(2,1)}), bf16[1,8,16,768]{3,2,0,1:T(8,128)(2,1)S(1)}, u32[]{:S(2)}, u32[]{:S(2)}) async-start(bf16[1,8,16,768]{3,2,0,1:T(8,128)(2,1)} %broadcast_in_dim.76), calls=%async_computation.12 | async-start | bytes 393216 | tf_op jit(solution)/shard_map/all_to_all | solution.py:132

commit v5 on v4

--- a/solution.py
+++ b/solution.py
@@ -191,17 +191,18 @@
         ).astype(jnp.bfloat16)
         if block_index == 0:
             key_marks = jnp.stack([chain_label, padding_key_mask], axis=-1).astype(jnp.bfloat16)
-            key_marks = jnp.broadcast_to(key_marks[:, None, None, :], (row_count, samples, 1, 2))
-            key_marks = jnp.pad(key_marks, ((0, 0), (0, 0), (0, 0), (0, head_size * group_members - 2)))
-            key_value = jnp.concatenate([key_value, key_marks], axis=2)
+            key_marks = jnp.broadcast_to(key_marks[:, None, :, None], (row_count, samples, 2, 1))
+            key_marks = jnp.pad(key_marks, ((0, 0), (0, 0), (0, 0), (0, 7)))
+            key_value = jnp.concatenate([key_value, key_marks], axis=3)
             key_value, gathered_pair_bias = lax.optimization_barrier(
                 (key_value, gathered_pair_bias)
             )
         gathered_key_value = gather_by_exchange(key_value, "row", 0)
         if block_index == 0:
-            gathered_marks = gathered_key_value[:, 0, 2, 0:2].astype(jnp.int32)
+            width = head_size * group_members
+            gathered_marks = gathered_key_value[:, 0, :, width].astype(jnp.int32)
             gathered_chain_ids, gathered_key_mask = gathered_marks[:, 0], gathered_marks[:, 1]
-            gathered_key_value = gathered_key_value[:, :, 0:2]
+            gathered_key_value = gathered_key_value[..., 0:width]
         query_vectors = (
             front[0].astype(jnp.bfloat16).reshape(samples, row_count, group_members, head_size)
         )

time: 263 us -> 262 us (level)
  no operation moved by 1% of the time
where the time goes in v5:
time: 262 us; the launch traced here: 260 us
  waiting for transfers between devices  82.2 us (31%)
  blocking collectives  80.1 us (31%)
  starting transfers between devices  44.2 us (17%)
  matrix products  19.6 us (7%)
  local copies, waits for them, and re-layouts  18.6 us (7%)
  other arithmetic  8.91 us (3%)
  between operations  6.26 us (2%)
    all_to_all x3, blocking collectives, scatter_sum_rows(): arrived = lax.all_to_all(pieces, axis_name, 1, 1, tiled=True)  40.9 us
    all_to_all x1, waiting for transfers between devices, relay_bias(): lax.all_to_all(spread, ('col', 'smp'), split_axis=1, concat_axis=3, tiled...  39.3 us
    all_to_all x3, blocking collectives, gather_by_exchange(): joined = lax.all_to_all(spread, axis_name, axis, axis, tiled=True)  39.3 us
    all_to_all x5, waiting for transfers between devices, gather_by_exchange(): joined = lax.all_to_all(spread, axis_name, axis, axis, tiled=True)  31.7 us
    all_to_all x5, starting transfers between devices, gather_by_exchange(): joined = lax.all_to_all(spread, axis_name, axis, axis, tiled=True)  23.7 us
    all_to_all x1, starting transfers between devices, relay_bias(): lax.all_to_all(spread, ('col', 'smp'), split_axis=1, concat_axis=3, tiled...  15.8 us
    all_to_all x1, waiting for transfers between devices, scatter_sum_rows(): arrived = lax.all_to_all(pieces, axis_name, 1, 1, tiled=True)  11.2 us
    dot_general x4, matrix products, absorb(): jnp.einsum('sqhd,kshd->shqk', query_vectors, key_rows, preferred_element_...  6.32 us
  transfers between devices with their start and end apart: 7, of which 7 were waited for; matrix products, arithmetic and copies ran while one was open for 6% of the time, Pallas kernels for 0%

profile of v5, /device:TPU:8, one launch (start us, length us, event | category | flops | bytes accessed | tf_op | source)
XLA Modules:
  0.0 259.9 jit_solution(654837457155734943)
XLA Ops:
  0.6 1.4 convert_reduce_fusion
  2.1 1.7 fusion.29
  3.8 1.6 fusion.43
  5.9 1.9 broadcast_in_dim.64
  7.8 15.8 %all-to-all-start = ((bf16[4,128,128,1,16]{2,4,3,0,1:T(8,128)(2,1)}), bf16[4,128,128,1,16]{2,4,3,0,1:T(8,128)(2,1)S(1)}, u32[]{:S(2)}, u32[]{:S(2)}) async-start(bf16[4,128,128,1,16]{2,4,3,0,1:T(8,128)(2,1)} %bitcast.285), calls=%async_computation | async-start | bytes 4194304 | tf_op jit(solution)/shard_map/all_to_all | solution.py:74
  29.2 2.6 %copy.47 = f32[3,8192]{0,1:T(8,128)} copy(f32[3,8192]{1,0:T(4,128)S(1)} %copy-done.5) | data formatting | bytes 196608 | tf_op args[2]
  31.8 2.8 %gather_fusion = f32[128,3]{1,0:T(8,128)S(1)} fusion(f32[3,8192]{0,1:T(8,128)} %copy.47, s32[1024]{0:T(1024)S(1)} %pad_clamp_fusion), kind=kCustom, calls=%fused_computation | custom fusion | bytes 3584 | tf_op jit(solution)/shard_map/jit(_take)/gather | solution.py:46
  36.0 1.3 fusion.18
  37.3 39.3 %all-to-all-done = bf16[4,128,128,1,16]{2,4,3,0,1:T(8,128)(2,1)S(1)} async-done(((bf16[4,128,128,1,16]{2,4,3,0,1:T(8,128)(2,1)}), bf16[4,128,128,1,16]{2,4,3,0,1:T(8,128)(2,1)S(1)}, u32[]{:S(2)}, u32[]{:S(2)}) %all-to-all-start) | async-done | bytes 2097184 | tf_op jit(solution)/shard_map/all_to_all | solution.py:74
  78.2 6.0 %all-to-all-start.1 = ((bf16[8,128,1,2,104]{1,4,3,2,0:T(8,128)(2,1)}), bf16[8,128,1,2,104]{1,4,3,2,0:T(8,128)(2,1)S(1)}, u32[]{:S(2)}, u32[]{:S(2)}) async-start(bf16[8,128,1,2,104]{1,4,3,2,0:T(8,128)(2,1)} %broadcast_in_dim.67), calls=%async_computation.1 | async-start | bytes 851968 | tf_op jit(solution)/shard_map/all_to_all | solution.py:132
  85.6 2.7 %copy.54 = bf16[4,2,128,1024]{3,2,1,0:T(8,128)(2,1)} copy(bf16[4,2,128,1024]{2,3,1,0:T(8,128)(2,1)S(1)} %bitcast.286) | data formatting | bytes 4194304 | tf_op jit(solution)/shard_map/optimization_barrier | solution.py:197
  88.3 4.2 %all-to-all-done.1 = bf16[8,128,1,2,104]{1,4,3,2,0:T(8,128)(2,1)S(1)} async-done(((bf16[8,128,1,2,104]{1,4,3,2,0:T(8,128)(2,1)}), bf16[8,128,1,2,104]{1,4,3,2,0:T(8,128)(2,1)S(1)}, u32[]{:S(2)}, u32[]{:S(2)}) %all-to-all-start.1) | async-done | bytes 426016 | tf_op jit(solution)/shard_map/all_to_all | solution.py:132
  93.6 1.6 fusion.127
  96.9 4.7 %all-to-all-start.2 = ((bf16[1,8,16,768]{3,2,0,1:T(8,128)(2,1)}), bf16[1,8,16,768]{3,2,0,1:T(8,128)(2,1)S(1)}, u32[]{:S(2)}, u32[]{:S(2)}) async-start(bf16[1,8,16,768]{3,2,0,1:T(8,128)(2,1)} %bitcast.59), calls=%async_computation.2 | async-start | bytes 393216 | tf_op jit(solution)/shard_map/all_to_all | solution.py:140
  101.6 11.2 %all-to-all-done.2 = bf16[1,8,16,768]{3,2,0,1:T(8,128)(2,1)S(1)} async-done(((bf16[1,8,16,768]{3,2,0,1:T(8,128)(2,1)}), bf16[1,8,16,768]{3,2,0,1:T(8,128)(2,1)S(1)}, u32[]{:S(2)}, u32[]{:S(2)}) %all-to-all-start.2) | async-done | bytes 196640 | tf_op jit(solution)/shard_map/all_to_all | solution.py:140
  113.3 13.4 %all_to_all.75 = bf16[1,8,16,768]{3,2,0,1:T(8,128)(2,1)S(1)} all-to-all(bf16[1,8,16,768]{3,2,0,1:T(8,128)(2,1)S(1)} %broadcast_in_dim.70), channel_id=1, replica_groups=mesh['row'=8,'col'=8,'smp'=8] {'col'}, dimensions={1} | all-to-all | bytes 393216 | tf_op jit(solution)/shard_map/all_to_all | solution.py:132
  128.6 4.6 %all-to-all-start.4 = ((bf16[8,128,1,2,96]{1,4,3,2,0:T(8,128)(2,1)}), bf16[8,128,1,2,96]{1,4,3,2,0:T(8,128)(2,1)S(1)}, u32[]{:S(2)}, u32[]{:S(2)}) async-start(bf16[8,128,1,2,96]{1,4,3,2,0:T(8,128)(2,1)} %broadcast_in_dim.71), calls=%async_computation.4 | async-start | bytes 786432 | tf_op jit(solution)/shard_map/all_to_all | solution.py:132
  134.4 5.6 %all-to-all-done.4 = bf16[8,128,1,2,96]{1,4,3,2,0:T(8,128)(2,1)S(1)} async-done(((bf16[8,128,1,2,96]{1,4,3,2,0:T(8,128)(2,1)}), bf16[8,128,1,2,96]{1,4,3,2,0:T(8,128)(2,1)S(1)}, u32[]{:S(2)}, u32[]{:S(2)}) %all-to-all-start.4) | async-done | bytes 393248 | tf_op jit(solution)/shard_map/all_to_all | solution.py:132
  140.2 1.6 fusion.128
  142.7 13.6 %all_to_all.76 = bf16[1,8,16,768]{3,2,0,1:T(8,128)(2,1)S(1)} all-to-all(bf16[1,8,16,768]{3,2,0,1:T(8,128)(2,1)S(1)} %bitcast.295), channel_id=1, replica_groups=mesh['row'=8,'col'=8,'smp'=8] {'col'}, dimensions={1} | all-to-all | bytes 393216 | tf_op jit(solution)/shard_map/all_to_all | solution.py:140
  156.8 12.7 %all_to_all.77 = bf16[1,8,16,768]{3,2,0,1:T(8,128)(2,1)S(1)} all-to-all(bf16[1,8,16,768]{3,2,0,1:T(8,128)(2,1)S(1)} %broadcast_in_dim.72), channel_id=1, replica_groups=mesh['row'=8,'col'=8,'smp'=8] {'col'}, dimensions={1} | all-to-all | bytes 393216 | tf_op jit(solution)/shard_map/all_to_all | solution.py:132
  171.4 5.1 %all-to-all-start.7 = ((bf16[8,128,1,2,96]{1,4,3,2,0:T(8,128)(2,1)}), bf16[8,128,1,2,96]{1,4,3,2,0:T(8,128)(2,1)S(1)}, u32[]{:S(2)}, u32[]{:S(2)}) async-start(bf16[8,128,1,2,96]{1,4,3,2,0:T(8,128)(2,1)} %broadcast_in_dim.73), calls=%async_computation.7 | async-start | bytes 786432 | tf_op jit(solution)/shard_map/all_to_all | solution.py:132
  177.9 5.5 %all-to-all-done.7 = bf16[8,128,1,2,96]{1,4,3,2,0:T(8,128)(2,1)S(1)} async-done(((bf16[8,128,1,2,96]{1,4,3,2,0:T(8,128)(2,1)}), bf16[8,128,1,2,96]{1,4,3,2,0:T(8,128)(2,1)S(1)}, u32[]{:S(2)}, u32[]{:S(2)}) %all-to-all-start.7) | async-done | bytes 393248 | tf_op jit(solution)/shard_map/all_to_all | solution.py:132
  183.5 1.6 fusion.129
  186.0 13.6 %all_to_all.78 = bf16[1,8,16,768]{3,2,0,1:T(8,128)(2,1)S(1)} all-to-all(bf16[1,8,16,768]{3,2,0,1:T(8,128)(2,1)S(1)} %bitcast.296), channel_id=1, replica_groups=mesh['row'=8,'col'=8,'smp'=8] {'col'}, dimensions={1} | all-to-all | bytes 393216 | tf_op jit(solution)/shard_map/all_to_all | solution.py:140
  200.1 13.2 %all_to_all.79 = bf16[1,8,16,768]{3,2,0,1:T(8,128)(2,1)S(1)} all-to-all(bf16[1,8,16,768]{3,2,0,1:T(8,128)(2,1)S(1)} %broadcast_in_dim.74), channel_id=1, replica_groups=mesh['row'=8,'col'=8,'smp'=8] {'col'}, dimensions={1} | all-to-all | bytes 393216 | tf_op jit(solution)/shard_map/all_to_all | solution.py:132
  215.3 4.6 %all-to-all-start.10 = ((bf16[8,128,1,2,96]{1,4,3,2,0:T(8,128)(2,1)}), bf16[8,128,1,2,96]{1,4,3,2,0:T(8,128)(2,1)S(1)}, u32[]{:S(2)}, u32[]{:S(2)}) async-start(bf16[8,128,1,2,96]{1,4,3,2,0:T(8,128)(2,1)} %broadcast_in_dim.75), calls=%async_computation.10 | async-start | bytes 786432 | tf_op jit(solution)/shard_map/all_to_all | solution.py:132
  221.2 5.6 %all-to-all-done.10 = bf16[8,128,1,2,96]{1,4,3,2,0:T(8,128)(2,1)S(1)} async-done(((bf16[8,128,1,2,96]{1,4,3,2,0:T(8,128)(2,1)}), bf16[8,128,1,2,96]{1,4,3,2,0:T(8,128)(2,1)S(1)}, u32[]{:S(2)}, u32[]{:S(2)}) %all-to-all-start.10) | async-done | bytes 393248 | tf_op jit(solution)/shard_map/all_to_all | solution.py:132
  226.9 1.6 fusion.130
  229.4 13.6 %all_to_all.80 = bf16[1,8,16,768]{3,2,0,1:T(8,128)(2,1)S(1)} all-to-all(bf16[1,8,16,768]{3,2,0,1:T(8,128)(2,1)S(1)} %bitcast.297), channel_id=1, replica_groups=mesh['row'=8,'col'=8,'smp'=8] {'col'}, dimensions={1} | all-to-all | bytes 393216 | tf_op jit(solution)/shard_map/all_to_all | solution.py:140
  243.7 3.4 %all-to-all-start.12 = ((bf16[1,8,16,768]{3,2,0,1:T(8,128)(2,1)}), bf16[1,8,16,768]{3,2,0,1:T(8,128)(2,1)S(1)}, u32[]{:S(2)}, u32[]{:S(2)}) async-start(bf16[1,8,16,768]{3,2,0,1:T(8,128)(2,1)} %broadcast_in_dim.76), calls=%async_computation.12 | async-start | bytes 393216 | tf_op jit(solution)/shard_map/all_to_all | solution.py:132
  247.2 10.7 %all-to-all-done.12 = bf16[1,8,16,768]{3,2,0,1:T(8,128)(2,1)S(1)} async-done(((bf16[1,8,16,768]{3,2,0,1:T(8,128)(2,1)}), bf16[1,8,16,768]{3,2,0,1:T(8,128)(2,1)S(1)}, u32[]{:S(2)}, u32[]{:S(2)}) %all-to-all-start.12) | async-done | bytes 196640 | tf_op jit(solution)/shard_map/all_to_all | solution.py:132
  (138 shorter events, 24.8 us)
Async XLA Ops:
  0.6 4.8 %copy-start = (bf16[128,4,16]{0,2,1:T(8,128)(2,1)S(1)}, bf16[128,4,16]{0,2,1:T(8,128)(2,1)}, u32[]{:S(2)}) copy-start(bf16[128,4,16]{0,2,1:T(8,128)(2,1)} %param.25) | copy-start | bytes 49156
  7.8 15.8 %copy-start.8 = (f32[1,3]{1,0:T(1,128)S(1)}, f32[1,3]{1,0:T(1,128)}, u32[]{:S(2)}) copy-start(f32[1,3]{1,0:T(1,128)} %param.21) | copy-start | bytes 40
  7.8 21.4 %copy-start.5 = (f32[3,8192]{1,0:T(4,128)S(1)}, f32[3,8192]{1,0:T(4,128)}, u32[]{:S(2)}) copy-start(f32[3,8192]{1,0:T(4,128)} %param.17) | copy-start | bytes 294916
  7.8 68.8 %all-to-all-start = ((bf16[4,128,128,1,16]{2,4,3,0,1:T(8,128)(2,1)}), bf16[4,128,128,1,16]{2,4,3,0,1:T(8,128)(2,1)S(1)}, u32[]{:S(2)}, u32[]{:S(2)}) async-start(bf16[4,128,128,1,16]{2,4,3,0,1:T(8,128)(2,1)} %bitcast.285), calls=%async_computation | async-start | bytes 4194304 | tf_op jit(solution)/shard_map/all_to_all | solution.py:74
  23.6 8.2 %copy-start.13 = (s32[128]{0:T(128)S(1)}, s32[128]{0:T(128)}, u32[]{:S(2)}) copy-start(s32[128]{0:T(128)} %param.18) | copy-start | bytes 1540
  23.6 11.2 %copy-start.9 = (s32[128]{0:T(128)S(1)}, s32[128]{0:T(128)}, u32[]{:S(2)}) copy-start(s32[128]{0:T(128)} %param.19) | copy-start | bytes 1540
  23.6 11.2 %copy-start.12 = (s32[128]{0:T(128)S(1)}, s32[128]{0:T(128)}, u32[]{:S(2)}) copy-start(s32[128]{0:T(128)} %param.20) | copy-start | bytes 1540
  23.6 11.4 %copy-start.6 = (f32[4,768]{1,0:T(4,128)S(1)}, f32[4,768]{1,0:T(4,128)}, u32[]{:S(2)}) copy-start(f32[4,768]{1,0:T(4,128)} %param.24) | copy-start | bytes 36868
  29.2 6.3 %copy-start.11 = (f32[1,3,128]{2,0,1:T(1,128)S(1)}, f32[1,3,128]{2,0,1:T(1,128)}, u32[]{:S(2)}) copy-start(f32[1,3,128]{2,0,1:T(1,128)} %param.23) | copy-start | bytes 4612
  29.2 6.3 %copy-start.4 = (bf16[128,768]{1,0:T(8,128)(2,1)S(1)}, bf16[128,768]{1,0:T(8,128)(2,1)}, u32[]{:S(2)}) copy-start(bf16[128,768]{1,0:T(8,128)(2,1)} %param.15) | copy-start | bytes 589828
  77.0 8.5 %copy-start.10 = (f32[4,16]{1,0:T(4,128)S(1)}, f32[4,16]{1,0:T(4,128)}, u32[]{:S(2)}) copy-start(f32[4,16]{1,0:T(4,128)} %param.26) | copy-start | bytes 772
  78.2 14.4 %all-to-all-start.1 = ((bf16[8,128,1,2,104]{1,4,3,2,0:T(8,128)(2,1)}), bf16[8,128,1,2,104]{1,4,3,2,0:T(8,128)(2,1)S(1)}, u32[]{:S(2)}, u32[]{:S(2)}) async-start(bf16[8,128,1,2,104]{1,4,3,2,0:T(8,128)(2,1)} %broadcast_in_dim.67), calls=%async_computation.1 | async-start | bytes 851968 | tf_op jit(solution)/shard_map/all_to_all | solution.py:132
  92.8 0.8 copy-start.3
  93.6 2.3 copy-start.2
  96.9 15.9 %all-to-all-start.2 = ((bf16[1,8,16,768]{3,2,0,1:T(8,128)(2,1)}), bf16[1,8,16,768]{3,2,0,1:T(8,128)(2,1)S(1)}, u32[]{:S(2)}, u32[]{:S(2)}) async-start(bf16[1,8,16,768]{3,2,0,1:T(8,128)(2,1)} %bitcast.59), calls=%async_computation.2 | async-start | bytes 393216 | tf_op jit(solution)/shard_map/all_to_all | solution.py:140
  113.2 26.9 %copy-start.1 = (bf16[4,2,128,1024]{3,2,1,0:T(8,128)(2,1)S(1)}, bf16[4,2,128,1024]{3,2,1,0:T(8,128)(2,1)}, u32[]{:S(2)}) copy-start(bf16[4,2,128,1024]{3,2,1,0:T(8,128)(2,1)} %copy.54) | copy-start | bytes 6291460
  128.6 11.4 %all-to-all-start.4 = ((bf16[8,128,1,2,96]{1,4,3,2,0:T(8,128)(2,1)}), bf16[8,128,1,2,96]{1,4,3,2,0:T(8,128)(2,1)S(1)}, u32[]{:S(2)}, u32[]{:S(2)}) async-start(bf16[8,128,1,2,96]{1,4,3,2,0:T(8,128)(2,1)} %broadcast_in_dim.71), calls=%async_computation.4 | async-start | bytes 786432 | tf_op jit(solution)/shard_map/all_to_all | solution.py:132
  171.4 12.0 %all-to-all-start.7 = ((bf16[8,128,1,2,96]{1,4,3,2,0:T(8,128)(2,1)}), bf16[8,128,1,2,96]{1,4,3,2,0:T(8,128)(2,1)S(1)}, u32[]{:S(2)}, u32[]{:S(2)}) async-start(bf16[8,128,1,2,96]{1,4,3,2,0:T(8,128)(2,1)} %broadcast_in_dim.73), calls=%async_computation.7 | async-start | bytes 786432 | tf_op jit(solution)/shard_map/all_to_all | solution.py:132
  215.3 11.4 %all-to-all-start.10 = ((bf16[8,128,1,2,96]{1,4,3,2,0:T(8,128)(2,1)}), bf16[8,128,1,2,96]{1,4,3,2,0:T(8,128)(2,1)S(1)}, u32[]{:S(2)}, u32[]{:S(2)}) async-start(bf16[8,128,1,2,96]{1,4,3,2,0:T(8,128)(2,1)} %broadcast_in_dim.75), calls=%async_computation.10 | async-start | bytes 786432 | tf_op jit(solution)/shard_map/all_to_all | solution.py:132
  228.4 30.0 %copy-start.7 = (bf16[3,768]{1,0:T(4,128)(2,1)S(1)}, bf16[3,768]{1,0:T(4,128)(2,1)}, u32[]{:S(2)}) copy-start(bf16[3,768]{1,0:T(4,128)(2,1)} %param.29) | copy-start | bytes 13828
  243.7 14.2 %all-to-all-start.12 = ((bf16[1,8,16,768]{3,2,0,1:T(8,128)(2,1)}), bf16[1,8,16,768]{3,2,0,1:T(8,128)(2,1)S(1)}, u32[]{:S(2)}, u32[]{:S(2)}) async-start(bf16[1,8,16,768]{3,2,0,1:T(8,128)(2,1)} %broadcast_in_dim.76), calls=%async_computation.12 | async-start | bytes 393216 | tf_op jit(solution)/shard_map/all_to_all | solution.py:132

commit v6 on v5

--- a/solution.py
+++ b/solution.py
@@ -1,6 +1,8 @@
 import jax
 import jax.numpy as jnp
 from jax import lax
+from jax.experimental import pallas as pl
+from jax.experimental.pallas import tpu as pltpu
 from jax.sharding import PartitionSpec as P
 
 EPSILON = 1e-05
@@ -59,6 +61,37 @@
     hidden_activity = hidden_activity + scaled[:, 2, :, None] * embedding_weight[2]
     hidden_activity = hidden_activity + log_level[:, None, None] * embedding_weight[3]
     return hidden_activity.astype(jnp.bfloat16)
+
+
+def pair_bias_kernel(pair_ref, weight_ref, out_ref):
+    pair = pair_ref[...].astype(jnp.float32)
+    average = jnp.mean(pair, axis=-1, keepdims=True)
+    centred = pair - average
+    spread = jnp.mean(centred * centred, axis=-1, keepdims=True)
+    normed = (centred * lax.rsqrt(spread + EPSILON)).astype(jnp.bfloat16)
+    out_ref[...] = jnp.dot(normed, weight_ref[...], preferred_element_type=jnp.float32).astype(
+        out_ref.dtype
+    )
+
+
+def local_pair_bias(pair_features, pair_bias_weight):
+    row_count, keys_dev, channels = pair_features.shape
+    _, blocks, total_heads = pair_bias_weight.shape
+    pairs = row_count * keys_dev
+    outputs = blocks * total_heads
+    flat_bias = pl.pallas_call(
+        pair_bias_kernel,
+        out_shape=jax.ShapeDtypeStruct((pairs, outputs), jnp.bfloat16),
+        in_specs=[pl.BlockSpec(memory_space=pltpu.VMEM)] * 2,
+        out_specs=pl.BlockSpec(memory_space=pltpu.VMEM),
+        cost_estimate=pl.CostEstimate(
+            flops=2 * pairs * channels * outputs + 8 * pairs * channels,
+            transcendentals=pairs,
+            bytes_accessed=2 * (pairs * channels + channels * outputs + pairs * outputs),
+        ),
+    )(pair_features.reshape(pairs, channels), pair_bias_weight.reshape(channels, outputs))
+    flat_bias = flat_bias.reshape(row_count, keys_dev, blocks, total_heads)
+    return jnp.transpose(flat_bias, (2, 3, 0, 1))
 
 
 def relay_bias(local_bias):
@@ -160,10 +193,7 @@
 ):
     noisy = noisy_centres(coords, token_centre_atom, angles, sample_noise_level, centre_noise)
     hidden_activity = embed_tokens(single, noisy, sample_noise_level, embedding_weight)
-    pair_normed = layer_norm(pair_features.astype(jnp.float32)).astype(jnp.bfloat16)
-    local_bias = jnp.einsum(
-        "ikc,cbh->bhik", pair_normed, pair_bias_weight, preferred_element_type=jnp.float32
-    ).astype(jnp.bfloat16)
+    local_bias = local_pair_bias(pair_features, pair_bias_weight)
     gathered_pair_bias = relay_bias(local_bias)
     samples, row_count, model_width = hidden_activity.shape
     col_count = lax.axis_size("col")

time: 262 us -> 264 us (level)
  local copies, waits for them, and re-layouts: 18.6 us -> 23.6 us
  other arithmetic: 8.91 us -> 4.24 us
    reshape x0 -> x2, local copies, waits for them, and re-layouts: none -> 3.14 us  [the longest x1 1.7 us: local_pair_bias(): flat_bias = flat_bias.reshape(row_count, keys_dev, blocks, total_heads)]
where the time goes in v6:
time: 264 us; the launch traced here: 263 us
  waiting for transfers between devices  82.1 us (31%)
  blocking collectives  80.1 us (30%)
  starting transfers between devices  44.6 us (17%)
  local copies, waits for them, and re-layouts  23.6 us (9%)
  matrix products  19.4 us (7%)
  between operations  6.22 us (2%)
  other arithmetic  4.24 us (2%)
    all_to_all x3, blocking collectives, scatter_sum_rows(): arrived = lax.all_to_all(pieces, axis_name, 1, 1, tiled=True)  40.9 us
    all_to_all x1, waiting for transfers between devices, relay_bias(): lax.all_to_all(spread, ('col', 'smp'), split_axis=1, concat_axis=3, tiled...  39.3 us
    all_to_all x3, blocking collectives, gather_by_exchange(): joined = lax.all_to_all(spread, axis_name, axis, axis, tiled=True)  39.3 us
    all_to_all x5, waiting for transfers between devices, gather_by_exchange(): joined = lax.all_to_all(spread, axis_name, axis, axis, tiled=True)  31.6 us
    all_to_all x5, starting transfers between devices, gather_by_exchange(): joined = lax.all_to_all(spread, axis_name, axis, axis, tiled=True)  23.9 us
    all_to_all x1, starting transfers between devices, relay_bias(): lax.all_to_all(spread, ('col', 'smp'), split_axis=1, concat_axis=3, tiled...  15.8 us
    all_to_all x1, waiting for transfers between devices, scatter_sum_rows(): arrived = lax.all_to_all(pieces, axis_name, 1, 1, tiled=True)  11.2 us
    dot_general x4, matrix products, absorb(): jnp.einsum('sqhd,kshd->shqk', query_vectors, key_rows, preferred_element_...  6.36 us
  transfers between devices with their start and end apart: 7, of which 7 were waited for; matrix products, arithmetic and copies ran while one was open for 6% of the time, Pallas kernels for 0%

profile of v6, /device:TPU:8, one launch (start us, length us, event | category | flops | bytes accessed | tf_op | source)
XLA Modules:
  0.0 262.8 jit_solution(14429778165713850516)
XLA Ops:
  0.6 1.4 copy.52.weight_ref
  2.1 2.6 shard_map.158
  5.9 1.7 reshape.1042
  8.4 1.9 broadcast_in_dim.64
  10.3 15.8 %all-to-all-start = ((bf16[4,128,128,1,16]{2,4,3,0,1:T(8,128)(2,1)}), bf16[4,128,128,1,16]{2,4,3,0,1:T(8,128)(2,1)S(1)}, u32[]{:S(2)}, u32[]{:S(2)}) async-start(bf16[4,128,128,1,16]{2,4,3,0,1:T(8,128)(2,1)} %bitcast.285), calls=%async_computation | async-start | bytes 4194304 | tf_op jit(solution)/shard_map/all_to_all | solution.py:107
  31.7 2.6 copy.50
  34.3 2.8 %gather_fusion = f32[128,3]{1,0:T(8,128)S(1)} fusion(f32[3,8192]{0,1:T(8,128)} %copy.50, s32[1024]{0:T(1024)S(1)} %pad_clamp_fusion), kind=kCustom, calls=%fused_computation | custom fusion | bytes 3584 | tf_op jit(solution)/shard_map/jit(_take)/gather | solution.py:48
  38.5 1.3 fusion.16
  39.8 39.3 %all-to-all-done = bf16[4,128,128,1,16]{2,4,3,0,1:T(8,128)(2,1)S(1)} async-done(((bf16[4,128,128,1,16]{2,4,3,0,1:T(8,128)(2,1)}), bf16[4,128,128,1,16]{2,4,3,0,1:T(8,128)(2,1)S(1)}, u32[]{:S(2)}, u32[]{:S(2)}) %all-to-all-start) | async-done | bytes 2097184 | tf_op jit(solution)/shard_map/all_to_all | solution.py:107
  80.7 6.2 %all-to-all-start.1 = ((bf16[8,128,1,2,104]{1,4,3,2,0:T(8,128)(2,1)}), bf16[8,128,1,2,104]{1,4,3,2,0:T(8,128)(2,1)S(1)}, u32[]{:S(2)}, u32[]{:S(2)}) async-start(bf16[8,128,1,2,104]{1,4,3,2,0:T(8,128)(2,1)} %broadcast_in_dim.67), calls=%async_computation.1 | async-start | bytes 851968 | tf_op jit(solution)/shard_map/all_to_all | solution.py:165
  88.3 2.7 %copy.59 = bf16[4,2,128,1024]{3,2,1,0:T(8,128)(2,1)} copy(bf16[4,2,128,1024]{2,3,1,0:T(8,128)(2,1)S(1)} %bitcast.286) | data formatting | bytes 4194304 | tf_op jit(solution)/shard_map/optimization_barrier | solution.py:227
  91.1 4.1 %all-to-all-done.1 = bf16[8,128,1,2,104]{1,4,3,2,0:T(8,128)(2,1)S(1)} async-done(((bf16[8,128,1,2,104]{1,4,3,2,0:T(8,128)(2,1)}), bf16[8,128,1,2,104]{1,4,3,2,0:T(8,128)(2,1)S(1)}, u32[]{:S(2)}, u32[]{:S(2)}) %all-to-all-start.1) | async-done | bytes 426016 | tf_op jit(solution)/shard_map/all_to_all | solution.py:165
  96.3 1.6 fusion.120
  99.5 4.8 %all-to-all-start.2 = ((bf16[1,8,16,768]{3,2,0,1:T(8,128)(2,1)}), bf16[1,8,16,768]{3,2,0,1:T(8,128)(2,1)S(1)}, u32[]{:S(2)}, u32[]{:S(2)}) async-start(bf16[1,8,16,768]{3,2,0,1:T(8,128)(2,1)} %bitcast.59), calls=%async_computation.2 | async-start | bytes 393216 | tf_op jit(solution)/shard_map/all_to_all | solution.py:173
  104.4 11.2 %all-to-all-done.2 = bf16[1,8,16,768]{3,2,0,1:T(8,128)(2,1)S(1)} async-done(((bf16[1,8,16,768]{3,2,0,1:T(8,128)(2,1)}), bf16[1,8,16,768]{3,2,0,1:T(8,128)(2,1)S(1)}, u32[]{:S(2)}, u32[]{:S(2)}) %all-to-all-start.2) | async-done | bytes 196640 | tf_op jit(solution)/shard_map/all_to_all | solution.py:173
  116.1 13.4 %all_to_all.75 = bf16[1,8,16,768]{3,2,0,1:T(8,128)(2,1)S(1)} all-to-all(bf16[1,8,16,768]{3,2,0,1:T(8,128)(2,1)S(1)} %broadcast_in_dim.70), channel_id=1, replica_groups=mesh['row'=8,'col'=8,'smp'=8] {'col'}, dimensions={1} | all-to-all | bytes 393216 | tf_op jit(solution)/shard_map/all_to_all | solution.py:165
  131.4 4.6 %all-to-all-start.4 = ((bf16[8,128,1,2,96]{1,4,3,2,0:T(8,128)(2,1)}), bf16[8,128,1,2,96]{1,4,3,2,0:T(8,128)(2,1)S(1)}, u32[]{:S(2)}, u32[]{:S(2)}) async-start(bf16[8,128,1,2,96]{1,4,3,2,0:T(8,128)(2,1)} %broadcast_in_dim.71), calls=%async_computation.4 | async-start | bytes 786432 | tf_op jit(solution)/shard_map/all_to_all | solution.py:165
  137.3 5.6 %all-to-all-done.4 = bf16[8,128,1,2,96]{1,4,3,2,0:T(8,128)(2,1)S(1)} async-done(((bf16[8,128,1,2,96]{1,4,3,2,0:T(8,128)(2,1)}), bf16[8,128,1,2,96]{1,4,3,2,0:T(8,128)(2,1)S(1)}, u32[]{:S(2)}, u32[]{:S(2)}) %all-to-all-start.4) | async-done | bytes 393248 | tf_op jit(solution)/shard_map/all_to_all | solution.py:165
  143.0 1.6 fusion.121
  145.5 13.6 %all_to_all.76 = bf16[1,8,16,768]{3,2,0,1:T(8,128)(2,1)S(1)} all-to-all(bf16[1,8,16,768]{3,2,0,1:T(8,128)(2,1)S(1)} %bitcast.294), channel_id=1, replica_groups=mesh['row'=8,'col'=8,'smp'=8] {'col'}, dimensions={1} | all-to-all | bytes 393216 | tf_op jit(solution)/shard_map/all_to_all | solution.py:173
  159.6 13.2 %all_to_all.77 = bf16[1,8,16,768]{3,2,0,1:T(8,128)(2,1)S(1)} all-to-all(bf16[1,8,16,768]{3,2,0,1:T(8,128)(2,1)S(1)} %broadcast_in_dim.72), channel_id=1, replica_groups=mesh['row'=8,'col'=8,'smp'=8] {'col'}, dimensions={1} | all-to-all | bytes 393216 | tf_op jit(solution)/shard_map/all_to_all | solution.py:165
  174.8 4.6 %all-to-all-start.7 = ((bf16[8,128,1,2,96]{1,4,3,2,0:T(8,128)(2,1)}), bf16[8,128,1,2,96]{1,4,3,2,0:T(8,128)(2,1)S(1)}, u32[]{:S(2)}, u32[]{:S(2)}) async-start(bf16[8,128,1,2,96]{1,4,3,2,0:T(8,128)(2,1)} %broadcast_in_dim.73), calls=%async_computation.7 | async-start | bytes 786432 | tf_op jit(solution)/shard_map/all_to_all | solution.py:165
  180.7 5.5 %all-to-all-done.7 = bf16[8,128,1,2,96]{1,4,3,2,0:T(8,128)(2,1)S(1)} async-done(((bf16[8,128,1,2,96]{1,4,3,2,0:T(8,128)(2,1)}), bf16[8,128,1,2,96]{1,4,3,2,0:T(8,128)(2,1)S(1)}, u32[]{:S(2)}, u32[]{:S(2)}) %all-to-all-start.7) | async-done | bytes 393248 | tf_op jit(solution)/shard_map/all_to_all | solution.py:165
  186.3 1.6 fusion.122
  188.9 13.6 %all_to_all.78 = bf16[1,8,16,768]{3,2,0,1:T(8,128)(2,1)S(1)} all-to-all(bf16[1,8,16,768]{3,2,0,1:T(8,128)(2,1)S(1)} %bitcast.295), channel_id=1, replica_groups=mesh['row'=8,'col'=8,'smp'=8] {'col'}, dimensions={1} | all-to-all | bytes 393216 | tf_op jit(solution)/shard_map/all_to_all | solution.py:173
  203.0 12.7 %all_to_all.79 = bf16[1,8,16,768]{3,2,0,1:T(8,128)(2,1)S(1)} all-to-all(bf16[1,8,16,768]{3,2,0,1:T(8,128)(2,1)S(1)} %broadcast_in_dim.74), channel_id=1, replica_groups=mesh['row'=8,'col'=8,'smp'=8] {'col'}, dimensions={1} | all-to-all | bytes 393216 | tf_op jit(solution)/shard_map/all_to_all | solution.py:165
  217.6 5.1 %all-to-all-start.10 = ((bf16[8,128,1,2,96]{1,4,3,2,0:T(8,128)(2,1)}), bf16[8,128,1,2,96]{1,4,3,2,0:T(8,128)(2,1)S(1)}, u32[]{:S(2)}, u32[]{:S(2)}) async-start(bf16[8,128,1,2,96]{1,4,3,2,0:T(8,128)(2,1)} %broadcast_in_dim.75), calls=%async_computation.10 | async-start | bytes 786432 | tf_op jit(solution)/shard_map/all_to_all | solution.py:165
  224.0 5.6 %all-to-all-done.10 = bf16[8,128,1,2,96]{1,4,3,2,0:T(8,128)(2,1)S(1)} async-done(((bf16[8,128,1,2,96]{1,4,3,2,0:T(8,128)(2,1)}), bf16[8,128,1,2,96]{1,4,3,2,0:T(8,128)(2,1)S(1)}, u32[]{:S(2)}, u32[]{:S(2)}) %all-to-all-start.10) | async-done | bytes 393248 | tf_op jit(solution)/shard_map/all_to_all | solution.py:165
  229.7 1.6 fusion.123
  232.3 13.6 %all_to_all.80 = bf16[1,8,16,768]{3,2,0,1:T(8,128)(2,1)S(1)} all-to-all(bf16[1,8,16,768]{3,2,0,1:T(8,128)(2,1)S(1)} %bitcast.296), channel_id=1, replica_groups=mesh['row'=8,'col'=8,'smp'=8] {'col'}, dimensions={1} | all-to-all | bytes 393216 | tf_op jit(solution)/shard_map/all_to_all | solution.py:173
  246.6 3.4 %all-to-all-start.12 = ((bf16[1,8,16,768]{3,2,0,1:T(8,128)(2,1)}), bf16[1,8,16,768]{3,2,0,1:T(8,128)(2,1)S(1)}, u32[]{:S(2)}, u32[]{:S(2)}) async-start(bf16[1,8,16,768]{3,2,0,1:T(8,128)(2,1)} %broadcast_in_dim.76), calls=%async_computation.12 | async-start | bytes 393216 | tf_op jit(solution)/shard_map/all_to_all | solution.py:165
  250.1 10.7 %all-to-all-done.12 = bf16[1,8,16,768]{3,2,0,1:T(8,128)(2,1)S(1)} async-done(((bf16[1,8,16,768]{3,2,0,1:T(8,128)(2,1)}), bf16[1,8,16,768]{3,2,0,1:T(8,128)(2,1)S(1)}, u32[]{:S(2)}, u32[]{:S(2)}) %all-to-all-start.12) | async-done | bytes 196640 | tf_op jit(solution)/shard_map/all_to_all | solution.py:165
  (134 shorter events, 26.4 us)
Async XLA Ops:
  0.6 260.7 %copy-start = (bf16[3,768]{1,0:T(4,128)(2,1)S(1)}, bf16[3,768]{1,0:T(4,128)(2,1)}, u32[]{:S(2)}) copy-start(bf16[3,768]{1,0:T(4,128)(2,1)} %param.29) | copy-start | bytes 13828
  10.3 15.8 %copy-start.7 = (f32[1,3]{1,0:T(1,128)S(1)}, f32[1,3]{1,0:T(1,128)}, u32[]{:S(2)}) copy-start(f32[1,3]{1,0:T(1,128)} %param.21) | copy-start | bytes 40
  10.3 21.4 %copy-start.5 = (f32[3,8192]{1,0:T(4,128)S(1)}, f32[3,8192]{1,0:T(4,128)}, u32[]{:S(2)}) copy-start(f32[3,8192]{1,0:T(4,128)} %param.17) | copy-start | bytes 294916
  10.3 68.8 %all-to-all-start = ((bf16[4,128,128,1,16]{2,4,3,0,1:T(8,128)(2,1)}), bf16[4,128,128,1,16]{2,4,3,0,1:T(8,128)(2,1)S(1)}, u32[]{:S(2)}, u32[]{:S(2)}) async-start(bf16[4,128,128,1,16]{2,4,3,0,1:T(8,128)(2,1)} %bitcast.285), calls=%async_computation | async-start | bytes 4194304 | tf_op jit(solution)/shard_map/all_to_all | solution.py:107
  26.1 8.2 %copy-start.12 = (s32[128]{0:T(128)S(1)}, s32[128]{0:T(128)}, u32[]{:S(2)}) copy-start(s32[128]{0:T(128)} %param.18) | copy-start | bytes 1540
  26.1 11.2 %copy-start.8 = (s32[128]{0:T(128)S(1)}, s32[128]{0:T(128)}, u32[]{:S(2)}) copy-start(s32[128]{0:T(128)} %param.19) | copy-start | bytes 1540
  26.1 11.2 %copy-start.11 = (s32[128]{0:T(128)S(1)}, s32[128]{0:T(128)}, u32[]{:S(2)}) copy-start(s32[128]{0:T(128)} %param.20) | copy-start | bytes 1540
  26.2 11.4 %copy-start.6 = (f32[4,768]{1,0:T(4,128)S(1)}, f32[4,768]{1,0:T(4,128)}, u32[]{:S(2)}) copy-start(f32[4,768]{1,0:T(4,128)} %param.24) | copy-start | bytes 36868
  31.7 6.3 %copy-start.10 = (f32[1,3,128]{2,0,1:T(1,128)S(1)}, f32[1,3,128]{2,0,1:T(1,128)}, u32[]{:S(2)}) copy-start(f32[1,3,128]{2,0,1:T(1,128)} %param.23) | copy-start | bytes 4612
  31.7 6.3 %copy-start.4 = (bf16[128,768]{1,0:T(8,128)(2,1)S(1)}, bf16[128,768]{1,0:T(8,128)(2,1)}, u32[]{:S(2)}) copy-start(bf16[128,768]{1,0:T(8,128)(2,1)} %param.15) | copy-start | bytes 589828
  79.5 8.7 %copy-start.9 = (f32[4,16]{1,0:T(4,128)S(1)}, f32[4,16]{1,0:T(4,128)}, u32[]{:S(2)}) copy-start(f32[4,16]{1,0:T(4,128)} %param.26) | copy-start | bytes 772
  80.7 14.5 %all-to-all-start.1 = ((bf16[8,128,1,2,104]{1,4,3,2,0:T(8,128)(2,1)}), bf16[8,128,1,2,104]{1,4,3,2,0:T(8,128)(2,1)S(1)}, u32[]{:S(2)}, u32[]{:S(2)}) async-start(bf16[8,128,1,2,104]{1,4,3,2,0:T(8,128)(2,1)} %broadcast_in_dim.67), calls=%async_computation.1 | async-start | bytes 851968 | tf_op jit(solution)/shard_map/all_to_all | solution.py:165
  95.5 0.8 copy-start.3
  96.3 2.4 copy-start.2
  99.5 16.0 %all-to-all-start.2 = ((bf16[1,8,16,768]{3,2,0,1:T(8,128)(2,1)}), bf16[1,8,16,768]{3,2,0,1:T(8,128)(2,1)S(1)}, u32[]{:S(2)}, u32[]{:S(2)}) async-start(bf16[1,8,16,768]{3,2,0,1:T(8,128)(2,1)} %bitcast.59), calls=%async_computation.2 | async-start | bytes 393216 | tf_op jit(solution)/shard_map/all_to_all | solution.py:173
  116.0 26.9 %copy-start.1 = (bf16[4,2,128,1024]{3,2,1,0:T(8,128)(2,1)S(1)}, bf16[4,2,128,1024]{3,2,1,0:T(8,128)(2,1)}, u32[]{:S(2)}) copy-start(bf16[4,2,128,1024]{3,2,1,0:T(8,128)(2,1)} %copy.59) | copy-start | bytes 6291460
  131.4 11.4 %all-to-all-start.4 = ((bf16[8,128,1,2,96]{1,4,3,2,0:T(8,128)(2,1)}), bf16[8,128,1,2,96]{1,4,3,2,0:T(8,128)(2,1)S(1)}, u32[]{:S(2)}, u32[]{:S(2)}) async-start(bf16[8,128,1,2,96]{1,4,3,2,0:T(8,128)(2,1)} %broadcast_in_dim.71), calls=%async_computation.4 | async-start | bytes 786432 | tf_op jit(solution)/shard_map/all_to_all | solution.py:165
  174.8 11.4 %all-to-all-start.7 = ((bf16[8,128,1,2,96]{1,4,3,2,0:T(8,128)(2,1)}), bf16[8,128,1,2,96]{1,4,3,2,0:T(8,128)(2,1)S(1)}, u32[]{:S(2)}, u32[]{:S(2)}) async-start(bf16[8,128,1,2,96]{1,4,3,2,0:T(8,128)(2,1)} %broadcast_in_dim.73), calls=%async_computation.7 | async-start | bytes 786432 | tf_op jit(solution)/shard_map/all_to_all | solution.py:165
  217.6 12.0 %all-to-all-start.10 = ((bf16[8,128,1,2,96]{1,4,3,2,0:T(8,128)(2,1)}), bf16[8,128,1,2,96]{1,4,3,2,0:T(8,128)(2,1)S(1)}, u32[]{:S(2)}, u32[]{:S(2)}) async-start(bf16[8,128,1,2,96]{1,4,3,2,0:T(8,128)(2,1)} %broadcast_in_dim.75), calls=%async_computation.10 | async-start | bytes 786432 | tf_op jit(solution)/shard_map/all_to_all | solution.py:165
  246.6 14.2 %all-to-all-start.12 = ((bf16[1,8,16,768]{3,2,0,1:T(8,128)(2,1)}), bf16[1,8,16,768]{3,2,0,1:T(8,128)(2,1)S(1)}, u32[]{:S(2)}, u32[]{:S(2)}) async-start(bf16[1,8,16,768]{3,2,0,1:T(8,128)(2,1)} %broadcast_in_dim.76), calls=%async_computation.12 | async-start | bytes 393216 | tf_op jit(solution)/shard_map/all_to_all | solution.py:165

commit v7 on v5

--- a/solution.py
+++ b/solution.py
@@ -64,15 +64,29 @@
 def relay_bias(local_bias):
     blocks, total_heads, row_count, keys_dev = local_bias.shape
     col_count = lax.axis_size("col")
+    group_members = total_heads // col_count
+    by_group = local_bias.reshape(blocks, col_count, group_members, row_count, 1, keys_dev)
+    return lax.all_to_all(by_group, "col", 1, 4, tiled=True)
+
+
+def spread_bias(column_bias):
+    blocks, _, group_members, row_count, col_count, keys_dev = column_bias.shape
     copies = lax.axis_size("smp")
-    group_members = total_heads // col_count
-    spread = jnp.broadcast_to(
-        local_bias.reshape(blocks, col_count, 1, group_members, row_count, 1, keys_dev),
-        (blocks, col_count, copies, group_members, row_count, 1, keys_dev),
-    )
-    spread = spread.reshape(blocks, col_count * copies * group_members, row_count, 1, keys_dev)
-    relayed = lax.all_to_all(spread, ("col", "smp"), split_axis=1, concat_axis=3, tiled=True)
-    return relayed.reshape(blocks, group_members, row_count, -1)
+    forward = [(i, (i + 1) % copies) for i in range(copies)]
+    backward = [(i, (i - 1) % copies) for i in range(copies)]
+    pieces = {0: column_bias}
+    rightward, leftward = column_bias, column_bias
+    for step in range(1, copies // 2 + 1):
+        rightward = lax.ppermute(rightward, "smp", forward)
+        pieces[-step] = rightward
+        if step < copies - copies // 2:
+            leftward = lax.ppermute(leftward, "smp", backward)
+            pieces[step] = leftward
+    offsets = sorted(pieces)
+    stacked = jnp.concatenate([pieces[d] for d in offsets], axis=1)
+    stacked = jnp.roll(stacked, lax.axis_index("smp") + offsets[0], axis=1)
+    stacked = jnp.transpose(stacked, (0, 2, 3, 4, 1, 5))
+    return stacked.reshape(blocks, group_members, row_count, col_count * copies * keys_dev)
 
 
 def build_absorber(
@@ -164,7 +178,8 @@
     local_bias = jnp.einsum(
         "ikc,cbh->bhik", pair_normed, pair_bias_weight, preferred_element_type=jnp.float32
     ).astype(jnp.bfloat16)
-    gathered_pair_bias = relay_bias(local_bias)
+    column_bias = relay_bias(local_bias)
+    gathered_pair_bias = spread_bias(column_bias)
     samples, row_count, model_width = hidden_activity.shape
     col_count = lax.axis_size("col")
     own_rows = row_count // col_count
@@ -194,9 +209,7 @@
             key_marks = jnp.broadcast_to(key_marks[:, None, :, None], (row_count, samples, 2, 1))
             key_marks = jnp.pad(key_marks, ((0, 0), (0, 0), (0, 0), (0, 7)))
             key_value = jnp.concatenate([key_value, key_marks], axis=3)
-            key_value, gathered_pair_bias = lax.optimization_barrier(
-                (key_value, gathered_pair_bias)
-            )
+            key_value, _ = lax.optimization_barrier((key_value, column_bias))
         gathered_key_value = gather_by_exchange(key_value, "row", 0)
         if block_index == 0:
             width = head_size * group_members

time: 262 us -> 257 us (0.981)
  waiting for transfers between devices: 82.2 us -> 53.1 us
  starting transfers between devices: 44.2 us -> 65.7 us
    all_to_all x1, waiting for transfers between devices: 39.3 us -> 0.01 us  [relay_bias(): return lax.all_to_all(by_group, 'col', 1, 4, tiled=True)]
    ppermute x0 -> x7, starting transfers between devices: none -> 28.2 us  [the longest x3 18.9 us: spread_bias(): leftward = lax.ppermute(leftward, 'smp', backward)]
    ppermute x0 -> x7, waiting for transfers between devices: none -> 16 us  [the longest x4 15.9 us: spread_bias(): rightward = lax.ppermute(rightward, 'smp', forward)]
    all_to_all x1, starting transfers between devices: 15.8 us -> 6.2 us  [relay_bias(): return lax.all_to_all(by_group, 'col', 1, 4, tiled=True)]
    all_to_all x5, waiting for transfers between devices: 31.7 us -> 26.9 us  [gather_by_exchange(): joined = lax.all_to_all(spread, axis_name, axis, axis, tiled=True)]
    dot_general x4, matrix products: 1.62 us -> 5.28 us  [body(): jnp.einsum('kxp,pj->kxj', gated_output, attention_output_weight[block_ind...]
    dot_general x4, matrix products: 6.32 us -> 2.92 us  [absorb(): jnp.einsum('sqhd,kshd->shqk', query_vectors, key_rows, preferred_element_...]
    optimization_barrier x1 -> x0, local copies, waits for them, and re-layouts: 2.74 us -> none  [body(): lax.optimization_barrier((key_value, gathered_pair_bias))]
  transfers between devices with their start and end apart: 7 -> 14, of which waited for: 7 -> 9; matrix products, arithmetic and copies ran while one was open for 6% -> 6% of each run, Pallas kernels for 0% -> 0%
where the time goes in v7:
time: 257 us; the launch traced here: 255 us
  blocking collectives  81 us (32%)
  starting transfers between devices  65.7 us (26%)
  waiting for transfers between devices  53.1 us (21%)
  matrix products  19.9 us (8%)
  local copies, waits for them, and re-layouts  19.3 us (8%)
  other arithmetic  9.72 us (4%)
  between operations  6.81 us (3%)
    all_to_all x3, blocking collectives, scatter_sum_rows(): arrived = lax.all_to_all(pieces, axis_name, 1, 1, tiled=True)  41 us
    all_to_all x3, blocking collectives, gather_by_exchange(): joined = lax.all_to_all(spread, axis_name, axis, axis, tiled=True)  39.9 us
    all_to_all x5, waiting for transfers between devices, gather_by_exchange(): joined = lax.all_to_all(spread, axis_name, axis, axis, tiled=True)  26.9 us
    all_to_all x5, starting transfers between devices, gather_by_exchange(): joined = lax.all_to_all(spread, axis_name, axis, axis, tiled=True)  25.2 us
    ppermute x3, starting transfers between devices, spread_bias(): leftward = lax.ppermute(leftward, 'smp', backward)  18.9 us
    ppermute x4, waiting for transfers between devices, spread_bias(): rightward = lax.ppermute(rightward, 'smp', forward)  15.9 us
    all_to_all x1, waiting for transfers between devices, scatter_sum_rows(): arrived = lax.all_to_all(pieces, axis_name, 1, 1, tiled=True)  10.3 us
    ppermute x4, starting transfers between devices, spread_bias(): rightward = lax.ppermute(rightward, 'smp', forward)  9.35 us
  transfers between devices with their start and end apart: 14, of which 9 were waited for; matrix products, arithmetic and copies ran while one was open for 6% of the time, Pallas kernels for 0%

profile of v7, /device:TPU:8, one launch (start us, length us, event | category | flops | bytes accessed | tf_op | source)
XLA Modules:
  0.0 255.5 jit_solution(8390035651533187647)
XLA Ops:
  6.9 6.2 %all-to-all-start = ((bf16[4,8,2,128,1,16]{3,5,2,0,4,1:T(8,128)(2,1)}), bf16[4,8,2,128,1,16]{3,5,2,0,4,1:T(8,128)(2,1)S(1)}, u32[]{:S(2)}, u32[]{:S(2)}) async-start(bf16[4,8,2,128,1,16]{3,5,2,0,4,1:T(8,128)(2,1)} %copy.51), calls=%async_computation | async-start | bytes 524288 | tf_op jit(solution)/shard_map/all_to_all | solution.py:69
  19.4 2.6 %copy.48 = f32[3,8192]{0,1:T(8,128)} copy(f32[3,8192]{1,0:T(4,128)S(1)} %copy-done.4) | data formatting | bytes 196608 | tf_op args[2]
  22.0 2.8 %gather_fusion = f32[128,3]{1,0:T(8,128)S(1)} fusion(f32[3,8192]{0,1:T(8,128)} %copy.48, s32[1024]{0:T(1024)S(1)} %pad_clamp_fusion), kind=kCustom, calls=%fused_computation | custom fusion | bytes 3584 | tf_op jit(solution)/shard_map/jit(_take)/gather | solution.py:46
  28.0 6.4 %all-to-all-start.1 = ((bf16[8,128,1,2,104]{1,4,3,2,0:T(8,128)(2,1)}), bf16[8,128,1,2,104]{1,4,3,2,0:T(8,128)(2,1)S(1)}, u32[]{:S(2)}, u32[]{:S(2)}) async-start(bf16[8,128,1,2,104]{1,4,3,2,0:T(8,128)(2,1)} %broadcast_in_dim.58), calls=%async_computation.1 | async-start | bytes 851968 | tf_op jit(solution)/shard_map/all_to_all | solution.py:146
  34.4 3.6 %collective-permute-start = (bf16[4,1,2,128,8,16]{3,5,1,4,2,0:T(8,128)(2,1)S(1)}, bf16[4,1,2,128,8,16]{3,5,1,4,2,0:T(8,128)(2,1)S(1)}, u32[]{:S(2)}, u32[]{:S(2)}) collective-permute-start(bf16[4,1,2,128,8,16]{3,5,1,4,2,0:T(8,128)(2,1)S(1)} %bitcast.305), channel_id=1, source_target_pairs={{0,1},{1,2},{2,3},{3,4},{4,5},{5,6},{6,7},{7,0},{8,9},{9,10},{10,1... | collective-permute-start | bytes 786440 | tf_op jit(solution)/shard_map/ppermute | solution.py:80
  38.0 8.6 %collective-permute-start.4 = (bf16[4,1,2,128,8,16]{3,5,1,4,2,0:T(8,128)(2,1)S(1)}, bf16[4,1,2,128,8,16]{3,5,1,4,2,0:T(8,128)(2,1)S(1)}, u32[]{:S(2)}, u32[]{:S(2)}) collective-permute-start(bf16[4,1,2,128,8,16]{3,5,1,4,2,0:T(8,128)(2,1)S(1)} %bitcast.306), channel_id=1, source_target_pairs={{0,7},{1,0},{2,1},{3,2},{4,3},{5,4},{6,5},{7,6},{8,15},{9,8},{10,9... | collective-permute-start | bytes 786440 | tf_op jit(solution)/shard_map/ppermute | solution.py:83
  47.9 3.2 %collective-permute-done = bf16[4,1,2,128,8,16]{3,5,1,4,2,0:T(8,128)(2,1)S(1)} collective-permute-done((bf16[4,1,2,128,8,16]{3,5,1,4,2,0:T(8,128)(2,1)S(1)}, bf16[4,1,2,128,8,16]{3,5,1,4,2,0:T(8,128)(2,1)S(1)}, u32[]{:S(2)}, u32[]{:S(2)}) %collective-permute-start) | collective-permute-done | bytes 262176 | tf_op jit(solution)/shard_map/ppermute | solution.py:80
  51.1 1.9 collective-permute-start.1
  53.0 5.1 %collective-permute-start.5 = (bf16[4,1,2,128,8,16]{3,5,1,4,2,0:T(8,128)(2,1)S(1)}, bf16[4,1,2,128,8,16]{3,5,1,4,2,0:T(8,128)(2,1)S(1)}, u32[]{:S(2)}, u32[]{:S(2)}) collective-permute-start(bf16[4,1,2,128,8,16]{3,5,1,4,2,0:T(8,128)(2,1)S(1)} %collective-permute-done.4), channel_id=1, source_target_pairs={{0,7},{1,0},{2,1},{3,2},{4,3},{5,4},{6,5},{7,6},{8,15},{9,8},{10,9... | collective-permute-start | bytes 786440 | tf_op jit(solution)/shard_map/ppermute | solution.py:83
  58.3 3.5 %collective-permute-done.1 = bf16[4,1,2,128,8,16]{3,5,1,4,2,0:T(8,128)(2,1)S(1)} collective-permute-done((bf16[4,1,2,128,8,16]{3,5,1,4,2,0:T(8,128)(2,1)S(1)}, bf16[4,1,2,128,8,16]{3,5,1,4,2,0:T(8,128)(2,1)S(1)}, u32[]{:S(2)}, u32[]{:S(2)}) %collective-permute-start.1) | collective-permute-done | bytes 262176 | tf_op jit(solution)/shard_map/ppermute | solution.py:80
  61.8 1.9 collective-permute-start.2
  63.7 5.1 %collective-permute-start.6 = (bf16[4,1,2,128,8,16]{3,5,1,4,2,0:T(8,128)(2,1)S(1)}, bf16[4,1,2,128,8,16]{3,5,1,4,2,0:T(8,128)(2,1)S(1)}, u32[]{:S(2)}, u32[]{:S(2)}) collective-permute-start(bf16[4,1,2,128,8,16]{3,5,1,4,2,0:T(8,128)(2,1)S(1)} %collective-permute-done.5), channel_id=1, source_target_pairs={{0,7},{1,0},{2,1},{3,2},{4,3},{5,4},{6,5},{7,6},{8,15},{9,8},{10,9... | collective-permute-start | bytes 786440 | tf_op jit(solution)/shard_map/ppermute | solution.py:83
  69.1 2.5 collective-permute-done.2
  71.6 1.9 collective-permute-start.3
  74.3 6.8 %collective-permute-done.3 = bf16[4,1,2,128,8,16]{3,5,1,4,2,0:T(8,128)(2,1)S(1)} collective-permute-done((bf16[4,1,2,128,8,16]{3,5,1,4,2,0:T(8,128)(2,1)S(1)}, bf16[4,1,2,128,8,16]{3,5,1,4,2,0:T(8,128)(2,1)S(1)}, u32[]{:S(2)}, u32[]{:S(2)}) %collective-permute-start.3) | collective-permute-done | bytes 262176 | tf_op jit(solution)/shard_map/ppermute | solution.py:80
  86.8 1.8 convolution_convert_fusion.4
  88.7 6.1 %all-to-all-start.2 = ((bf16[1,8,16,768]{3,2,0,1:T(8,128)(2,1)}), bf16[1,8,16,768]{3,2,0,1:T(8,128)(2,1)S(1)}, u32[]{:S(2)}, u32[]{:S(2)}) async-start(bf16[1,8,16,768]{3,2,0,1:T(8,128)(2,1)} %bitcast.61), calls=%async_computation.2 | async-start | bytes 393216 | tf_op jit(solution)/shard_map/all_to_all | solution.py:154
  94.8 10.3 %all-to-all-done.2 = bf16[1,8,16,768]{3,2,0,1:T(8,128)(2,1)S(1)} async-done(((bf16[1,8,16,768]{3,2,0,1:T(8,128)(2,1)}), bf16[1,8,16,768]{3,2,0,1:T(8,128)(2,1)S(1)}, u32[]{:S(2)}, u32[]{:S(2)}) %all-to-all-start.2) | async-done | bytes 196640 | tf_op jit(solution)/shard_map/all_to_all | solution.py:154
  106.3 14.1 %all_to_all.78 = bf16[1,8,16,768]{3,2,0,1:T(8,128)(2,1)S(1)} all-to-all(bf16[1,8,16,768]{3,2,0,1:T(8,128)(2,1)S(1)} %broadcast_in_dim.61), channel_id=1, replica_groups=mesh['row'=8,'col'=8,'smp'=8] {'col'}, dimensions={1} | all-to-all | bytes 393216 | tf_op jit(solution)/shard_map/all_to_all | solution.py:146
  122.3 5.6 %all-to-all-start.4 = ((bf16[8,128,1,2,96]{1,4,3,2,0:T(8,128)(2,1)}), bf16[8,128,1,2,96]{1,4,3,2,0:T(8,128)(2,1)}, u32[]{:S(2)}, u32[]{:S(2)}) async-start(bf16[8,128,1,2,96]{1,4,3,2,0:T(8,128)(2,1)} %broadcast_in_dim.62), calls=%async_computation.4 | async-start | bytes 786432 | tf_op jit(solution)/shard_map/all_to_all | solution.py:146
  129.4 5.5 %all-to-all-done.4 = bf16[8,128,1,2,96]{1,4,3,2,0:T(8,128)(2,1)} async-done(((bf16[8,128,1,2,96]{1,4,3,2,0:T(8,128)(2,1)}), bf16[8,128,1,2,96]{1,4,3,2,0:T(8,128)(2,1)}, u32[]{:S(2)}, u32[]{:S(2)}) %all-to-all-start.4) | async-done | bytes 393248 | tf_op jit(solution)/shard_map/all_to_all | solution.py:146
  138.3 13.6 %all_to_all.79 = bf16[1,8,16,768]{3,2,0,1:T(8,128)(2,1)S(1)} all-to-all(bf16[1,8,16,768]{3,2,0,1:T(8,128)(2,1)S(1)} %bitcast.292), channel_id=1, replica_groups=mesh['row'=8,'col'=8,'smp'=8] {'col'}, dimensions={1} | all-to-all | bytes 393216 | tf_op jit(solution)/shard_map/all_to_all | solution.py:154
  152.4 12.7 %all_to_all.80 = bf16[1,8,16,768]{3,2,0,1:T(8,128)(2,1)S(1)} all-to-all(bf16[1,8,16,768]{3,2,0,1:T(8,128)(2,1)S(1)} %broadcast_in_dim.63), channel_id=1, replica_groups=mesh['row'=8,'col'=8,'smp'=8] {'col'}, dimensions={1} | all-to-all | bytes 393216 | tf_op jit(solution)/shard_map/all_to_all | solution.py:146
  167.1 5.2 %all-to-all-start.7 = ((bf16[8,128,1,2,96]{1,4,3,2,0:T(8,128)(2,1)}), bf16[8,128,1,2,96]{1,4,3,2,0:T(8,128)(2,1)S(1)}, u32[]{:S(2)}, u32[]{:S(2)}) async-start(bf16[8,128,1,2,96]{1,4,3,2,0:T(8,128)(2,1)} %broadcast_in_dim.64), calls=%async_computation.7 | async-start | bytes 786432 | tf_op jit(solution)/shard_map/all_to_all | solution.py:146
  173.8 5.3 %all-to-all-done.7 = bf16[8,128,1,2,96]{1,4,3,2,0:T(8,128)(2,1)S(1)} async-done(((bf16[8,128,1,2,96]{1,4,3,2,0:T(8,128)(2,1)}), bf16[8,128,1,2,96]{1,4,3,2,0:T(8,128)(2,1)S(1)}, u32[]{:S(2)}, u32[]{:S(2)}) %all-to-all-start.7) | async-done | bytes 393248 | tf_op jit(solution)/shard_map/all_to_all | solution.py:146
  181.5 13.8 %all_to_all.81 = bf16[1,8,16,768]{3,2,0,1:T(8,128)(2,1)S(1)} all-to-all(bf16[1,8,16,768]{3,2,0,1:T(8,128)(2,1)S(1)} %bitcast.293), channel_id=1, replica_groups=mesh['row'=8,'col'=8,'smp'=8] {'col'}, dimensions={1} | all-to-all | bytes 393216 | tf_op jit(solution)/shard_map/all_to_all | solution.py:154
  195.8 13.2 %all_to_all.82 = bf16[1,8,16,768]{3,2,0,1:T(8,128)(2,1)S(1)} all-to-all(bf16[1,8,16,768]{3,2,0,1:T(8,128)(2,1)S(1)} %broadcast_in_dim.65), channel_id=1, replica_groups=mesh['row'=8,'col'=8,'smp'=8] {'col'}, dimensions={1} | all-to-all | bytes 393216 | tf_op jit(solution)/shard_map/all_to_all | solution.py:146
  211.0 4.6 %all-to-all-start.10 = ((bf16[8,128,1,2,96]{1,4,3,2,0:T(8,128)(2,1)}), bf16[8,128,1,2,96]{1,4,3,2,0:T(8,128)(2,1)S(1)}, u32[]{:S(2)}, u32[]{:S(2)}) async-start(bf16[8,128,1,2,96]{1,4,3,2,0:T(8,128)(2,1)} %broadcast_in_dim.66), calls=%async_computation.10 | async-start | bytes 786432 | tf_op jit(solution)/shard_map/all_to_all | solution.py:146
  217.1 5.4 %all-to-all-done.10 = bf16[8,128,1,2,96]{1,4,3,2,0:T(8,128)(2,1)S(1)} async-done(((bf16[8,128,1,2,96]{1,4,3,2,0:T(8,128)(2,1)}), bf16[8,128,1,2,96]{1,4,3,2,0:T(8,128)(2,1)S(1)}, u32[]{:S(2)}, u32[]{:S(2)}) %all-to-all-start.10) | async-done | bytes 393248 | tf_op jit(solution)/shard_map/all_to_all | solution.py:146
  224.9 13.6 %all_to_all.83 = bf16[1,8,16,768]{3,2,0,1:T(8,128)(2,1)S(1)} all-to-all(bf16[1,8,16,768]{3,2,0,1:T(8,128)(2,1)S(1)} %bitcast.294), channel_id=1, replica_groups=mesh['row'=8,'col'=8,'smp'=8] {'col'}, dimensions={1} | all-to-all | bytes 393216 | tf_op jit(solution)/shard_map/all_to_all | solution.py:154
  239.3 3.4 %all-to-all-start.12 = ((bf16[1,8,16,768]{3,2,0,1:T(8,128)(2,1)}), bf16[1,8,16,768]{3,2,0,1:T(8,128)(2,1)S(1)}, u32[]{:S(2)}, u32[]{:S(2)}) async-start(bf16[1,8,16,768]{3,2,0,1:T(8,128)(2,1)} %broadcast_in_dim.67), calls=%async_computation.12 | async-start | bytes 393216 | tf_op jit(solution)/shard_map/all_to_all | solution.py:146
  242.7 10.7 %all-to-all-done.12 = bf16[1,8,16,768]{3,2,0,1:T(8,128)(2,1)S(1)} async-done(((bf16[1,8,16,768]{3,2,0,1:T(8,128)(2,1)}), bf16[1,8,16,768]{3,2,0,1:T(8,128)(2,1)S(1)}, u32[]{:S(2)}, u32[]{:S(2)}) %all-to-all-start.12) | async-done | bytes 196640 | tf_op jit(solution)/shard_map/all_to_all | solution.py:146
  (169 shorter events, 41.6 us)
Async XLA Ops:
  0.6 5.0 %copy-start = (bf16[128,4,16]{0,2,1:T(8,128)(2,1)S(1)}, bf16[128,4,16]{0,2,1:T(8,128)(2,1)}, u32[]{:S(2)}) copy-start(bf16[128,4,16]{0,2,1:T(8,128)(2,1)} %param.25) | copy-start | bytes 49156
  0.6 12.5 %copy-start.7 = (f32[1,3]{1,0:T(1,128)S(1)}, f32[1,3]{1,0:T(1,128)}, u32[]{:S(2)}) copy-start(f32[1,3]{1,0:T(1,128)} %param.21) | copy-start | bytes 40
  0.7 17.6 %copy-start.12 = (s32[128]{0:T(128)S(1)}, s32[128]{0:T(128)}, u32[]{:S(2)}) copy-start(s32[128]{0:T(128)} %param.18) | copy-start | bytes 1540
  0.7 18.7 %copy-start.4 = (f32[3,8192]{1,0:T(4,128)S(1)}, f32[3,8192]{1,0:T(4,128)}, u32[]{:S(2)}) copy-start(f32[3,8192]{1,0:T(4,128)} %param.17) | copy-start | bytes 294916
  2.1 23.0 %copy-start.10 = (f32[1,3,128]{2,0,1:T(1,128)S(1)}, f32[1,3,128]{2,0,1:T(1,128)}, u32[]{:S(2)}) copy-start(f32[1,3,128]{2,0,1:T(1,128)} %param.23) | copy-start | bytes 4612
  2.1 23.1 %copy-start.5 = (f32[4,768]{1,0:T(4,128)S(1)}, f32[4,768]{1,0:T(4,128)}, u32[]{:S(2)}) copy-start(f32[4,768]{1,0:T(4,128)} %param.24) | copy-start | bytes 36868
  2.1 23.1 %copy-start.3 = (bf16[128,768]{1,0:T(8,128)(2,1)S(1)}, bf16[128,768]{1,0:T(8,128)(2,1)}, u32[]{:S(2)}) copy-start(bf16[128,768]{1,0:T(8,128)(2,1)} %param.15) | copy-start | bytes 589828
  3.9 21.9 %copy-start.8 = (s32[128]{0:T(128)S(1)}, s32[128]{0:T(128)}, u32[]{:S(2)}) copy-start(s32[128]{0:T(128)} %param.19) | copy-start | bytes 1540
  3.9 21.9 %copy-start.11 = (s32[128]{0:T(128)S(1)}, s32[128]{0:T(128)}, u32[]{:S(2)}) copy-start(s32[128]{0:T(128)} %param.20) | copy-start | bytes 1540
  6.9 20.2 %all-to-all-start = ((bf16[4,8,2,128,1,16]{3,5,2,0,4,1:T(8,128)(2,1)}), bf16[4,8,2,128,1,16]{3,5,2,0,4,1:T(8,128)(2,1)S(1)}, u32[]{:S(2)}, u32[]{:S(2)}) async-start(bf16[4,8,2,128,1,16]{3,5,2,0,4,1:T(8,128)(2,1)} %copy.51), calls=%async_computation | async-start | bytes 524288 | tf_op jit(solution)/shard_map/all_to_all | solution.py:69
  19.4 28.5 %copy-start.9 = (f32[4,16]{1,0:T(4,128)S(1)}, f32[4,16]{1,0:T(4,128)}, u32[]{:S(2)}) copy-start(f32[4,16]{1,0:T(4,128)} %param.26) | copy-start | bytes 772
  25.6 27.4 %copy-start.1 = (bf16[128,768]{1,0:T(8,128)(2,1)}, bf16[128,768]{1,0:T(8,128)(2,1)S(1)}, u32[]{:S(2)}) copy-start(bf16[128,768]{1,0:T(8,128)(2,1)S(1)} %get-tuple-element.29) | copy-start | bytes 589828
  28.0 40.9 %all-to-all-start.1 = ((bf16[8,128,1,2,104]{1,4,3,2,0:T(8,128)(2,1)}), bf16[8,128,1,2,104]{1,4,3,2,0:T(8,128)(2,1)S(1)}, u32[]{:S(2)}, u32[]{:S(2)}) async-start(bf16[8,128,1,2,104]{1,4,3,2,0:T(8,128)(2,1)} %broadcast_in_dim.58), calls=%async_computation.1 | async-start | bytes 851968 | tf_op jit(solution)/shard_map/all_to_all | solution.py:146
  34.4 16.7 %collective-permute-start = (bf16[4,1,2,128,8,16]{3,5,1,4,2,0:T(8,128)(2,1)S(1)}, bf16[4,1,2,128,8,16]{3,5,1,4,2,0:T(8,128)(2,1)S(1)}, u32[]{:S(2)}, u32[]{:S(2)}) collective-permute-start(bf16[4,1,2,128,8,16]{3,5,1,4,2,0:T(8,128)(2,1)S(1)} %bitcast.305), channel_id=1, source_target_pairs={{0,1},{1,2},{2,3},{3,4},{4,5},{5,6},{6,7},{7,0},{8,9},{9,10},{10,1... | collective-permute-start | bytes 786440 | tf_op jit(solution)/shard_map/ppermute | solution.py:80
  38.0 15.0 %collective-permute-start.4 = (bf16[4,1,2,128,8,16]{3,5,1,4,2,0:T(8,128)(2,1)S(1)}, bf16[4,1,2,128,8,16]{3,5,1,4,2,0:T(8,128)(2,1)S(1)}, u32[]{:S(2)}, u32[]{:S(2)}) collective-permute-start(bf16[4,1,2,128,8,16]{3,5,1,4,2,0:T(8,128)(2,1)S(1)} %bitcast.306), channel_id=1, source_target_pairs={{0,7},{1,0},{2,1},{3,2},{4,3},{5,4},{6,5},{7,6},{8,15},{9,8},{10,9... | collective-permute-start | bytes 786440 | tf_op jit(solution)/shard_map/ppermute | solution.py:83
  51.1 10.7 %collective-permute-start.1 = (bf16[4,1,2,128,8,16]{3,5,1,4,2,0:T(8,128)(2,1)S(1)}, bf16[4,1,2,128,8,16]{3,5,1,4,2,0:T(8,128)(2,1)S(1)}, u32[]{:S(2)}, u32[]{:S(2)}) collective-permute-start(bf16[4,1,2,128,8,16]{3,5,1,4,2,0:T(8,128)(2,1)S(1)} %collective-permute-done), channel_id=1, source_target_pairs={{0,1},{1,2},{2,3},{3,4},{4,5},{5,6},{6,7},{7,0},{8,9},{9,10},{10,1... | collective-permute-start | bytes 786440 | tf_op jit(solution)/shard_map/ppermute | solution.py:80
  53.0 10.7 %collective-permute-start.5 = (bf16[4,1,2,128,8,16]{3,5,1,4,2,0:T(8,128)(2,1)S(1)}, bf16[4,1,2,128,8,16]{3,5,1,4,2,0:T(8,128)(2,1)S(1)}, u32[]{:S(2)}, u32[]{:S(2)}) collective-permute-start(bf16[4,1,2,128,8,16]{3,5,1,4,2,0:T(8,128)(2,1)S(1)} %collective-permute-done.4), channel_id=1, source_target_pairs={{0,7},{1,0},{2,1},{3,2},{4,3},{5,4},{6,5},{7,6},{8,15},{9,8},{10,9... | collective-permute-start | bytes 786440 | tf_op jit(solution)/shard_map/ppermute | solution.py:83
  61.8 9.8 %collective-permute-start.2 = (bf16[4,1,2,128,8,16]{3,5,1,4,2,0:T(8,128)(2,1)S(1)}, bf16[4,1,2,128,8,16]{3,5,1,4,2,0:T(8,128)(2,1)S(1)}, u32[]{:S(2)}, u32[]{:S(2)}) collective-permute-start(bf16[4,1,2,128,8,16]{3,5,1,4,2,0:T(8,128)(2,1)S(1)} %collective-permute-done.1), channel_id=1, source_target_pairs={{0,1},{1,2},{2,3},{3,4},{4,5},{5,6},{6,7},{7,0},{8,9},{9,10},{10,1... | collective-permute-start | bytes 786440 | tf_op jit(solution)/shard_map/ppermute | solution.py:80
  63.7 17.7 %collective-permute-start.6 = (bf16[4,1,2,128,8,16]{3,5,1,4,2,0:T(8,128)(2,1)S(1)}, bf16[4,1,2,128,8,16]{3,5,1,4,2,0:T(8,128)(2,1)S(1)}, u32[]{:S(2)}, u32[]{:S(2)}) collective-permute-start(bf16[4,1,2,128,8,16]{3,5,1,4,2,0:T(8,128)(2,1)S(1)} %collective-permute-done.5), channel_id=1, source_target_pairs={{0,7},{1,0},{2,1},{3,2},{4,3},{5,4},{6,5},{7,6},{8,15},{9,8},{10,9... | collective-permute-start | bytes 786440 | tf_op jit(solution)/shard_map/ppermute | solution.py:83
  71.6 9.5 %collective-permute-start.3 = (bf16[4,1,2,128,8,16]{3,5,1,4,2,0:T(8,128)(2,1)S(1)}, bf16[4,1,2,128,8,16]{3,5,1,4,2,0:T(8,128)(2,1)S(1)}, u32[]{:S(2)}, u32[]{:S(2)}) collective-permute-start(bf16[4,1,2,128,8,16]{3,5,1,4,2,0:T(8,128)(2,1)S(1)} %collective-permute-done.2), channel_id=1, source_target_pairs={{0,1},{1,2},{2,3},{3,4},{4,5},{5,6},{6,7},{7,0},{8,9},{9,10},{10,1... | collective-permute-start | bytes 786440 | tf_op jit(solution)/shard_map/ppermute | solution.py:80
  82.3 4.2 %copy-start.2 = (bf16[1024,1,1,96]{0,3,2,1:T(8,128)(2,1)S(1)}, bf16[1024,1,1,96]{0,3,2,1:T(8,128)(2,1)}, u32[]{:S(2)}) copy-start(bf16[1024,1,1,96]{0,3,2,1:T(8,128)(2,1)} %get-tuple-element.37) | copy-start | bytes 589828
  88.7 16.4 %all-to-all-start.2 = ((bf16[1,8,16,768]{3,2,0,1:T(8,128)(2,1)}), bf16[1,8,16,768]{3,2,0,1:T(8,128)(2,1)S(1)}, u32[]{:S(2)}, u32[]{:S(2)}) async-start(bf16[1,8,16,768]{3,2,0,1:T(8,128)(2,1)} %bitcast.61), calls=%async_computation.2 | async-start | bytes 393216 | tf_op jit(solution)/shard_map/all_to_all | solution.py:154
  122.3 12.6 %all-to-all-start.4 = ((bf16[8,128,1,2,96]{1,4,3,2,0:T(8,128)(2,1)}), bf16[8,128,1,2,96]{1,4,3,2,0:T(8,128)(2,1)}, u32[]{:S(2)}, u32[]{:S(2)}) async-start(bf16[8,128,1,2,96]{1,4,3,2,0:T(8,128)(2,1)} %broadcast_in_dim.62), calls=%async_computation.4 | async-start | bytes 786432 | tf_op jit(solution)/shard_map/all_to_all | solution.py:146
  167.1 12.0 %all-to-all-start.7 = ((bf16[8,128,1,2,96]{1,4,3,2,0:T(8,128)(2,1)}), bf16[8,128,1,2,96]{1,4,3,2,0:T(8,128)(2,1)S(1)}, u32[]{:S(2)}, u32[]{:S(2)}) async-start(bf16[8,128,1,2,96]{1,4,3,2,0:T(8,128)(2,1)} %broadcast_in_dim.64), calls=%async_computation.7 | async-start | bytes 786432 | tf_op jit(solution)/shard_map/all_to_all | solution.py:146
  211.0 11.4 %all-to-all-start.10 = ((bf16[8,128,1,2,96]{1,4,3,2,0:T(8,128)(2,1)}), bf16[8,128,1,2,96]{1,4,3,2,0:T(8,128)(2,1)S(1)}, u32[]{:S(2)}, u32[]{:S(2)}) async-start(bf16[8,128,1,2,96]{1,4,3,2,0:T(8,128)(2,1)} %broadcast_in_dim.66), calls=%async_computation.10 | async-start | bytes 786432 | tf_op jit(solution)/shard_map/all_to_all | solution.py:146
  222.5 31.5 %copy-start.6 = (bf16[3,768]{1,0:T(4,128)(2,1)S(1)}, bf16[3,768]{1,0:T(4,128)(2,1)}, u32[]{:S(2)}) copy-start(bf16[3,768]{1,0:T(4,128)(2,1)} %param.29) | copy-start | bytes 13828
  239.3 14.2 %all-to-all-start.12 = ((bf16[1,8,16,768]{3,2,0,1:T(8,128)(2,1)}), bf16[1,8,16,768]{3,2,0,1:T(8,128)(2,1)S(1)}, u32[]{:S(2)}, u32[]{:S(2)}) async-start(bf16[1,8,16,768]{3,2,0,1:T(8,128)(2,1)} %broadcast_in_dim.67), calls=%async_computation.12 | async-start | bytes 393216 | tf_op jit(solution)/shard_map/all_to_all | solution.py:146

commit v8 on v7

--- a/solution.py
+++ b/solution.py
@@ -179,14 +179,15 @@
         "ikc,cbh->bhik", pair_normed, pair_bias_weight, preferred_element_type=jnp.float32
     ).astype(jnp.bfloat16)
     column_bias = relay_bias(local_bias)
-    gathered_pair_bias = spread_bias(column_bias)
+    first_bias = spread_bias(column_bias[:1])
+    later_bias = spread_bias(column_bias[1:])
     samples, row_count, model_width = hidden_activity.shape
     col_count = lax.axis_size("col")
     own_rows = row_count // col_count
     own_start = lax.axis_index("col") * own_rows
     own_hidden = lax.dynamic_slice_in_dim(hidden_activity, own_start, own_rows, 1)
     normed = layer_norm(hidden_activity.astype(jnp.float32)).astype(jnp.bfloat16)
-    group_members = gathered_pair_bias.shape[1]
+    group_members = first_bias.shape[1]
     head_size = query_key_value_gate_weight.shape[2] // group_members
     group_offset = lax.axis_index("col") * group_members
     input_scaling = head_size ** (-0.5)
@@ -224,7 +225,7 @@
         )
         absorb = build_absorber(
             query_vectors,
-            gathered_pair_bias[block_index],
+            first_bias[0] if block_index == 0 else later_bias[block_index - 1],
             chain_offset,
             chain_label,
             gathered_chain_ids,

time: 257 us -> 274 us (1.066)
  starting transfers between devices: 65.7 us -> 90.9 us
  waiting for transfers between devices: 53.1 us -> 33.6 us
  local copies, waits for them, and re-layouts: 19.3 us -> 36.5 us
  blocking collectives: 81 us -> 71 us
    all_to_all x3 -> x2, blocking collectives: 39.9 us -> 25.9 us  [gather_by_exchange(): joined = lax.all_to_all(spread, axis_name, axis, axis, tiled=True)]
    unnamed x45 -> x66, local copies, waits for them, and re-layouts: 4.68 us -> 16.7 us
    all_to_all x1, waiting for transfers between devices: 10.3 us -> 0.01 us  [scatter_sum_rows(): arrived = lax.all_to_all(pieces, axis_name, 1, 1, tiled=True)]
    ppermute x4 -> x8, starting transfers between devices: 9.35 us -> 18.3 us  [spread_bias(): rightward = lax.ppermute(rightward, 'smp', forward)]
    ppermute x3 -> x6, starting transfers between devices: 18.9 us -> 27.1 us  [spread_bias(): leftward = lax.ppermute(leftward, 'smp', backward)]
    ppermute x4 -> x8, waiting for transfers between devices: 15.9 us -> 8.89 us  [spread_bias(): rightward = lax.ppermute(rightward, 'smp', forward)]
    all_to_all x5 -> x6, starting transfers between devices: 25.2 us -> 32.1 us  [gather_by_exchange(): joined = lax.all_to_all(spread, axis_name, axis, axis, tiled=True)]
    all_to_all x5 -> x6, waiting for transfers between devices: 26.9 us -> 21.2 us  [gather_by_exchange(): joined = lax.all_to_all(spread, axis_name, axis, axis, tiled=True)]
  transfers between devices with their start and end apart: 14 -> 22, of which waited for: 9 -> 7; matrix products, arithmetic and copies ran while one was open for 6% -> 16% of each run, Pallas kernels for 0% -> 0%
where the time goes in v8:
time: 274 us; the launch traced here: 272 us
  starting transfers between devices  90.9 us (33%)
  blocking collectives  71 us (26%)
  local copies, waits for them, and re-layouts  36.5 us (13%)
  waiting for transfers between devices  33.6 us (12%)
  matrix products  22 us (8%)
  other arithmetic  10.7 us (4%)
  between operations  6.88 us (3%)
    all_to_all x3, blocking collectives, scatter_sum_rows(): arrived = lax.all_to_all(pieces, axis_name, 1, 1, tiled=True)  45.1 us
    all_to_all x6, starting transfers between devices, gather_by_exchange(): joined = lax.all_to_all(spread, axis_name, axis, axis, tiled=True)  32.1 us
    ppermute x6, starting transfers between devices, spread_bias(): leftward = lax.ppermute(leftward, 'smp', backward)  27.1 us
    all_to_all x2, blocking collectives, gather_by_exchange(): joined = lax.all_to_all(spread, axis_name, axis, axis, tiled=True)  25.9 us
    all_to_all x6, waiting for transfers between devices, gather_by_exchange(): joined = lax.all_to_all(spread, axis_name, axis, axis, tiled=True)  21.2 us
    ppermute x8, starting transfers between devices, spread_bias(): rightward = lax.ppermute(rightward, 'smp', forward)  18.3 us
    unnamed x66, local copies, waits for them, and re-layouts  16.7 us
    ppermute x8, waiting for transfers between devices, spread_bias(): rightward = lax.ppermute(rightward, 'smp', forward)  8.89 us
  transfers between devices with their start and end apart: 22, of which 7 were waited for; matrix products, arithmetic and copies ran while one was open for 16% of the time, Pallas kernels for 0%

profile of v8, /device:TPU:8, one launch (start us, length us, event | category | flops | bytes accessed | tf_op | source)
XLA Modules:
  0.0 271.5 jit_solution(14928001324937865851)
XLA Ops:
  6.9 6.2 %all-to-all-start.1 = ((bf16[4,8,2,128,1,16]{3,5,2,0,4,1:T(8,128)(2,1)}), bf16[4,8,2,128,1,16]{3,5,2,0,4,1:T(8,128)(2,1)S(1)}, u32[]{:S(2)}, u32[]{:S(2)}) async-start(bf16[4,8,2,128,1,16]{3,5,2,0,4,1:T(8,128)(2,1)} %copy.56), calls=%async_computation.1 | async-start | bytes 524288 | tf_op jit(solution)/shard_map/all_to_all | solution.py:69
  19.3 2.6 copy.52
  22.0 2.8 %gather_fusion = f32[128,3]{1,0:T(8,128)S(1)} fusion(f32[3,8192]{0,1:T(8,128)} %copy.52, s32[1024]{0:T(1024)S(1)} %pad_clamp_fusion), kind=kCustom, calls=%fused_computation | custom fusion | bytes 3584 | tf_op jit(solution)/shard_map/jit(_take)/gather | solution.py:46
  29.2 6.4 %all-to-all-start = ((bf16[8,128,1,2,104]{1,4,3,2,0:T(8,128)(2,1)}), bf16[8,128,1,2,104]{1,4,3,2,0:T(8,128)(2,1)S(1)}, u32[]{:S(2)}, u32[]{:S(2)}) async-start(bf16[8,128,1,2,104]{1,4,3,2,0:T(8,128)(2,1)} %broadcast_in_dim.58), calls=%async_computation | async-start | bytes 851968 | tf_op jit(solution)/shard_map/all_to_all | solution.py:146
  35.6 3.6 %collective-permute-start = (bf16[1,1,2,128,8,16]{3,5,1,4,2,0:T(8,128)(2,1)S(1)}, bf16[1,1,2,128,8,16]{3,5,1,4,2,0:T(8,128)(2,1)S(1)}, u32[]{:S(2)}, u32[]{:S(2)}) collective-permute-start(bf16[1,1,2,128,8,16]{3,5,1,4,2,0:T(8,128)(2,1)S(1)} %slice_bitcast_fusion.1), channel_id=1, source_target_pairs={{0,1},{1,2},{2,3},{3,4},{4,5},{5,6},{6,7},{7,0},{8,9},{9,10},{10,1... | collective-permute-start | bytes 196616 | tf_op jit(solution)/shard_map/ppermute | solution.py:80
  39.3 8.9 %collective-permute-done = bf16[1,1,2,128,8,16]{3,5,1,4,2,0:T(8,128)(2,1)S(1)} collective-permute-done((bf16[1,1,2,128,8,16]{3,5,1,4,2,0:T(8,128)(2,1)S(1)}, bf16[1,1,2,128,8,16]{3,5,1,4,2,0:T(8,128)(2,1)S(1)}, u32[]{:S(2)}, u32[]{:S(2)}) %collective-permute-start) | collective-permute-done | bytes 65568 | tf_op jit(solution)/shard_map/ppermute | solution.py:80
  50.8 5.1 %collective-permute-start.4 = (bf16[1,1,2,128,8,16]{3,5,1,4,2,0:T(8,128)(2,1)S(1)}, bf16[1,1,2,128,8,16]{3,5,1,4,2,0:T(8,128)(2,1)S(1)}, u32[]{:S(2)}, u32[]{:S(2)}) collective-permute-start(bf16[1,1,2,128,8,16]{3,5,1,4,2,0:T(8,128)(2,1)S(1)} %slice_bitcast_fusion.1), channel_id=1, source_target_pairs={{0,7},{1,0},{2,1},{3,2},{4,3},{5,4},{6,5},{7,6},{8,15},{9,8},{10,9... | collective-permute-start | bytes 196616 | tf_op jit(solution)/shard_map/ppermute | solution.py:83
  57.8 1.9 collective-permute-start.2
  60.9 5.1 %collective-permute-start.5 = (bf16[1,1,2,128,8,16]{3,5,1,4,2,0:T(8,128)(2,1)S(1)}, bf16[1,1,2,128,8,16]{3,5,1,4,2,0:T(8,128)(2,1)S(1)}, u32[]{:S(2)}, u32[]{:S(2)}) collective-permute-start(bf16[1,1,2,128,8,16]{3,5,1,4,2,0:T(8,128)(2,1)S(1)} %collective-permute-done.4), channel_id=1, source_target_pairs={{0,7},{1,0},{2,1},{3,2},{4,3},{5,4},{6,5},{7,6},{8,15},{9,8},{10,9... | collective-permute-start | bytes 196616 | tf_op jit(solution)/shard_map/ppermute | solution.py:83
  66.0 1.9 collective-permute-start.3
  68.5 5.1 %collective-permute-start.11 = (bf16[3,1,2,128,8,16]{3,5,4,2,1,0:T(8,128)(2,1)}, bf16[3,1,2,128,8,16]{3,5,4,2,1,0:T(8,128)(2,1)S(1)}, u32[]{:S(2)}, u32[]{:S(2)}) collective-permute-start(bf16[3,1,2,128,8,16]{3,5,4,2,1,0:T(8,128)(2,1)} %slice_bitcast_fusion), channel_id=1, source_target_pairs={{0,7},{1,0},{2,1},{3,2},{4,3},{5,4},{6,5},{7,6},{8,15},{9,8},{10,9... | collective-permute-start | bytes 589832 | tf_op jit(solution)/shard_map/ppermute | solution.py:83
  73.7 2.7 collective-permute-start.6
  76.4 3.1 %collective-permute-start.8 = (bf16[3,1,2,128,8,16]{3,5,4,2,1,0:T(8,128)(2,1)S(1)}, bf16[3,1,2,128,8,16]{3,5,4,2,1,0:T(8,128)(2,1)}, u32[]{:S(2)}, u32[]{:S(2)}) collective-permute-start(bf16[3,1,2,128,8,16]{3,5,4,2,1,0:T(8,128)(2,1)S(1)} %collective-permute-done.7), channel_id=1, source_target_pairs={{0,1},{1,2},{2,3},{3,4},{4,5},{5,6},{6,7},{7,0},{8,9},{9,10},{10,1... | collective-permute-start | bytes 589832 | tf_op jit(solution)/shard_map/ppermute | solution.py:80
  84.7 7.2 %all-to-all-start.2 = ((bf16[1,8,16,768]{3,2,0,1:T(8,128)(2,1)}), bf16[1,8,16,768]{3,2,0,1:T(8,128)(2,1)S(1)}, u32[]{:S(2)}, u32[]{:S(2)}) async-start(bf16[1,8,16,768]{3,2,0,1:T(8,128)(2,1)} %bitcast.59), calls=%async_computation.2 | async-start | bytes 393216 | tf_op jit(solution)/shard_map/all_to_all | solution.py:154
  91.9 3.9 %collective-permute-start.12 = (bf16[3,1,2,128,8,16]{3,5,4,2,1,0:T(8,128)(2,1)S(1)}, bf16[3,1,2,128,8,16]{3,5,4,2,1,0:T(8,128)(2,1)S(1)}, u32[]{:S(2)}, u32[]{:S(2)}) collective-permute-start(bf16[3,1,2,128,8,16]{3,5,4,2,1,0:T(8,128)(2,1)S(1)} %collective-permute-done.11), channel_id=1, source_target_pairs={{0,7},{1,0},{2,1},{3,2},{4,3},{5,4},{6,5},{7,6},{8,15},{9,8},{10,9... | collective-permute-start | bytes 589832 | tf_op jit(solution)/shard_map/ppermute | solution.py:83
  97.8 3.3 %collective-permute-done.12 = bf16[3,1,2,128,8,16]{3,5,4,2,1,0:T(8,128)(2,1)S(1)} collective-permute-done((bf16[3,1,2,128,8,16]{3,5,4,2,1,0:T(8,128)(2,1)S(1)}, bf16[3,1,2,128,8,16]{3,5,4,2,1,0:T(8,128)(2,1)S(1)}, u32[]{:S(2)}, u32[]{:S(2)}) %collective-permute-start.12) | collective-permute-done | bytes 196640 | tf_op jit(solution)/shard_map/ppermute | solution.py:83
  101.1 5.1 %collective-permute-start.13 = (bf16[3,1,2,128,8,16]{3,5,4,2,1,0:T(8,128)(2,1)S(1)}, bf16[3,1,2,128,8,16]{3,5,4,2,1,0:T(8,128)(2,1)S(1)}, u32[]{:S(2)}, u32[]{:S(2)}) collective-permute-start(bf16[3,1,2,128,8,16]{3,5,4,2,1,0:T(8,128)(2,1)S(1)} %collective-permute-done.12), channel_id=1, source_target_pairs={{0,7},{1,0},{2,1},{3,2},{4,3},{5,4},{6,5},{7,6},{8,15},{9,8},{10,9... | collective-permute-start | bytes 589832 | tf_op jit(solution)/shard_map/ppermute | solution.py:83
  106.3 1.9 collective-permute-start.10
  109.4 6.8 %all-to-all-start.3 = ((bf16[1,8,16,768]{3,2,0,1:T(8,128)(2,1)}), bf16[1,8,16,768]{3,2,0,1:T(8,128)(2,1)S(1)}, u32[]{:S(2)}, u32[]{:S(2)}) async-start(bf16[1,8,16,768]{3,2,0,1:T(8,128)(2,1)} %broadcast_in_dim.61), calls=%async_computation.3 | async-start | bytes 393216 | tf_op jit(solution)/shard_map/all_to_all | solution.py:146
  131.5 5.7 %all-to-all-start.4 = ((bf16[8,128,1,2,96]{1,4,3,2,0:T(8,128)(2,1)}), bf16[8,128,1,2,96]{1,4,3,2,0:T(8,128)(2,1)S(1)}, u32[]{:S(2)}, u32[]{:S(2)}) async-start(bf16[8,128,1,2,96]{1,4,3,2,0:T(8,128)(2,1)} %broadcast_in_dim.62), calls=%async_computation.4 | async-start | bytes 786432 | tf_op jit(solution)/shard_map/all_to_all | solution.py:146
  143.0 2.5 all-to-all-done.4
  149.1 17.8 %all_to_all.75 = bf16[1,8,16,768]{3,2,0,1:T(8,128)(2,1)S(1)} all-to-all(bf16[1,8,16,768]{3,2,0,1:T(8,128)(2,1)S(1)} %bitcast.303), channel_id=1, replica_groups=mesh['row'=8,'col'=8,'smp'=8] {'col'}, dimensions={1} | all-to-all | bytes 393216 | tf_op jit(solution)/shard_map/all_to_all | solution.py:154
  167.4 12.6 %all_to_all.76 = bf16[1,8,16,768]{3,2,0,1:T(8,128)(2,1)S(1)} all-to-all(bf16[1,8,16,768]{3,2,0,1:T(8,128)(2,1)S(1)} %broadcast_in_dim.63), channel_id=1, replica_groups=mesh['row'=8,'col'=8,'smp'=8] {'col'}, dimensions={1} | all-to-all | bytes 393216 | tf_op jit(solution)/shard_map/all_to_all | solution.py:146
  182.1 5.2 %all-to-all-start.7 = ((bf16[8,128,1,2,96]{1,4,3,2,0:T(8,128)(2,1)}), bf16[8,128,1,2,96]{1,4,3,2,0:T(8,128)(2,1)S(1)}, u32[]{:S(2)}, u32[]{:S(2)}) async-start(bf16[8,128,1,2,96]{1,4,3,2,0:T(8,128)(2,1)} %broadcast_in_dim.64), calls=%async_computation.7 | async-start | bytes 786432 | tf_op jit(solution)/shard_map/all_to_all | solution.py:146
  191.3 2.8 %all-to-all-done.7 = bf16[8,128,1,2,96]{1,4,3,2,0:T(8,128)(2,1)S(1)} async-done(((bf16[8,128,1,2,96]{1,4,3,2,0:T(8,128)(2,1)}), bf16[8,128,1,2,96]{1,4,3,2,0:T(8,128)(2,1)S(1)}, u32[]{:S(2)}, u32[]{:S(2)}) %all-to-all-start.7) | async-done | bytes 393248 | tf_op jit(solution)/shard_map/all_to_all | solution.py:146
  197.8 13.6 %all_to_all.77 = bf16[1,8,16,768]{3,2,0,1:T(8,128)(2,1)S(1)} all-to-all(bf16[1,8,16,768]{3,2,0,1:T(8,128)(2,1)S(1)} %bitcast.304), channel_id=1, replica_groups=mesh['row'=8,'col'=8,'smp'=8] {'col'}, dimensions={1} | all-to-all | bytes 393216 | tf_op jit(solution)/shard_map/all_to_all | solution.py:154
  211.9 13.2 %all_to_all.78 = bf16[1,8,16,768]{3,2,0,1:T(8,128)(2,1)S(1)} all-to-all(bf16[1,8,16,768]{3,2,0,1:T(8,128)(2,1)S(1)} %broadcast_in_dim.65), channel_id=1, replica_groups=mesh['row'=8,'col'=8,'smp'=8] {'col'}, dimensions={1} | all-to-all | bytes 393216 | tf_op jit(solution)/shard_map/all_to_all | solution.py:146
  227.1 4.6 %all-to-all-start.10 = ((bf16[8,128,1,2,96]{1,4,3,2,0:T(8,128)(2,1)}), bf16[8,128,1,2,96]{1,4,3,2,0:T(8,128)(2,1)S(1)}, u32[]{:S(2)}, u32[]{:S(2)}) async-start(bf16[8,128,1,2,96]{1,4,3,2,0:T(8,128)(2,1)} %broadcast_in_dim.66), calls=%async_computation.10 | async-start | bytes 786432 | tf_op jit(solution)/shard_map/all_to_all | solution.py:146
  233.4 5.1 %all-to-all-done.10 = bf16[8,128,1,2,96]{1,4,3,2,0:T(8,128)(2,1)S(1)} async-done(((bf16[8,128,1,2,96]{1,4,3,2,0:T(8,128)(2,1)}), bf16[8,128,1,2,96]{1,4,3,2,0:T(8,128)(2,1)S(1)}, u32[]{:S(2)}, u32[]{:S(2)}) %all-to-all-start.10) | async-done | bytes 393248 | tf_op jit(solution)/shard_map/all_to_all | solution.py:146
  241.0 13.6 %all_to_all.79 = bf16[1,8,16,768]{3,2,0,1:T(8,128)(2,1)S(1)} all-to-all(bf16[1,8,16,768]{3,2,0,1:T(8,128)(2,1)S(1)} %bitcast.305), channel_id=1, replica_groups=mesh['row'=8,'col'=8,'smp'=8] {'col'}, dimensions={1} | all-to-all | bytes 393216 | tf_op jit(solution)/shard_map/all_to_all | solution.py:154
  255.3 3.4 %all-to-all-start.12 = ((bf16[1,8,16,768]{3,2,0,1:T(8,128)(2,1)}), bf16[1,8,16,768]{3,2,0,1:T(8,128)(2,1)S(1)}, u32[]{:S(2)}, u32[]{:S(2)}) async-start(bf16[1,8,16,768]{3,2,0,1:T(8,128)(2,1)} %broadcast_in_dim.67), calls=%async_computation.12 | async-start | bytes 393216 | tf_op jit(solution)/shard_map/all_to_all | solution.py:146
  258.8 10.7 %all-to-all-done.12 = bf16[1,8,16,768]{3,2,0,1:T(8,128)(2,1)S(1)} async-done(((bf16[1,8,16,768]{3,2,0,1:T(8,128)(2,1)}), bf16[1,8,16,768]{3,2,0,1:T(8,128)(2,1)S(1)}, u32[]{:S(2)}, u32[]{:S(2)}) %all-to-all-start.12) | async-done | bytes 196640 | tf_op jit(solution)/shard_map/all_to_all | solution.py:146
  (213 shorter events, 69.7 us)
Async XLA Ops:
  0.7 18.6 %copy-start.4 = (f32[3,8192]{1,0:T(4,128)S(1)}, f32[3,8192]{1,0:T(4,128)}, u32[]{:S(2)}) copy-start(f32[3,8192]{1,0:T(4,128)} %param.17) | copy-start | bytes 294916
  5.5 19.6 %copy-start.13 = (f32[1,3,128]{2,0,1:T(1,128)S(1)}, f32[1,3,128]{2,0,1:T(1,128)}, u32[]{:S(2)}) copy-start(f32[1,3,128]{2,0,1:T(1,128)} %param.23) | copy-start | bytes 4612
  5.5 19.7 %copy-start.5 = (f32[4,768]{1,0:T(4,128)S(1)}, f32[4,768]{1,0:T(4,128)}, u32[]{:S(2)}) copy-start(f32[4,768]{1,0:T(4,128)} %param.24) | copy-start | bytes 36868
  5.8 19.4 %copy-start.3 = (bf16[128,768]{1,0:T(8,128)(2,1)S(1)}, bf16[128,768]{1,0:T(8,128)(2,1)}, u32[]{:S(2)}) copy-start(bf16[128,768]{1,0:T(8,128)(2,1)} %param.15) | copy-start | bytes 589828
  5.8 19.9 %copy-start.8 = (s32[128]{0:T(128)S(1)}, s32[128]{0:T(128)}, u32[]{:S(2)}) copy-start(s32[128]{0:T(128)} %param.19) | copy-start | bytes 1540
  5.8 19.9 %copy-start.14 = (s32[128]{0:T(128)S(1)}, s32[128]{0:T(128)}, u32[]{:S(2)}) copy-start(s32[128]{0:T(128)} %param.20) | copy-start | bytes 1540
  6.9 21.5 %all-to-all-start.1 = ((bf16[4,8,2,128,1,16]{3,5,2,0,4,1:T(8,128)(2,1)}), bf16[4,8,2,128,1,16]{3,5,2,0,4,1:T(8,128)(2,1)S(1)}, u32[]{:S(2)}, u32[]{:S(2)}) async-start(bf16[4,8,2,128,1,16]{3,5,2,0,4,1:T(8,128)(2,1)} %copy.56), calls=%async_computation.1 | async-start | bytes 524288 | tf_op jit(solution)/shard_map/all_to_all | solution.py:69
  21.9 37.8 %copy-start.9 = (f32[4,16]{1,0:T(4,128)S(1)}, f32[4,16]{1,0:T(4,128)}, u32[]{:S(2)}) copy-start(f32[4,16]{1,0:T(4,128)} %param.26) | copy-start | bytes 772
  29.2 51.3 %all-to-all-start = ((bf16[8,128,1,2,104]{1,4,3,2,0:T(8,128)(2,1)}), bf16[8,128,1,2,104]{1,4,3,2,0:T(8,128)(2,1)S(1)}, u32[]{:S(2)}, u32[]{:S(2)}) async-start(bf16[8,128,1,2,104]{1,4,3,2,0:T(8,128)(2,1)} %broadcast_in_dim.58), calls=%async_computation | async-start | bytes 851968 | tf_op jit(solution)/shard_map/all_to_all | solution.py:146
  35.6 12.5 %collective-permute-start = (bf16[1,1,2,128,8,16]{3,5,1,4,2,0:T(8,128)(2,1)S(1)}, bf16[1,1,2,128,8,16]{3,5,1,4,2,0:T(8,128)(2,1)S(1)}, u32[]{:S(2)}, u32[]{:S(2)}) collective-permute-start(bf16[1,1,2,128,8,16]{3,5,1,4,2,0:T(8,128)(2,1)S(1)} %slice_bitcast_fusion.1), channel_id=1, source_target_pairs={{0,1},{1,2},{2,3},{3,4},{4,5},{5,6},{6,7},{7,0},{8,9},{9,10},{10,1... | collective-permute-start | bytes 196616 | tf_op jit(solution)/shard_map/ppermute | solution.py:80
  48.2 9.7 %collective-permute-start.1 = (bf16[1,1,2,128,8,16]{3,5,1,4,2,0:T(8,128)(2,1)S(1)}, bf16[1,1,2,128,8,16]{3,5,1,4,2,0:T(8,128)(2,1)S(1)}, u32[]{:S(2)}, u32[]{:S(2)}) collective-permute-start(bf16[1,1,2,128,8,16]{3,5,1,4,2,0:T(8,128)(2,1)S(1)} %collective-permute-done), channel_id=1, source_target_pairs={{0,1},{1,2},{2,3},{3,4},{4,5},{5,6},{6,7},{7,0},{8,9},{9,10},{10,1... | collective-permute-start | bytes 196616 | tf_op jit(solution)/shard_map/ppermute | solution.py:80
  50.8 10.1 %collective-permute-start.4 = (bf16[1,1,2,128,8,16]{3,5,1,4,2,0:T(8,128)(2,1)S(1)}, bf16[1,1,2,128,8,16]{3,5,1,4,2,0:T(8,128)(2,1)S(1)}, u32[]{:S(2)}, u32[]{:S(2)}) collective-permute-start(bf16[1,1,2,128,8,16]{3,5,1,4,2,0:T(8,128)(2,1)S(1)} %slice_bitcast_fusion.1), channel_id=1, source_target_pairs={{0,7},{1,0},{2,1},{3,2},{4,3},{5,4},{6,5},{7,6},{8,15},{9,8},{10,9... | collective-permute-start | bytes 196616 | tf_op jit(solution)/shard_map/ppermute | solution.py:83
  55.9 20.5 %collective-permute-start.7 = (bf16[3,1,2,128,8,16]{3,5,4,2,1,0:T(8,128)(2,1)}, bf16[3,1,2,128,8,16]{3,5,4,2,1,0:T(8,128)(2,1)S(1)}, u32[]{:S(2)}, u32[]{:S(2)}) collective-permute-start(bf16[3,1,2,128,8,16]{3,5,4,2,1,0:T(8,128)(2,1)} %slice_bitcast_fusion), channel_id=1, source_target_pairs={{0,1},{1,2},{2,3},{3,4},{4,5},{5,6},{6,7},{7,0},{8,9},{9,10},{10,1... | collective-permute-start | bytes 589832 | tf_op jit(solution)/shard_map/ppermute | solution.py:80
  57.8 8.2 %collective-permute-start.2 = (bf16[1,1,2,128,8,16]{3,5,1,4,2,0:T(8,128)(2,1)S(1)}, bf16[1,1,2,128,8,16]{3,5,1,4,2,0:T(8,128)(2,1)S(1)}, u32[]{:S(2)}, u32[]{:S(2)}) collective-permute-start(bf16[1,1,2,128,8,16]{3,5,1,4,2,0:T(8,128)(2,1)S(1)} %collective-permute-done.1), channel_id=1, source_target_pairs={{0,1},{1,2},{2,3},{3,4},{4,5},{5,6},{6,7},{7,0},{8,9},{9,10},{10,1... | collective-permute-start | bytes 196616 | tf_op jit(solution)/shard_map/ppermute | solution.py:80
  60.9 12.8 %collective-permute-start.5 = (bf16[1,1,2,128,8,16]{3,5,1,4,2,0:T(8,128)(2,1)S(1)}, bf16[1,1,2,128,8,16]{3,5,1,4,2,0:T(8,128)(2,1)S(1)}, u32[]{:S(2)}, u32[]{:S(2)}) collective-permute-start(bf16[1,1,2,128,8,16]{3,5,1,4,2,0:T(8,128)(2,1)S(1)} %collective-permute-done.4), channel_id=1, source_target_pairs={{0,7},{1,0},{2,1},{3,2},{4,3},{5,4},{6,5},{7,6},{8,15},{9,8},{10,9... | collective-permute-start | bytes 196616 | tf_op jit(solution)/shard_map/ppermute | solution.py:83
  66.0 13.5 %collective-permute-start.3 = (bf16[1,1,2,128,8,16]{3,5,1,4,2,0:T(8,128)(2,1)S(1)}, bf16[1,1,2,128,8,16]{3,5,1,4,2,0:T(8,128)(2,1)S(1)}, u32[]{:S(2)}, u32[]{:S(2)}) collective-permute-start(bf16[1,1,2,128,8,16]{3,5,1,4,2,0:T(8,128)(2,1)S(1)} %collective-permute-done.2), channel_id=1, source_target_pairs={{0,1},{1,2},{2,3},{3,4},{4,5},{5,6},{6,7},{7,0},{8,9},{9,10},{10,1... | collective-permute-start | bytes 196616 | tf_op jit(solution)/shard_map/ppermute | solution.py:80
  68.5 23.4 %collective-permute-start.11 = (bf16[3,1,2,128,8,16]{3,5,4,2,1,0:T(8,128)(2,1)}, bf16[3,1,2,128,8,16]{3,5,4,2,1,0:T(8,128)(2,1)S(1)}, u32[]{:S(2)}, u32[]{:S(2)}) collective-permute-start(bf16[3,1,2,128,8,16]{3,5,4,2,1,0:T(8,128)(2,1)} %slice_bitcast_fusion), channel_id=1, source_target_pairs={{0,7},{1,0},{2,1},{3,2},{4,3},{5,4},{6,5},{7,6},{8,15},{9,8},{10,9... | collective-permute-start | bytes 589832 | tf_op jit(solution)/shard_map/ppermute | solution.py:83
  73.7 6.2 %collective-permute-start.6 = (bf16[1,1,2,128,8,16]{3,5,1,4,2,0:T(8,128)(2,1)S(1)}, bf16[1,1,2,128,8,16]{3,5,1,4,2,0:T(8,128)(2,1)S(1)}, u32[]{:S(2)}, u32[]{:S(2)}) collective-permute-start(bf16[1,1,2,128,8,16]{3,5,1,4,2,0:T(8,128)(2,1)S(1)} %collective-permute-done.5), channel_id=1, source_target_pairs={{0,7},{1,0},{2,1},{3,2},{4,3},{5,4},{6,5},{7,6},{8,15},{9,8},{10,9... | collective-permute-start | bytes 196616 | tf_op jit(solution)/shard_map/ppermute | solution.py:83
  76.4 19.5 %collective-permute-start.8 = (bf16[3,1,2,128,8,16]{3,5,4,2,1,0:T(8,128)(2,1)S(1)}, bf16[3,1,2,128,8,16]{3,5,4,2,1,0:T(8,128)(2,1)}, u32[]{:S(2)}, u32[]{:S(2)}) collective-permute-start(bf16[3,1,2,128,8,16]{3,5,4,2,1,0:T(8,128)(2,1)S(1)} %collective-permute-done.7), channel_id=1, source_target_pairs={{0,1},{1,2},{2,3},{3,4},{4,5},{5,6},{6,7},{7,0},{8,9},{9,10},{10,1... | collective-permute-start | bytes 589832 | tf_op jit(solution)/shard_map/ppermute | solution.py:80
  84.7 23.5 %all-to-all-start.2 = ((bf16[1,8,16,768]{3,2,0,1:T(8,128)(2,1)}), bf16[1,8,16,768]{3,2,0,1:T(8,128)(2,1)S(1)}, u32[]{:S(2)}, u32[]{:S(2)}) async-start(bf16[1,8,16,768]{3,2,0,1:T(8,128)(2,1)} %bitcast.59), calls=%async_computation.2 | async-start | bytes 393216 | tf_op jit(solution)/shard_map/all_to_all | solution.py:154
  91.9 9.2 %collective-permute-start.12 = (bf16[3,1,2,128,8,16]{3,5,4,2,1,0:T(8,128)(2,1)S(1)}, bf16[3,1,2,128,8,16]{3,5,4,2,1,0:T(8,128)(2,1)S(1)}, u32[]{:S(2)}, u32[]{:S(2)}) collective-permute-start(bf16[3,1,2,128,8,16]{3,5,4,2,1,0:T(8,128)(2,1)S(1)} %collective-permute-done.11), channel_id=1, source_target_pairs={{0,7},{1,0},{2,1},{3,2},{4,3},{5,4},{6,5},{7,6},{8,15},{9,8},{10,9... | collective-permute-start | bytes 589832 | tf_op jit(solution)/shard_map/ppermute | solution.py:83
  95.9 10.4 %collective-permute-start.9 = (bf16[3,1,2,128,8,16]{3,5,4,2,1,0:T(8,128)(2,1)}, bf16[3,1,2,128,8,16]{3,5,4,2,1,0:T(8,128)(2,1)S(1)}, u32[]{:S(2)}, u32[]{:S(2)}) collective-permute-start(bf16[3,1,2,128,8,16]{3,5,4,2,1,0:T(8,128)(2,1)} %collective-permute-done.8), channel_id=1, source_target_pairs={{0,1},{1,2},{2,3},{3,4},{4,5},{5,6},{6,7},{7,0},{8,9},{9,10},{10,1... | collective-permute-start | bytes 589832 | tf_op jit(solution)/shard_map/ppermute | solution.py:80
  101.1 21.0 %collective-permute-start.13 = (bf16[3,1,2,128,8,16]{3,5,4,2,1,0:T(8,128)(2,1)S(1)}, bf16[3,1,2,128,8,16]{3,5,4,2,1,0:T(8,128)(2,1)S(1)}, u32[]{:S(2)}, u32[]{:S(2)}) collective-permute-start(bf16[3,1,2,128,8,16]{3,5,4,2,1,0:T(8,128)(2,1)S(1)} %collective-permute-done.12), channel_id=1, source_target_pairs={{0,7},{1,0},{2,1},{3,2},{4,3},{5,4},{6,5},{7,6},{8,15},{9,8},{10,9... | collective-permute-start | bytes 589832 | tf_op jit(solution)/shard_map/ppermute | solution.py:83
  106.3 9.9 %collective-permute-start.10 = (bf16[3,1,2,128,8,16]{3,5,4,2,1,0:T(8,128)(2,1)S(1)}, bf16[3,1,2,128,8,16]{3,5,4,2,1,0:T(8,128)(2,1)S(1)}, u32[]{:S(2)}, u32[]{:S(2)}) collective-permute-start(bf16[3,1,2,128,8,16]{3,5,4,2,1,0:T(8,128)(2,1)S(1)} %collective-permute-done.9), channel_id=1, source_target_pairs={{0,1},{1,2},{2,3},{3,4},{4,5},{5,6},{6,7},{7,0},{8,9},{9,10},{10,1... | collective-permute-start | bytes 589832 | tf_op jit(solution)/shard_map/ppermute | solution.py:80
  109.4 20.1 %all-to-all-start.3 = ((bf16[1,8,16,768]{3,2,0,1:T(8,128)(2,1)}), bf16[1,8,16,768]{3,2,0,1:T(8,128)(2,1)S(1)}, u32[]{:S(2)}, u32[]{:S(2)}) async-start(bf16[1,8,16,768]{3,2,0,1:T(8,128)(2,1)} %broadcast_in_dim.61), calls=%async_computation.3 | async-start | bytes 393216 | tf_op jit(solution)/shard_map/all_to_all | solution.py:146
  131.5 13.9 %all-to-all-start.4 = ((bf16[8,128,1,2,96]{1,4,3,2,0:T(8,128)(2,1)}), bf16[8,128,1,2,96]{1,4,3,2,0:T(8,128)(2,1)S(1)}, u32[]{:S(2)}, u32[]{:S(2)}) async-start(bf16[8,128,1,2,96]{1,4,3,2,0:T(8,128)(2,1)} %broadcast_in_dim.62), calls=%async_computation.4 | async-start | bytes 786432 | tf_op jit(solution)/shard_map/all_to_all | solution.py:146
  147.3 40.0 %copy-start.10 = (f32[1,16]{1,0:T(1,128)S(1)}, f32[1,16]{1,0:T(1,128)}, u32[]{:S(2)}) copy-start(f32[1,16]{1,0:T(1,128)} %get-tuple-element.43) | copy-start | bytes 196
  147.3 40.0 %copy-start.11 = (f32[1,16]{1,0:T(1,128)S(1)}, f32[1,16]{1,0:T(1,128)}, u32[]{:S(2)}) copy-start(f32[1,16]{1,0:T(1,128)} %get-tuple-element.46) | copy-start | bytes 196
  182.1 12.0 %all-to-all-start.7 = ((bf16[8,128,1,2,96]{1,4,3,2,0:T(8,128)(2,1)}), bf16[8,128,1,2,96]{1,4,3,2,0:T(8,128)(2,1)S(1)}, u32[]{:S(2)}, u32[]{:S(2)}) async-start(bf16[8,128,1,2,96]{1,4,3,2,0:T(8,128)(2,1)} %broadcast_in_dim.64), calls=%async_computation.7 | async-start | bytes 786432 | tf_op jit(solution)/shard_map/all_to_all | solution.py:146
  227.1 11.4 %all-to-all-start.10 = ((bf16[8,128,1,2,96]{1,4,3,2,0:T(8,128)(2,1)}), bf16[8,128,1,2,96]{1,4,3,2,0:T(8,128)(2,1)S(1)}, u32[]{:S(2)}, u32[]{:S(2)}) async-start(bf16[8,128,1,2,96]{1,4,3,2,0:T(8,128)(2,1)} %broadcast_in_dim.66), calls=%async_computation.10 | async-start | bytes 786432 | tf_op jit(solution)/shard_map/all_to_all | solution.py:146
  239.1 31.0 %copy-start.6 = (bf16[3,768]{1,0:T(4,128)(2,1)S(1)}, bf16[3,768]{1,0:T(4,128)(2,1)}, u32[]{:S(2)}) copy-start(bf16[3,768]{1,0:T(4,128)(2,1)} %param.29) | copy-start | bytes 13828
  255.3 14.2 %all-to-all-start.12 = ((bf16[1,8,16,768]{3,2,0,1:T(8,128)(2,1)}), bf16[1,8,16,768]{3,2,0,1:T(8,128)(2,1)S(1)}, u32[]{:S(2)}, u32[]{:S(2)}) async-start(bf16[1,8,16,768]{3,2,0,1:T(8,128)(2,1)} %broadcast_in_dim.67), calls=%async_computation.12 | async-start | bytes 393216 | tf_op jit(solution)/shard_map/all_to_all | solution.py:146
  (6 other events, 52.3 us)

commit v9 on v7

--- a/solution.py
+++ b/solution.py
@@ -76,17 +76,21 @@
     backward = [(i, (i - 1) % copies) for i in range(copies)]
     pieces = {0: column_bias}
     rightward, leftward = column_bias, column_bias
+    first_hop = None
     for step in range(1, copies // 2 + 1):
         rightward = lax.ppermute(rightward, "smp", forward)
         pieces[-step] = rightward
         if step < copies - copies // 2:
             leftward = lax.ppermute(leftward, "smp", backward)
             pieces[step] = leftward
+        if first_hop is None:
+            first_hop = (rightward, leftward)
     offsets = sorted(pieces)
     stacked = jnp.concatenate([pieces[d] for d in offsets], axis=1)
     stacked = jnp.roll(stacked, lax.axis_index("smp") + offsets[0], axis=1)
     stacked = jnp.transpose(stacked, (0, 2, 3, 4, 1, 5))
-    return stacked.reshape(blocks, group_members, row_count, col_count * copies * keys_dev)
+    spread = stacked.reshape(blocks, group_members, row_count, col_count * copies * keys_dev)
+    return spread, first_hop
 
 
 def build_absorber(
@@ -172,14 +176,15 @@
     attention_output_weight,
     position_update_weight,
 ):
-    noisy = noisy_centres(coords, token_centre_atom, angles, sample_noise_level, centre_noise)
-    hidden_activity = embed_tokens(single, noisy, sample_noise_level, embedding_weight)
     pair_normed = layer_norm(pair_features.astype(jnp.float32)).astype(jnp.bfloat16)
     local_bias = jnp.einsum(
         "ikc,cbh->bhik", pair_normed, pair_bias_weight, preferred_element_type=jnp.float32
     ).astype(jnp.bfloat16)
     column_bias = relay_bias(local_bias)
-    gathered_pair_bias = spread_bias(column_bias)
+    gathered_pair_bias, first_hop = spread_bias(column_bias)
+    coords, single, _ = lax.optimization_barrier((coords, single, first_hop))
+    noisy = noisy_centres(coords, token_centre_atom, angles, sample_noise_level, centre_noise)
+    hidden_activity = embed_tokens(single, noisy, sample_noise_level, embedding_weight)
     samples, row_count, model_width = hidden_activity.shape
     col_count = lax.axis_size("col")
     own_rows = row_count // col_count

time: 257 us -> 259 us (level)
  waiting for transfers between devices: 53.1 us -> 57.5 us
    all_to_all x1, waiting for transfers between devices: 0.01 us -> 6.61 us  [relay_bias(): return lax.all_to_all(by_group, 'col', 1, 4, tiled=True)]
    ppermute x4, waiting for transfers between devices: 15.9 us -> 12.3 us  [spread_bias(): rightward = lax.ppermute(rightward, 'smp', forward)]
    all_to_all x1, starting transfers between devices: 6.13 us -> 3.43 us  [scatter_sum_rows(): arrived = lax.all_to_all(pieces, axis_name, 1, 1, tiled=True)]
    unnamed x45 -> x44, local copies, waits for them, and re-layouts: 4.68 us -> 2.05 us
    optimization_barrier x0 -> x1, local copies, waits for them, and re-layouts: none -> 2.61 us  [body(): coords, single, _ = lax.optimization_barrier((coords, single, first_hop))]
  transfers between devices with their start and end apart: 14 -> 14, of which waited for: 9 -> 11; matrix products, arithmetic and copies ran while one was open for 6% -> 3% of each run, Pallas kernels for 0% -> 0%
where the time goes in v9:
time: 259 us; the launch traced here: 258 us
  blocking collectives  81.2 us (31%)
  starting transfers between devices  63.3 us (24%)
  waiting for transfers between devices  57.5 us (22%)
  matrix products  19.9 us (8%)
  local copies, waits for them, and re-layouts  19.3 us (7%)
  other arithmetic  9.73 us (4%)
  between operations  6.65 us (3%)
    all_to_all x3, blocking collectives, scatter_sum_rows(): arrived = lax.all_to_all(pieces, axis_name, 1, 1, tiled=True)  41 us
    all_to_all x3, blocking collectives, gather_by_exchange(): joined = lax.all_to_all(spread, axis_name, axis, axis, tiled=True)  40.2 us
    all_to_all x5, waiting for transfers between devices, gather_by_exchange(): joined = lax.all_to_all(spread, axis_name, axis, axis, tiled=True)  26.9 us
    all_to_all x5, starting transfers between devices, gather_by_exchange(): joined = lax.all_to_all(spread, axis_name, axis, axis, tiled=True)  24.4 us
    ppermute x3, starting transfers between devices, spread_bias(): leftward = lax.ppermute(leftward, 'smp', backward)  19.3 us
    ppermute x4, waiting for transfers between devices, spread_bias(): rightward = lax.ppermute(rightward, 'smp', forward)  12.3 us
    all_to_all x1, waiting for transfers between devices, scatter_sum_rows(): arrived = lax.all_to_all(pieces, axis_name, 1, 1, tiled=True)  10.3 us
    ppermute x4, starting transfers between devices, spread_bias(): rightward = lax.ppermute(rightward, 'smp', forward)  9.95 us
  transfers between devices with their start and end apart: 14, of which 11 were waited for; matrix products, arithmetic and copies ran while one was open for 3% of the time, Pallas kernels for 0%

profile of v9, /device:TPU:8, one launch (start us, length us, event | category | flops | bytes accessed | tf_op | source)
XLA Modules:
  0.0 257.5 jit_solution(10213097191049132606)
XLA Ops:
  6.9 6.2 %all-to-all-start = ((bf16[4,8,2,128,1,16]{3,5,2,0,4,1:T(8,128)(2,1)}), bf16[4,8,2,128,1,16]{3,5,2,0,4,1:T(8,128)(2,1)S(1)}, u32[]{:S(2)}, u32[]{:S(2)}) async-start(bf16[4,8,2,128,1,16]{3,5,2,0,4,1:T(8,128)(2,1)} %copy.49), calls=%async_computation | async-start | bytes 524288 | tf_op jit(solution)/shard_map/all_to_all | solution.py:69
  19.3 6.6 %all-to-all-done = bf16[4,8,2,128,1,16]{3,5,2,0,4,1:T(8,128)(2,1)S(1)} async-done(((bf16[4,8,2,128,1,16]{3,5,2,0,4,1:T(8,128)(2,1)}), bf16[4,8,2,128,1,16]{3,5,2,0,4,1:T(8,128)(2,1)S(1)}, u32[]{:S(2)}, u32[]{:S(2)}) %all-to-all-start) | async-done | bytes 262176 | tf_op jit(solution)/shard_map/all_to_all | solution.py:69
  25.9 4.2 %collective-permute-start = (bf16[4,1,2,128,8,16]{3,5,1,4,2,0:T(8,128)(2,1)S(1)}, bf16[4,1,2,128,8,16]{3,5,1,4,2,0:T(8,128)(2,1)S(1)}, u32[]{:S(2)}, u32[]{:S(2)}) collective-permute-start(bf16[4,1,2,128,8,16]{3,5,1,4,2,0:T(8,128)(2,1)S(1)} %bitcast.305), channel_id=1, source_target_pairs={{0,1},{1,2},{2,3},{3,4},{4,5},{5,6},{6,7},{7,0},{8,9},{9,10},{10,1... | collective-permute-start | bytes 786440 | tf_op jit(solution)/shard_map/ppermute | solution.py:81
  30.1 8.6 %collective-permute-start.1 = (bf16[4,1,2,128,8,16]{3,5,1,4,2,0:T(8,128)(2,1)S(1)}, bf16[4,1,2,128,8,16]{3,5,1,4,2,0:T(8,128)(2,1)S(1)}, u32[]{:S(2)}, u32[]{:S(2)}) collective-permute-start(bf16[4,1,2,128,8,16]{3,5,1,4,2,0:T(8,128)(2,1)S(1)} %bitcast.306), channel_id=1, source_target_pairs={{0,7},{1,0},{2,1},{3,2},{4,3},{5,4},{6,5},{7,6},{8,15},{9,8},{10,9... | collective-permute-start | bytes 786440 | tf_op jit(solution)/shard_map/ppermute | solution.py:84
  38.8 2.3 collective-permute-done
  42.6 2.6 %copy.51 = f32[3,8192]{0,1:T(8,128)} copy(f32[3,8192]{1,0:T(4,128)S(1)} %copy-done.4) | data formatting | bytes 196608 | tf_op jit(solution)/shard_map/optimization_barrier | solution.py:185
  45.2 2.8 %gather_fusion = f32[128,3]{1,0:T(8,128)S(1)} fusion(f32[3,8192]{0,1:T(8,128)} %copy.51, s32[1024]{0:T(1024)S(1)} %pad_clamp_fusion), kind=kCustom, calls=%fused_computation | custom fusion | bytes 3584 | tf_op jit(solution)/shard_map/jit(_take)/gather | solution.py:46
  51.0 5.9 %all-to-all-start.1 = ((bf16[8,128,1,2,104]{1,4,3,2,0:T(8,128)(2,1)}), bf16[8,128,1,2,104]{1,4,3,2,0:T(8,128)(2,1)S(1)}, u32[]{:S(2)}, u32[]{:S(2)}) async-start(bf16[8,128,1,2,104]{1,4,3,2,0:T(8,128)(2,1)} %broadcast_in_dim.58), calls=%async_computation.1 | async-start | bytes 851968 | tf_op jit(solution)/shard_map/all_to_all | solution.py:150
  56.9 1.9 collective-permute-start.2
  58.9 5.6 %collective-permute-start.5 = (bf16[4,1,2,128,8,16]{3,5,1,4,2,0:T(8,128)(2,1)S(1)}, bf16[4,1,2,128,8,16]{3,5,1,4,2,0:T(8,128)(2,1)S(1)}, u32[]{:S(2)}, u32[]{:S(2)}) collective-permute-start(bf16[4,1,2,128,8,16]{3,5,1,4,2,0:T(8,128)(2,1)S(1)} %collective-permute-done.1), channel_id=1, source_target_pairs={{0,7},{1,0},{2,1},{3,2},{4,3},{5,4},{6,5},{7,6},{8,15},{9,8},{10,9... | collective-permute-start | bytes 786440 | tf_op jit(solution)/shard_map/ppermute | solution.py:84
  64.5 2.3 collective-permute-done.2
  66.8 1.9 collective-permute-start.3
  70.1 5.1 %collective-permute-start.6 = (bf16[4,1,2,128,8,16]{3,5,1,4,2,0:T(8,128)(2,1)S(1)}, bf16[4,1,2,128,8,16]{3,5,1,4,2,0:T(8,128)(2,1)S(1)}, u32[]{:S(2)}, u32[]{:S(2)}) collective-permute-start(bf16[4,1,2,128,8,16]{3,5,1,4,2,0:T(8,128)(2,1)S(1)} %collective-permute-done.5), channel_id=1, source_target_pairs={{0,7},{1,0},{2,1},{3,2},{4,3},{5,4},{6,5},{7,6},{8,15},{9,8},{10,9... | collective-permute-start | bytes 786440 | tf_op jit(solution)/shard_map/ppermute | solution.py:84
  76.3 1.9 collective-permute-start.4
  79.2 6.5 %collective-permute-done.4 = bf16[4,1,2,128,8,16]{3,5,1,4,2,0:T(8,128)(2,1)S(1)} collective-permute-done((bf16[4,1,2,128,8,16]{3,5,1,4,2,0:T(8,128)(2,1)S(1)}, bf16[4,1,2,128,8,16]{3,5,1,4,2,0:T(8,128)(2,1)S(1)}, u32[]{:S(2)}, u32[]{:S(2)}) %collective-permute-start.4) | collective-permute-done | bytes 262176 | tf_op jit(solution)/shard_map/ppermute | solution.py:81
  91.6 1.8 convolution_convert_fusion.4
  93.4 3.4 %all-to-all-start.2 = ((bf16[1,8,16,768]{3,2,0,1:T(8,128)(2,1)}), bf16[1,8,16,768]{3,2,0,1:T(8,128)(2,1)S(1)}, u32[]{:S(2)}, u32[]{:S(2)}) async-start(bf16[1,8,16,768]{3,2,0,1:T(8,128)(2,1)} %bitcast.61), calls=%async_computation.2 | async-start | bytes 393216 | tf_op jit(solution)/shard_map/all_to_all | solution.py:158
  96.8 10.3 %all-to-all-done.2 = bf16[1,8,16,768]{3,2,0,1:T(8,128)(2,1)S(1)} async-done(((bf16[1,8,16,768]{3,2,0,1:T(8,128)(2,1)}), bf16[1,8,16,768]{3,2,0,1:T(8,128)(2,1)S(1)}, u32[]{:S(2)}, u32[]{:S(2)}) %all-to-all-start.2) | async-done | bytes 196640 | tf_op jit(solution)/shard_map/all_to_all | solution.py:158
  108.3 13.7 %all_to_all.78 = bf16[1,8,16,768]{3,2,0,1:T(8,128)(2,1)S(1)} all-to-all(bf16[1,8,16,768]{3,2,0,1:T(8,128)(2,1)S(1)} %broadcast_in_dim.61), channel_id=1, replica_groups=mesh['row'=8,'col'=8,'smp'=8] {'col'}, dimensions={1} | all-to-all | bytes 393216 | tf_op jit(solution)/shard_map/all_to_all | solution.py:150
  124.0 6.0 %all-to-all-start.4 = ((bf16[8,128,1,2,96]{1,4,3,2,0:T(8,128)(2,1)}), bf16[8,128,1,2,96]{1,4,3,2,0:T(8,128)(2,1)}, u32[]{:S(2)}, u32[]{:S(2)}) async-start(bf16[8,128,1,2,96]{1,4,3,2,0:T(8,128)(2,1)} %broadcast_in_dim.62), calls=%async_computation.4 | async-start | bytes 786432 | tf_op jit(solution)/shard_map/all_to_all | solution.py:150
  131.5 5.5 %all-to-all-done.4 = bf16[8,128,1,2,96]{1,4,3,2,0:T(8,128)(2,1)} async-done(((bf16[8,128,1,2,96]{1,4,3,2,0:T(8,128)(2,1)}), bf16[8,128,1,2,96]{1,4,3,2,0:T(8,128)(2,1)}, u32[]{:S(2)}, u32[]{:S(2)}) %all-to-all-start.4) | async-done | bytes 393248 | tf_op jit(solution)/shard_map/all_to_all | solution.py:150
  140.4 13.6 %all_to_all.79 = bf16[1,8,16,768]{3,2,0,1:T(8,128)(2,1)S(1)} all-to-all(bf16[1,8,16,768]{3,2,0,1:T(8,128)(2,1)S(1)} %bitcast.292), channel_id=1, replica_groups=mesh['row'=8,'col'=8,'smp'=8] {'col'}, dimensions={1} | all-to-all | bytes 393216 | tf_op jit(solution)/shard_map/all_to_all | solution.py:158
  154.5 13.2 %all_to_all.80 = bf16[1,8,16,768]{3,2,0,1:T(8,128)(2,1)S(1)} all-to-all(bf16[1,8,16,768]{3,2,0,1:T(8,128)(2,1)S(1)} %broadcast_in_dim.63), channel_id=1, replica_groups=mesh['row'=8,'col'=8,'smp'=8] {'col'}, dimensions={1} | all-to-all | bytes 393216 | tf_op jit(solution)/shard_map/all_to_all | solution.py:150
  169.7 4.6 %all-to-all-start.7 = ((bf16[8,128,1,2,96]{1,4,3,2,0:T(8,128)(2,1)}), bf16[8,128,1,2,96]{1,4,3,2,0:T(8,128)(2,1)S(1)}, u32[]{:S(2)}, u32[]{:S(2)}) async-start(bf16[8,128,1,2,96]{1,4,3,2,0:T(8,128)(2,1)} %broadcast_in_dim.64), calls=%async_computation.7 | async-start | bytes 786432 | tf_op jit(solution)/shard_map/all_to_all | solution.py:150
  175.8 5.3 %all-to-all-done.7 = bf16[8,128,1,2,96]{1,4,3,2,0:T(8,128)(2,1)S(1)} async-done(((bf16[8,128,1,2,96]{1,4,3,2,0:T(8,128)(2,1)}), bf16[8,128,1,2,96]{1,4,3,2,0:T(8,128)(2,1)S(1)}, u32[]{:S(2)}, u32[]{:S(2)}) %all-to-all-start.7) | async-done | bytes 393248 | tf_op jit(solution)/shard_map/all_to_all | solution.py:150
  183.6 13.8 %all_to_all.81 = bf16[1,8,16,768]{3,2,0,1:T(8,128)(2,1)S(1)} all-to-all(bf16[1,8,16,768]{3,2,0,1:T(8,128)(2,1)S(1)} %bitcast.293), channel_id=1, replica_groups=mesh['row'=8,'col'=8,'smp'=8] {'col'}, dimensions={1} | all-to-all | bytes 393216 | tf_op jit(solution)/shard_map/all_to_all | solution.py:158
  197.8 13.2 %all_to_all.82 = bf16[1,8,16,768]{3,2,0,1:T(8,128)(2,1)S(1)} all-to-all(bf16[1,8,16,768]{3,2,0,1:T(8,128)(2,1)S(1)} %broadcast_in_dim.65), channel_id=1, replica_groups=mesh['row'=8,'col'=8,'smp'=8] {'col'}, dimensions={1} | all-to-all | bytes 393216 | tf_op jit(solution)/shard_map/all_to_all | solution.py:150
  213.1 4.6 %all-to-all-start.10 = ((bf16[8,128,1,2,96]{1,4,3,2,0:T(8,128)(2,1)}), bf16[8,128,1,2,96]{1,4,3,2,0:T(8,128)(2,1)S(1)}, u32[]{:S(2)}, u32[]{:S(2)}) async-start(bf16[8,128,1,2,96]{1,4,3,2,0:T(8,128)(2,1)} %broadcast_in_dim.66), calls=%async_computation.10 | async-start | bytes 786432 | tf_op jit(solution)/shard_map/all_to_all | solution.py:150
  219.1 5.4 %all-to-all-done.10 = bf16[8,128,1,2,96]{1,4,3,2,0:T(8,128)(2,1)S(1)} async-done(((bf16[8,128,1,2,96]{1,4,3,2,0:T(8,128)(2,1)}), bf16[8,128,1,2,96]{1,4,3,2,0:T(8,128)(2,1)S(1)}, u32[]{:S(2)}, u32[]{:S(2)}) %all-to-all-start.10) | async-done | bytes 393248 | tf_op jit(solution)/shard_map/all_to_all | solution.py:150
  227.0 13.6 %all_to_all.83 = bf16[1,8,16,768]{3,2,0,1:T(8,128)(2,1)S(1)} all-to-all(bf16[1,8,16,768]{3,2,0,1:T(8,128)(2,1)S(1)} %bitcast.294), channel_id=1, replica_groups=mesh['row'=8,'col'=8,'smp'=8] {'col'}, dimensions={1} | all-to-all | bytes 393216 | tf_op jit(solution)/shard_map/all_to_all | solution.py:158
  241.3 3.4 %all-to-all-start.12 = ((bf16[1,8,16,768]{3,2,0,1:T(8,128)(2,1)}), bf16[1,8,16,768]{3,2,0,1:T(8,128)(2,1)S(1)}, u32[]{:S(2)}, u32[]{:S(2)}) async-start(bf16[1,8,16,768]{3,2,0,1:T(8,128)(2,1)} %broadcast_in_dim.67), calls=%async_computation.12 | async-start | bytes 393216 | tf_op jit(solution)/shard_map/all_to_all | solution.py:150
  244.8 10.7 %all-to-all-done.12 = bf16[1,8,16,768]{3,2,0,1:T(8,128)(2,1)S(1)} async-done(((bf16[1,8,16,768]{3,2,0,1:T(8,128)(2,1)}), bf16[1,8,16,768]{3,2,0,1:T(8,128)(2,1)S(1)}, u32[]{:S(2)}, u32[]{:S(2)}) %all-to-all-start.12) | async-done | bytes 196640 | tf_op jit(solution)/shard_map/all_to_all | solution.py:150
  (169 shorter events, 44.1 us)
Async XLA Ops:
  0.6 5.0 %copy-start = (bf16[128,4,16]{0,2,1:T(8,128)(2,1)S(1)}, bf16[128,4,16]{0,2,1:T(8,128)(2,1)}, u32[]{:S(2)}) copy-start(bf16[128,4,16]{0,2,1:T(8,128)(2,1)} %param.25) | copy-start | bytes 49156
  0.6 12.5 %copy-start.7 = (f32[1,3]{1,0:T(1,128)S(1)}, f32[1,3]{1,0:T(1,128)}, u32[]{:S(2)}) copy-start(f32[1,3]{1,0:T(1,128)} %param.21) | copy-start | bytes 40
  0.7 17.4 %copy-start.12 = (s32[128]{0:T(128)S(1)}, s32[128]{0:T(128)}, u32[]{:S(2)}) copy-start(s32[128]{0:T(128)} %param.18) | copy-start | bytes 1540
  0.7 18.5 %copy-start.5 = (f32[4,768]{1,0:T(4,128)S(1)}, f32[4,768]{1,0:T(4,128)}, u32[]{:S(2)}) copy-start(f32[4,768]{1,0:T(4,128)} %param.24) | copy-start | bytes 36868
  0.7 18.6 %copy-start.8 = (s32[128]{0:T(128)S(1)}, s32[128]{0:T(128)}, u32[]{:S(2)}) copy-start(s32[128]{0:T(128)} %param.19) | copy-start | bytes 1540
  0.7 18.6 %copy-start.11 = (s32[128]{0:T(128)S(1)}, s32[128]{0:T(128)}, u32[]{:S(2)}) copy-start(s32[128]{0:T(128)} %param.20) | copy-start | bytes 1540
  0.7 41.9 %copy-start.4 = (f32[3,8192]{1,0:T(4,128)S(1)}, f32[3,8192]{1,0:T(4,128)}, u32[]{:S(2)}) copy-start(f32[3,8192]{1,0:T(4,128)} %param.17) | copy-start | bytes 294916
  3.9 44.4 %copy-start.10 = (f32[1,3,128]{2,0,1:T(1,128)S(1)}, f32[1,3,128]{2,0,1:T(1,128)}, u32[]{:S(2)}) copy-start(f32[1,3,128]{2,0,1:T(1,128)} %param.23) | copy-start | bytes 4612
  3.9 44.5 %copy-start.3 = (bf16[128,768]{1,0:T(8,128)(2,1)S(1)}, bf16[128,768]{1,0:T(8,128)(2,1)}, u32[]{:S(2)}) copy-start(bf16[128,768]{1,0:T(8,128)(2,1)} %param.15) | copy-start | bytes 589828
  6.9 19.0 %all-to-all-start = ((bf16[4,8,2,128,1,16]{3,5,2,0,4,1:T(8,128)(2,1)}), bf16[4,8,2,128,1,16]{3,5,2,0,4,1:T(8,128)(2,1)S(1)}, u32[]{:S(2)}, u32[]{:S(2)}) async-start(bf16[4,8,2,128,1,16]{3,5,2,0,4,1:T(8,128)(2,1)} %copy.49), calls=%async_computation | async-start | bytes 524288 | tf_op jit(solution)/shard_map/all_to_all | solution.py:69
  13.1 45.7 %copy-start.9 = (f32[4,16]{1,0:T(4,128)S(1)}, f32[4,16]{1,0:T(4,128)}, u32[]{:S(2)}) copy-start(f32[4,16]{1,0:T(4,128)} %param.26) | copy-start | bytes 772
  25.9 15.2 %collective-permute-start = (bf16[4,1,2,128,8,16]{3,5,1,4,2,0:T(8,128)(2,1)S(1)}, bf16[4,1,2,128,8,16]{3,5,1,4,2,0:T(8,128)(2,1)S(1)}, u32[]{:S(2)}, u32[]{:S(2)}) collective-permute-start(bf16[4,1,2,128,8,16]{3,5,1,4,2,0:T(8,128)(2,1)S(1)} %bitcast.305), channel_id=1, source_target_pairs={{0,1},{1,2},{2,3},{3,4},{4,5},{5,6},{6,7},{7,0},{8,9},{9,10},{10,1... | collective-permute-start | bytes 786440 | tf_op jit(solution)/shard_map/ppermute | solution.py:81
  30.1 12.5 %collective-permute-start.1 = (bf16[4,1,2,128,8,16]{3,5,1,4,2,0:T(8,128)(2,1)S(1)}, bf16[4,1,2,128,8,16]{3,5,1,4,2,0:T(8,128)(2,1)S(1)}, u32[]{:S(2)}, u32[]{:S(2)}) collective-permute-start(bf16[4,1,2,128,8,16]{3,5,1,4,2,0:T(8,128)(2,1)S(1)} %bitcast.306), channel_id=1, source_target_pairs={{0,7},{1,0},{2,1},{3,2},{4,3},{5,4},{6,5},{7,6},{8,15},{9,8},{10,9... | collective-permute-start | bytes 786440 | tf_op jit(solution)/shard_map/ppermute | solution.py:84
  48.7 21.4 %copy-start.1 = (bf16[128,768]{1,0:T(8,128)(2,1)}, bf16[128,768]{1,0:T(8,128)(2,1)S(1)}, u32[]{:S(2)}) copy-start(bf16[128,768]{1,0:T(8,128)(2,1)S(1)} %get-tuple-element.33) | copy-start | bytes 589828
  51.0 27.2 %all-to-all-start.1 = ((bf16[8,128,1,2,104]{1,4,3,2,0:T(8,128)(2,1)}), bf16[8,128,1,2,104]{1,4,3,2,0:T(8,128)(2,1)S(1)}, u32[]{:S(2)}, u32[]{:S(2)}) async-start(bf16[8,128,1,2,104]{1,4,3,2,0:T(8,128)(2,1)} %broadcast_in_dim.58), calls=%async_computation.1 | async-start | bytes 851968 | tf_op jit(solution)/shard_map/all_to_all | solution.py:150
  56.9 9.9 %collective-permute-start.2 = (bf16[4,1,2,128,8,16]{3,5,1,4,2,0:T(8,128)(2,1)S(1)}, bf16[4,1,2,128,8,16]{3,5,1,4,2,0:T(8,128)(2,1)S(1)}, u32[]{:S(2)}, u32[]{:S(2)}) collective-permute-start(bf16[4,1,2,128,8,16]{3,5,1,4,2,0:T(8,128)(2,1)S(1)} %collective-permute-done), channel_id=1, source_target_pairs={{0,1},{1,2},{2,3},{3,4},{4,5},{5,6},{6,7},{7,0},{8,9},{9,10},{10,1... | collective-permute-start | bytes 786440 | tf_op jit(solution)/shard_map/ppermute | solution.py:81
  58.9 11.2 %collective-permute-start.5 = (bf16[4,1,2,128,8,16]{3,5,1,4,2,0:T(8,128)(2,1)S(1)}, bf16[4,1,2,128,8,16]{3,5,1,4,2,0:T(8,128)(2,1)S(1)}, u32[]{:S(2)}, u32[]{:S(2)}) collective-permute-start(bf16[4,1,2,128,8,16]{3,5,1,4,2,0:T(8,128)(2,1)S(1)} %collective-permute-done.1), channel_id=1, source_target_pairs={{0,7},{1,0},{2,1},{3,2},{4,3},{5,4},{6,5},{7,6},{8,15},{9,8},{10,9... | collective-permute-start | bytes 786440 | tf_op jit(solution)/shard_map/ppermute | solution.py:84
  66.8 9.5 %collective-permute-start.3 = (bf16[4,1,2,128,8,16]{3,5,1,4,2,0:T(8,128)(2,1)S(1)}, bf16[4,1,2,128,8,16]{3,5,1,4,2,0:T(8,128)(2,1)S(1)}, u32[]{:S(2)}, u32[]{:S(2)}) collective-permute-start(bf16[4,1,2,128,8,16]{3,5,1,4,2,0:T(8,128)(2,1)S(1)} %collective-permute-done.2), channel_id=1, source_target_pairs={{0,1},{1,2},{2,3},{3,4},{4,5},{5,6},{6,7},{7,0},{8,9},{9,10},{10,1... | collective-permute-start | bytes 786440 | tf_op jit(solution)/shard_map/ppermute | solution.py:81
  70.1 16.0 %collective-permute-start.6 = (bf16[4,1,2,128,8,16]{3,5,1,4,2,0:T(8,128)(2,1)S(1)}, bf16[4,1,2,128,8,16]{3,5,1,4,2,0:T(8,128)(2,1)S(1)}, u32[]{:S(2)}, u32[]{:S(2)}) collective-permute-start(bf16[4,1,2,128,8,16]{3,5,1,4,2,0:T(8,128)(2,1)S(1)} %collective-permute-done.5), channel_id=1, source_target_pairs={{0,7},{1,0},{2,1},{3,2},{4,3},{5,4},{6,5},{7,6},{8,15},{9,8},{10,9... | collective-permute-start | bytes 786440 | tf_op jit(solution)/shard_map/ppermute | solution.py:84
  76.3 9.5 %collective-permute-start.4 = (bf16[4,1,2,128,8,16]{3,5,1,4,2,0:T(8,128)(2,1)S(1)}, bf16[4,1,2,128,8,16]{3,5,1,4,2,0:T(8,128)(2,1)S(1)}, u32[]{:S(2)}, u32[]{:S(2)}) collective-permute-start(bf16[4,1,2,128,8,16]{3,5,1,4,2,0:T(8,128)(2,1)S(1)} %collective-permute-done.3), channel_id=1, source_target_pairs={{0,1},{1,2},{2,3},{3,4},{4,5},{5,6},{6,7},{7,0},{8,9},{9,10},{10,1... | collective-permute-start | bytes 786440 | tf_op jit(solution)/shard_map/ppermute | solution.py:81
  87.0 4.2 %copy-start.2 = (bf16[1024,1,1,96]{0,3,2,1:T(8,128)(2,1)S(1)}, bf16[1024,1,1,96]{0,3,2,1:T(8,128)(2,1)}, u32[]{:S(2)}) copy-start(bf16[1024,1,1,96]{0,3,2,1:T(8,128)(2,1)} %get-tuple-element.41) | copy-start | bytes 589828
  93.4 13.7 %all-to-all-start.2 = ((bf16[1,8,16,768]{3,2,0,1:T(8,128)(2,1)}), bf16[1,8,16,768]{3,2,0,1:T(8,128)(2,1)S(1)}, u32[]{:S(2)}, u32[]{:S(2)}) async-start(bf16[1,8,16,768]{3,2,0,1:T(8,128)(2,1)} %bitcast.61), calls=%async_computation.2 | async-start | bytes 393216 | tf_op jit(solution)/shard_map/all_to_all | solution.py:158
  124.0 12.9 %all-to-all-start.4 = ((bf16[8,128,1,2,96]{1,4,3,2,0:T(8,128)(2,1)}), bf16[8,128,1,2,96]{1,4,3,2,0:T(8,128)(2,1)}, u32[]{:S(2)}, u32[]{:S(2)}) async-start(bf16[8,128,1,2,96]{1,4,3,2,0:T(8,128)(2,1)} %broadcast_in_dim.62), calls=%async_computation.4 | async-start | bytes 786432 | tf_op jit(solution)/shard_map/all_to_all | solution.py:150
  169.7 11.4 %all-to-all-start.7 = ((bf16[8,128,1,2,96]{1,4,3,2,0:T(8,128)(2,1)}), bf16[8,128,1,2,96]{1,4,3,2,0:T(8,128)(2,1)S(1)}, u32[]{:S(2)}, u32[]{:S(2)}) async-start(bf16[8,128,1,2,96]{1,4,3,2,0:T(8,128)(2,1)} %broadcast_in_dim.64), calls=%async_computation.7 | async-start | bytes 786432 | tf_op jit(solution)/shard_map/all_to_all | solution.py:150
  213.1 11.4 %all-to-all-start.10 = ((bf16[8,128,1,2,96]{1,4,3,2,0:T(8,128)(2,1)}), bf16[8,128,1,2,96]{1,4,3,2,0:T(8,128)(2,1)S(1)}, u32[]{:S(2)}, u32[]{:S(2)}) async-start(bf16[8,128,1,2,96]{1,4,3,2,0:T(8,128)(2,1)} %broadcast_in_dim.66), calls=%async_computation.10 | async-start | bytes 786432 | tf_op jit(solution)/shard_map/all_to_all | solution.py:150
  224.6 31.5 %copy-start.6 = (bf16[3,768]{1,0:T(4,128)(2,1)S(1)}, bf16[3,768]{1,0:T(4,128)(2,1)}, u32[]{:S(2)}) copy-start(bf16[3,768]{1,0:T(4,128)(2,1)} %param.29) | copy-start | bytes 13828
  241.3 14.2 %all-to-all-start.12 = ((bf16[1,8,16,768]{3,2,0,1:T(8,128)(2,1)}), bf16[1,8,16,768]{3,2,0,1:T(8,128)(2,1)S(1)}, u32[]{:S(2)}, u32[]{:S(2)}) async-start(bf16[1,8,16,768]{3,2,0,1:T(8,128)(2,1)} %broadcast_in_dim.67), calls=%async_computation.12 | async-start | bytes 393216 | tf_op jit(solution)/shard_map/all_to_all | solution.py:150

commit v10 on v7

--- a/solution.py
+++ b/solution.py
@@ -83,9 +83,9 @@
             leftward = lax.ppermute(leftward, "smp", backward)
             pieces[step] = leftward
     offsets = sorted(pieces)
-    stacked = jnp.concatenate([pieces[d] for d in offsets], axis=1)
-    stacked = jnp.roll(stacked, lax.axis_index("smp") + offsets[0], axis=1)
-    stacked = jnp.transpose(stacked, (0, 2, 3, 4, 1, 5))
+    shape = (blocks, group_members, row_count, col_count, 1, keys_dev)
+    stacked = jnp.concatenate([pieces[d].reshape(shape) for d in offsets], axis=4)
+    stacked = jnp.roll(stacked, lax.axis_index("smp") + offsets[0], axis=4)
     return stacked.reshape(blocks, group_members, row_count, col_count * copies * keys_dev)
 
 

time: 257 us -> 257 us (level)
  no operation moved by 1% of the time
where the time goes in v10:
time: 257 us; the launch traced here: 255 us
  blocking collectives  81 us (32%)
  starting transfers between devices  65.7 us (26%)
  waiting for transfers between devices  53.1 us (21%)
  matrix products  19.9 us (8%)
  local copies, waits for them, and re-layouts  19 us (7%)
  other arithmetic  9.72 us (4%)
  between operations  6.8 us (3%)
    all_to_all x3, blocking collectives, scatter_sum_rows(): arrived = lax.all_to_all(pieces, axis_name, 1, 1, tiled=True)  40.8 us
    all_to_all x3, blocking collectives, gather_by_exchange(): joined = lax.all_to_all(spread, axis_name, axis, axis, tiled=True)  40.1 us
    all_to_all x5, waiting for transfers between devices, gather_by_exchange(): joined = lax.all_to_all(spread, axis_name, axis, axis, tiled=True)  26.9 us
    all_to_all x5, starting transfers between devices, gather_by_exchange(): joined = lax.all_to_all(spread, axis_name, axis, axis, tiled=True)  25.2 us
    ppermute x3, starting transfers between devices, spread_bias(): leftward = lax.ppermute(leftward, 'smp', backward)  18.9 us
    ppermute x4, waiting for transfers between devices, spread_bias(): rightward = lax.ppermute(rightward, 'smp', forward)  15.9 us
    all_to_all x1, waiting for transfers between devices, scatter_sum_rows(): arrived = lax.all_to_all(pieces, axis_name, 1, 1, tiled=True)  10.3 us
    ppermute x4, starting transfers between devices, spread_bias(): rightward = lax.ppermute(rightward, 'smp', forward)  9.3 us
  transfers between devices with their start and end apart: 14, of which 9 were waited for; matrix products, arithmetic and copies ran while one was open for 6% of the time, Pallas kernels for 0%

profile of v10, /device:TPU:8, one launch (start us, length us, event | category | flops | bytes accessed | tf_op | source)
XLA Modules:
  0.0 255.2 jit_solution(11520604718380971266)
XLA Ops:
  6.9 6.2 %all-to-all-start = ((bf16[4,8,2,128,1,16]{3,5,2,0,4,1:T(8,128)(2,1)}), bf16[4,8,2,128,1,16]{3,5,2,0,4,1:T(8,128)(2,1)S(1)}, u32[]{:S(2)}, u32[]{:S(2)}) async-start(bf16[4,8,2,128,1,16]{3,5,2,0,4,1:T(8,128)(2,1)} %copy.79), calls=%async_computation | async-start | bytes 524288 | tf_op jit(solution)/shard_map/all_to_all | solution.py:69
  19.4 2.6 %copy.76 = f32[3,8192]{0,1:T(8,128)} copy(f32[3,8192]{1,0:T(4,128)S(1)} %copy-done.4) | data formatting | bytes 196608 | tf_op args[2]
  22.0 2.8 %gather_fusion = f32[128,3]{1,0:T(8,128)S(1)} fusion(f32[3,8192]{0,1:T(8,128)} %copy.76, s32[1024]{0:T(1024)S(1)} %pad_clamp_fusion), kind=kCustom, calls=%fused_computation | custom fusion | bytes 3584 | tf_op jit(solution)/shard_map/jit(_take)/gather | solution.py:46
  28.0 6.4 %all-to-all-start.1 = ((bf16[8,128,1,2,104]{1,4,3,2,0:T(8,128)(2,1)}), bf16[8,128,1,2,104]{1,4,3,2,0:T(8,128)(2,1)S(1)}, u32[]{:S(2)}, u32[]{:S(2)}) async-start(bf16[8,128,1,2,104]{1,4,3,2,0:T(8,128)(2,1)} %broadcast_in_dim.58), calls=%async_computation.1 | async-start | bytes 851968 | tf_op jit(solution)/shard_map/all_to_all | solution.py:146
  34.4 3.6 %collective-permute-start = (bf16[4,1,2,128,8,16]{3,5,4,2,0,1:T(8,128)(2,1)S(1)}, bf16[4,1,2,128,8,16]{3,5,4,2,0,1:T(8,128)(2,1)S(1)}, u32[]{:S(2)}, u32[]{:S(2)}) collective-permute-start(bf16[4,1,2,128,8,16]{3,5,4,2,0,1:T(8,128)(2,1)S(1)} %bitcast.345), channel_id=1, source_target_pairs={{0,1},{1,2},{2,3},{3,4},{4,5},{5,6},{6,7},{7,0},{8,9},{9,10},{10,1... | collective-permute-start | bytes 786440 | tf_op jit(solution)/shard_map/ppermute | solution.py:80
  38.0 8.6 %collective-permute-start.4 = (bf16[4,1,2,128,8,16]{3,5,4,2,0,1:T(8,128)(2,1)S(1)}, bf16[4,1,2,128,8,16]{3,5,4,2,0,1:T(8,128)(2,1)S(1)}, u32[]{:S(2)}, u32[]{:S(2)}) collective-permute-start(bf16[4,1,2,128,8,16]{3,5,4,2,0,1:T(8,128)(2,1)S(1)} %bitcast.346), channel_id=1, source_target_pairs={{0,7},{1,0},{2,1},{3,2},{4,3},{5,4},{6,5},{7,6},{8,15},{9,8},{10,9... | collective-permute-start | bytes 786440 | tf_op jit(solution)/shard_map/ppermute | solution.py:83
  47.9 3.2 %collective-permute-done = bf16[4,1,2,128,8,16]{3,5,4,2,0,1:T(8,128)(2,1)S(1)} collective-permute-done((bf16[4,1,2,128,8,16]{3,5,4,2,0,1:T(8,128)(2,1)S(1)}, bf16[4,1,2,128,8,16]{3,5,4,2,0,1:T(8,128)(2,1)S(1)}, u32[]{:S(2)}, u32[]{:S(2)}) %collective-permute-start) | collective-permute-done | bytes 262176 | tf_op jit(solution)/shard_map/ppermute | solution.py:80
  51.1 1.9 collective-permute-start.1
  53.0 5.1 %collective-permute-start.5 = (bf16[4,1,2,128,8,16]{3,5,4,2,0,1:T(8,128)(2,1)S(1)}, bf16[4,1,2,128,8,16]{3,5,4,2,0,1:T(8,128)(2,1)S(1)}, u32[]{:S(2)}, u32[]{:S(2)}) collective-permute-start(bf16[4,1,2,128,8,16]{3,5,4,2,0,1:T(8,128)(2,1)S(1)} %collective-permute-done.4), channel_id=1, source_target_pairs={{0,7},{1,0},{2,1},{3,2},{4,3},{5,4},{6,5},{7,6},{8,15},{9,8},{10,9... | collective-permute-start | bytes 786440 | tf_op jit(solution)/shard_map/ppermute | solution.py:83
  58.3 3.5 %collective-permute-done.1 = bf16[4,1,2,128,8,16]{3,5,4,2,0,1:T(8,128)(2,1)S(1)} collective-permute-done((bf16[4,1,2,128,8,16]{3,5,4,2,0,1:T(8,128)(2,1)S(1)}, bf16[4,1,2,128,8,16]{3,5,4,2,0,1:T(8,128)(2,1)S(1)}, u32[]{:S(2)}, u32[]{:S(2)}) %collective-permute-start.1) | collective-permute-done | bytes 262176 | tf_op jit(solution)/shard_map/ppermute | solution.py:80
  61.8 1.9 collective-permute-start.2
  63.7 5.1 %collective-permute-start.6 = (bf16[4,1,2,128,8,16]{3,5,4,2,0,1:T(8,128)(2,1)S(1)}, bf16[4,1,2,128,8,16]{3,5,4,2,0,1:T(8,128)(2,1)S(1)}, u32[]{:S(2)}, u32[]{:S(2)}) collective-permute-start(bf16[4,1,2,128,8,16]{3,5,4,2,0,1:T(8,128)(2,1)S(1)} %collective-permute-done.5), channel_id=1, source_target_pairs={{0,7},{1,0},{2,1},{3,2},{4,3},{5,4},{6,5},{7,6},{8,15},{9,8},{10,9... | collective-permute-start | bytes 786440 | tf_op jit(solution)/shard_map/ppermute | solution.py:83
  69.1 2.5 collective-permute-done.2
  71.6 1.9 collective-permute-start.3
  74.3 6.8 %collective-permute-done.3 = bf16[4,1,2,128,8,16]{3,5,4,2,0,1:T(8,128)(2,1)S(1)} collective-permute-done((bf16[4,1,2,128,8,16]{3,5,4,2,0,1:T(8,128)(2,1)S(1)}, bf16[4,1,2,128,8,16]{3,5,4,2,0,1:T(8,128)(2,1)S(1)}, u32[]{:S(2)}, u32[]{:S(2)}) %collective-permute-start.3) | collective-permute-done | bytes 262176 | tf_op jit(solution)/shard_map/ppermute | solution.py:80
  86.5 1.8 convolution_convert_fusion.4
  88.3 6.1 %all-to-all-start.2 = ((bf16[1,8,16,768]{3,2,0,1:T(8,128)(2,1)}), bf16[1,8,16,768]{3,2,0,1:T(8,128)(2,1)S(1)}, u32[]{:S(2)}, u32[]{:S(2)}) async-start(bf16[1,8,16,768]{3,2,0,1:T(8,128)(2,1)} %bitcast.83), calls=%async_computation.2 | async-start | bytes 393216 | tf_op jit(solution)/shard_map/all_to_all | solution.py:154
  94.5 10.3 %all-to-all-done.2 = bf16[1,8,16,768]{3,2,0,1:T(8,128)(2,1)S(1)} async-done(((bf16[1,8,16,768]{3,2,0,1:T(8,128)(2,1)}), bf16[1,8,16,768]{3,2,0,1:T(8,128)(2,1)S(1)}, u32[]{:S(2)}, u32[]{:S(2)}) %all-to-all-start.2) | async-done | bytes 196640 | tf_op jit(solution)/shard_map/all_to_all | solution.py:154
  106.0 14.1 %all_to_all.78 = bf16[1,8,16,768]{3,2,0,1:T(8,128)(2,1)S(1)} all-to-all(bf16[1,8,16,768]{3,2,0,1:T(8,128)(2,1)S(1)} %broadcast_in_dim.61), channel_id=1, replica_groups=mesh['row'=8,'col'=8,'smp'=8] {'col'}, dimensions={1} | all-to-all | bytes 393216 | tf_op jit(solution)/shard_map/all_to_all | solution.py:146
  122.0 5.6 %all-to-all-start.4 = ((bf16[8,128,1,2,96]{1,4,3,2,0:T(8,128)(2,1)}), bf16[8,128,1,2,96]{1,4,3,2,0:T(8,128)(2,1)}, u32[]{:S(2)}, u32[]{:S(2)}) async-start(bf16[8,128,1,2,96]{1,4,3,2,0:T(8,128)(2,1)} %broadcast_in_dim.62), calls=%async_computation.4 | async-start | bytes 786432 | tf_op jit(solution)/shard_map/all_to_all | solution.py:146
  129.1 5.5 %all-to-all-done.4 = bf16[8,128,1,2,96]{1,4,3,2,0:T(8,128)(2,1)} async-done(((bf16[8,128,1,2,96]{1,4,3,2,0:T(8,128)(2,1)}), bf16[8,128,1,2,96]{1,4,3,2,0:T(8,128)(2,1)}, u32[]{:S(2)}, u32[]{:S(2)}) %all-to-all-start.4) | async-done | bytes 393248 | tf_op jit(solution)/shard_map/all_to_all | solution.py:146
  138.0 13.6 %all_to_all.79 = bf16[1,8,16,768]{3,2,0,1:T(8,128)(2,1)S(1)} all-to-all(bf16[1,8,16,768]{3,2,0,1:T(8,128)(2,1)S(1)} %bitcast.332), channel_id=1, replica_groups=mesh['row'=8,'col'=8,'smp'=8] {'col'}, dimensions={1} | all-to-all | bytes 393216 | tf_op jit(solution)/shard_map/all_to_all | solution.py:154
  152.1 12.7 %all_to_all.80 = bf16[1,8,16,768]{3,2,0,1:T(8,128)(2,1)S(1)} all-to-all(bf16[1,8,16,768]{3,2,0,1:T(8,128)(2,1)S(1)} %broadcast_in_dim.63), channel_id=1, replica_groups=mesh['row'=8,'col'=8,'smp'=8] {'col'}, dimensions={1} | all-to-all | bytes 393216 | tf_op jit(solution)/shard_map/all_to_all | solution.py:146
  166.8 5.2 %all-to-all-start.7 = ((bf16[8,128,1,2,96]{1,4,3,2,0:T(8,128)(2,1)}), bf16[8,128,1,2,96]{1,4,3,2,0:T(8,128)(2,1)S(1)}, u32[]{:S(2)}, u32[]{:S(2)}) async-start(bf16[8,128,1,2,96]{1,4,3,2,0:T(8,128)(2,1)} %broadcast_in_dim.64), calls=%async_computation.7 | async-start | bytes 786432 | tf_op jit(solution)/shard_map/all_to_all | solution.py:146
  173.5 5.3 %all-to-all-done.7 = bf16[8,128,1,2,96]{1,4,3,2,0:T(8,128)(2,1)S(1)} async-done(((bf16[8,128,1,2,96]{1,4,3,2,0:T(8,128)(2,1)}), bf16[8,128,1,2,96]{1,4,3,2,0:T(8,128)(2,1)S(1)}, u32[]{:S(2)}, u32[]{:S(2)}) %all-to-all-start.7) | async-done | bytes 393248 | tf_op jit(solution)/shard_map/all_to_all | solution.py:146
  181.2 13.6 %all_to_all.81 = bf16[1,8,16,768]{3,2,0,1:T(8,128)(2,1)S(1)} all-to-all(bf16[1,8,16,768]{3,2,0,1:T(8,128)(2,1)S(1)} %bitcast.333), channel_id=1, replica_groups=mesh['row'=8,'col'=8,'smp'=8] {'col'}, dimensions={1} | all-to-all | bytes 393216 | tf_op jit(solution)/shard_map/all_to_all | solution.py:154
  195.3 13.4 %all_to_all.82 = bf16[1,8,16,768]{3,2,0,1:T(8,128)(2,1)S(1)} all-to-all(bf16[1,8,16,768]{3,2,0,1:T(8,128)(2,1)S(1)} %broadcast_in_dim.65), channel_id=1, replica_groups=mesh['row'=8,'col'=8,'smp'=8] {'col'}, dimensions={1} | all-to-all | bytes 393216 | tf_op jit(solution)/shard_map/all_to_all | solution.py:146
  210.7 4.6 %all-to-all-start.10 = ((bf16[8,128,1,2,96]{1,4,3,2,0:T(8,128)(2,1)}), bf16[8,128,1,2,96]{1,4,3,2,0:T(8,128)(2,1)S(1)}, u32[]{:S(2)}, u32[]{:S(2)}) async-start(bf16[8,128,1,2,96]{1,4,3,2,0:T(8,128)(2,1)} %broadcast_in_dim.66), calls=%async_computation.10 | async-start | bytes 786432 | tf_op jit(solution)/shard_map/all_to_all | solution.py:146
  216.8 5.4 %all-to-all-done.10 = bf16[8,128,1,2,96]{1,4,3,2,0:T(8,128)(2,1)S(1)} async-done(((bf16[8,128,1,2,96]{1,4,3,2,0:T(8,128)(2,1)}), bf16[8,128,1,2,96]{1,4,3,2,0:T(8,128)(2,1)S(1)}, u32[]{:S(2)}, u32[]{:S(2)}) %all-to-all-start.10) | async-done | bytes 393248 | tf_op jit(solution)/shard_map/all_to_all | solution.py:146
  224.6 13.6 %all_to_all.83 = bf16[1,8,16,768]{3,2,0,1:T(8,128)(2,1)S(1)} all-to-all(bf16[1,8,16,768]{3,2,0,1:T(8,128)(2,1)S(1)} %bitcast.334), channel_id=1, replica_groups=mesh['row'=8,'col'=8,'smp'=8] {'col'}, dimensions={1} | all-to-all | bytes 393216 | tf_op jit(solution)/shard_map/all_to_all | solution.py:154
  239.0 3.4 %all-to-all-start.12 = ((bf16[1,8,16,768]{3,2,0,1:T(8,128)(2,1)}), bf16[1,8,16,768]{3,2,0,1:T(8,128)(2,1)S(1)}, u32[]{:S(2)}, u32[]{:S(2)}) async-start(bf16[1,8,16,768]{3,2,0,1:T(8,128)(2,1)} %broadcast_in_dim.67), calls=%async_computation.12 | async-start | bytes 393216 | tf_op jit(solution)/shard_map/all_to_all | solution.py:146
  242.4 10.7 %all-to-all-done.12 = bf16[1,8,16,768]{3,2,0,1:T(8,128)(2,1)S(1)} async-done(((bf16[1,8,16,768]{3,2,0,1:T(8,128)(2,1)}), bf16[1,8,16,768]{3,2,0,1:T(8,128)(2,1)S(1)}, u32[]{:S(2)}, u32[]{:S(2)}) %all-to-all-start.12) | async-done | bytes 196640 | tf_op jit(solution)/shard_map/all_to_all | solution.py:146
  (168 shorter events, 41.3 us)
Async XLA Ops:
  0.6 5.0 %copy-start = (bf16[128,4,16]{0,2,1:T(8,128)(2,1)S(1)}, bf16[128,4,16]{0,2,1:T(8,128)(2,1)}, u32[]{:S(2)}) copy-start(bf16[128,4,16]{0,2,1:T(8,128)(2,1)} %param.25) | copy-start | bytes 49156
  0.6 12.5 %copy-start.7 = (f32[1,3]{1,0:T(1,128)S(1)}, f32[1,3]{1,0:T(1,128)}, u32[]{:S(2)}) copy-start(f32[1,3]{1,0:T(1,128)} %param.21) | copy-start | bytes 40
  0.7 17.6 %copy-start.12 = (s32[128]{0:T(128)S(1)}, s32[128]{0:T(128)}, u32[]{:S(2)}) copy-start(s32[128]{0:T(128)} %param.18) | copy-start | bytes 1540
  0.7 18.7 %copy-start.4 = (f32[3,8192]{1,0:T(4,128)S(1)}, f32[3,8192]{1,0:T(4,128)}, u32[]{:S(2)}) copy-start(f32[3,8192]{1,0:T(4,128)} %param.17) | copy-start | bytes 294916
  2.1 23.0 %copy-start.10 = (f32[1,3,128]{2,0,1:T(1,128)S(1)}, f32[1,3,128]{2,0,1:T(1,128)}, u32[]{:S(2)}) copy-start(f32[1,3,128]{2,0,1:T(1,128)} %param.23) | copy-start | bytes 4612
  2.1 23.1 %copy-start.5 = (f32[4,768]{1,0:T(4,128)S(1)}, f32[4,768]{1,0:T(4,128)}, u32[]{:S(2)}) copy-start(f32[4,768]{1,0:T(4,128)} %param.24) | copy-start | bytes 36868
  2.1 23.1 %copy-start.3 = (bf16[128,768]{1,0:T(8,128)(2,1)S(1)}, bf16[128,768]{1,0:T(8,128)(2,1)}, u32[]{:S(2)}) copy-start(bf16[128,768]{1,0:T(8,128)(2,1)} %param.15) | copy-start | bytes 589828
  3.9 21.9 %copy-start.8 = (s32[128]{0:T(128)S(1)}, s32[128]{0:T(128)}, u32[]{:S(2)}) copy-start(s32[128]{0:T(128)} %param.19) | copy-start | bytes 1540
  3.9 21.9 %copy-start.11 = (s32[128]{0:T(128)S(1)}, s32[128]{0:T(128)}, u32[]{:S(2)}) copy-start(s32[128]{0:T(128)} %param.20) | copy-start | bytes 1540
  6.9 20.2 %all-to-all-start = ((bf16[4,8,2,128,1,16]{3,5,2,0,4,1:T(8,128)(2,1)}), bf16[4,8,2,128,1,16]{3,5,2,0,4,1:T(8,128)(2,1)S(1)}, u32[]{:S(2)}, u32[]{:S(2)}) async-start(bf16[4,8,2,128,1,16]{3,5,2,0,4,1:T(8,128)(2,1)} %copy.79), calls=%async_computation | async-start | bytes 524288 | tf_op jit(solution)/shard_map/all_to_all | solution.py:69
  19.4 28.5 %copy-start.9 = (f32[4,16]{1,0:T(4,128)S(1)}, f32[4,16]{1,0:T(4,128)}, u32[]{:S(2)}) copy-start(f32[4,16]{1,0:T(4,128)} %param.26) | copy-start | bytes 772
  25.6 27.4 %copy-start.1 = (bf16[128,768]{1,0:T(8,128)(2,1)}, bf16[128,768]{1,0:T(8,128)(2,1)S(1)}, u32[]{:S(2)}) copy-start(bf16[128,768]{1,0:T(8,128)(2,1)S(1)} %get-tuple-element.29) | copy-start | bytes 589828
  28.0 40.9 %all-to-all-start.1 = ((bf16[8,128,1,2,104]{1,4,3,2,0:T(8,128)(2,1)}), bf16[8,128,1,2,104]{1,4,3,2,0:T(8,128)(2,1)S(1)}, u32[]{:S(2)}, u32[]{:S(2)}) async-start(bf16[8,128,1,2,104]{1,4,3,2,0:T(8,128)(2,1)} %broadcast_in_dim.58), calls=%async_computation.1 | async-start | bytes 851968 | tf_op jit(solution)/shard_map/all_to_all | solution.py:146
  34.4 16.7 %collective-permute-start = (bf16[4,1,2,128,8,16]{3,5,4,2,0,1:T(8,128)(2,1)S(1)}, bf16[4,1,2,128,8,16]{3,5,4,2,0,1:T(8,128)(2,1)S(1)}, u32[]{:S(2)}, u32[]{:S(2)}) collective-permute-start(bf16[4,1,2,128,8,16]{3,5,4,2,0,1:T(8,128)(2,1)S(1)} %bitcast.345), channel_id=1, source_target_pairs={{0,1},{1,2},{2,3},{3,4},{4,5},{5,6},{6,7},{7,0},{8,9},{9,10},{10,1... | collective-permute-start | bytes 786440 | tf_op jit(solution)/shard_map/ppermute | solution.py:80
  38.0 15.0 %collective-permute-start.4 = (bf16[4,1,2,128,8,16]{3,5,4,2,0,1:T(8,128)(2,1)S(1)}, bf16[4,1,2,128,8,16]{3,5,4,2,0,1:T(8,128)(2,1)S(1)}, u32[]{:S(2)}, u32[]{:S(2)}) collective-permute-start(bf16[4,1,2,128,8,16]{3,5,4,2,0,1:T(8,128)(2,1)S(1)} %bitcast.346), channel_id=1, source_target_pairs={{0,7},{1,0},{2,1},{3,2},{4,3},{5,4},{6,5},{7,6},{8,15},{9,8},{10,9... | collective-permute-start | bytes 786440 | tf_op jit(solution)/shard_map/ppermute | solution.py:83
  51.1 10.7 %collective-permute-start.1 = (bf16[4,1,2,128,8,16]{3,5,4,2,0,1:T(8,128)(2,1)S(1)}, bf16[4,1,2,128,8,16]{3,5,4,2,0,1:T(8,128)(2,1)S(1)}, u32[]{:S(2)}, u32[]{:S(2)}) collective-permute-start(bf16[4,1,2,128,8,16]{3,5,4,2,0,1:T(8,128)(2,1)S(1)} %collective-permute-done), channel_id=1, source_target_pairs={{0,1},{1,2},{2,3},{3,4},{4,5},{5,6},{6,7},{7,0},{8,9},{9,10},{10,1... | collective-permute-start | bytes 786440 | tf_op jit(solution)/shard_map/ppermute | solution.py:80
  53.0 10.7 %collective-permute-start.5 = (bf16[4,1,2,128,8,16]{3,5,4,2,0,1:T(8,128)(2,1)S(1)}, bf16[4,1,2,128,8,16]{3,5,4,2,0,1:T(8,128)(2,1)S(1)}, u32[]{:S(2)}, u32[]{:S(2)}) collective-permute-start(bf16[4,1,2,128,8,16]{3,5,4,2,0,1:T(8,128)(2,1)S(1)} %collective-permute-done.4), channel_id=1, source_target_pairs={{0,7},{1,0},{2,1},{3,2},{4,3},{5,4},{6,5},{7,6},{8,15},{9,8},{10,9... | collective-permute-start | bytes 786440 | tf_op jit(solution)/shard_map/ppermute | solution.py:83
  61.8 9.8 %collective-permute-start.2 = (bf16[4,1,2,128,8,16]{3,5,4,2,0,1:T(8,128)(2,1)S(1)}, bf16[4,1,2,128,8,16]{3,5,4,2,0,1:T(8,128)(2,1)S(1)}, u32[]{:S(2)}, u32[]{:S(2)}) collective-permute-start(bf16[4,1,2,128,8,16]{3,5,4,2,0,1:T(8,128)(2,1)S(1)} %collective-permute-done.1), channel_id=1, source_target_pairs={{0,1},{1,2},{2,3},{3,4},{4,5},{5,6},{6,7},{7,0},{8,9},{9,10},{10,1... | collective-permute-start | bytes 786440 | tf_op jit(solution)/shard_map/ppermute | solution.py:80
  63.7 17.7 %collective-permute-start.6 = (bf16[4,1,2,128,8,16]{3,5,4,2,0,1:T(8,128)(2,1)S(1)}, bf16[4,1,2,128,8,16]{3,5,4,2,0,1:T(8,128)(2,1)S(1)}, u32[]{:S(2)}, u32[]{:S(2)}) collective-permute-start(bf16[4,1,2,128,8,16]{3,5,4,2,0,1:T(8,128)(2,1)S(1)} %collective-permute-done.5), channel_id=1, source_target_pairs={{0,7},{1,0},{2,1},{3,2},{4,3},{5,4},{6,5},{7,6},{8,15},{9,8},{10,9... | collective-permute-start | bytes 786440 | tf_op jit(solution)/shard_map/ppermute | solution.py:83
  71.6 9.5 %collective-permute-start.3 = (bf16[4,1,2,128,8,16]{3,5,4,2,0,1:T(8,128)(2,1)S(1)}, bf16[4,1,2,128,8,16]{3,5,4,2,0,1:T(8,128)(2,1)S(1)}, u32[]{:S(2)}, u32[]{:S(2)}) collective-permute-start(bf16[4,1,2,128,8,16]{3,5,4,2,0,1:T(8,128)(2,1)S(1)} %collective-permute-done.2), channel_id=1, source_target_pairs={{0,1},{1,2},{2,3},{3,4},{4,5},{5,6},{6,7},{7,0},{8,9},{9,10},{10,1... | collective-permute-start | bytes 786440 | tf_op jit(solution)/shard_map/ppermute | solution.py:80
  81.9 4.2 %copy-start.2 = (bf16[1024,1,1,96]{0,3,2,1:T(8,128)(2,1)S(1)}, bf16[1024,1,1,96]{0,3,2,1:T(8,128)(2,1)}, u32[]{:S(2)}) copy-start(bf16[1024,1,1,96]{0,3,2,1:T(8,128)(2,1)} %get-tuple-element.37) | copy-start | bytes 589828
  88.3 16.4 %all-to-all-start.2 = ((bf16[1,8,16,768]{3,2,0,1:T(8,128)(2,1)}), bf16[1,8,16,768]{3,2,0,1:T(8,128)(2,1)S(1)}, u32[]{:S(2)}, u32[]{:S(2)}) async-start(bf16[1,8,16,768]{3,2,0,1:T(8,128)(2,1)} %bitcast.83), calls=%async_computation.2 | async-start | bytes 393216 | tf_op jit(solution)/shard_map/all_to_all | solution.py:154
  122.0 12.6 %all-to-all-start.4 = ((bf16[8,128,1,2,96]{1,4,3,2,0:T(8,128)(2,1)}), bf16[8,128,1,2,96]{1,4,3,2,0:T(8,128)(2,1)}, u32[]{:S(2)}, u32[]{:S(2)}) async-start(bf16[8,128,1,2,96]{1,4,3,2,0:T(8,128)(2,1)} %broadcast_in_dim.62), calls=%async_computation.4 | async-start | bytes 786432 | tf_op jit(solution)/shard_map/all_to_all | solution.py:146
  166.8 12.0 %all-to-all-start.7 = ((bf16[8,128,1,2,96]{1,4,3,2,0:T(8,128)(2,1)}), bf16[8,128,1,2,96]{1,4,3,2,0:T(8,128)(2,1)S(1)}, u32[]{:S(2)}, u32[]{:S(2)}) async-start(bf16[8,128,1,2,96]{1,4,3,2,0:T(8,128)(2,1)} %broadcast_in_dim.64), calls=%async_computation.7 | async-start | bytes 786432 | tf_op jit(solution)/shard_map/all_to_all | solution.py:146
  210.7 11.4 %all-to-all-start.10 = ((bf16[8,128,1,2,96]{1,4,3,2,0:T(8,128)(2,1)}), bf16[8,128,1,2,96]{1,4,3,2,0:T(8,128)(2,1)S(1)}, u32[]{:S(2)}, u32[]{:S(2)}) async-start(bf16[8,128,1,2,96]{1,4,3,2,0:T(8,128)(2,1)} %broadcast_in_dim.66), calls=%async_computation.10 | async-start | bytes 786432 | tf_op jit(solution)/shard_map/all_to_all | solution.py:146
  222.2 31.5 %copy-start.6 = (bf16[3,768]{1,0:T(4,128)(2,1)S(1)}, bf16[3,768]{1,0:T(4,128)(2,1)}, u32[]{:S(2)}) copy-start(bf16[3,768]{1,0:T(4,128)(2,1)} %param.29) | copy-start | bytes 13828
  239.0 14.2 %all-to-all-start.12 = ((bf16[1,8,16,768]{3,2,0,1:T(8,128)(2,1)}), bf16[1,8,16,768]{3,2,0,1:T(8,128)(2,1)S(1)}, u32[]{:S(2)}, u32[]{:S(2)}) async-start(bf16[1,8,16,768]{3,2,0,1:T(8,128)(2,1)} %broadcast_in_dim.67), calls=%async_computation.12 | async-start | bytes 393216 | tf_op jit(solution)/shard_map/all_to_all | solution.py:146

commit v11 on v10

--- a/solution.py
+++ b/solution.py
@@ -85,8 +85,13 @@
     offsets = sorted(pieces)
     shape = (blocks, group_members, row_count, col_count, 1, keys_dev)
     stacked = jnp.concatenate([pieces[d].reshape(shape) for d in offsets], axis=4)
-    stacked = jnp.roll(stacked, lax.axis_index("smp") + offsets[0], axis=4)
-    return stacked.reshape(blocks, group_members, row_count, col_count * copies * keys_dev)
+    return stacked, lax.axis_index("smp") + offsets[0]
+
+
+def block_bias(stacked, shift, block_index):
+    _, group_members, row_count, col_count, copies, keys_dev = stacked.shape
+    rolled = jnp.roll(stacked[block_index], shift, axis=3)
+    return rolled.reshape(group_members, row_count, col_count * copies * keys_dev)
 
 
 def build_absorber(
@@ -179,14 +184,14 @@
         "ikc,cbh->bhik", pair_normed, pair_bias_weight, preferred_element_type=jnp.float32
     ).astype(jnp.bfloat16)
     column_bias = relay_bias(local_bias)
-    gathered_pair_bias = spread_bias(column_bias)
+    stacked_bias, bias_shift = spread_bias(column_bias)
     samples, row_count, model_width = hidden_activity.shape
     col_count = lax.axis_size("col")
     own_rows = row_count // col_count
     own_start = lax.axis_index("col") * own_rows
     own_hidden = lax.dynamic_slice_in_dim(hidden_activity, own_start, own_rows, 1)
     normed = layer_norm(hidden_activity.astype(jnp.float32)).astype(jnp.bfloat16)
-    group_members = gathered_pair_bias.shape[1]
+    group_members = stacked_bias.shape[1]
     head_size = query_key_value_gate_weight.shape[2] // group_members
     group_offset = lax.axis_index("col") * group_members
     input_scaling = head_size ** (-0.5)
@@ -224,7 +229,7 @@
         )
         absorb = build_absorber(
             query_vectors,
-            gathered_pair_bias[block_index],
+            block_bias(stacked_bias, bias_shift, block_index),
             chain_offset,
             chain_label,
             gathered_chain_ids,

time: 257 us -> 258 us (level)
  blocking collectives: 81 us -> 67.6 us
  waiting for transfers between devices: 53.1 us -> 57.9 us
  starting transfers between devices: 65.7 us -> 69 us
  local copies, waits for them, and re-layouts: 19 us -> 22.2 us
    all_to_all x3 -> x2, blocking collectives: 40.1 us -> 26.7 us  [gather_by_exchange(): joined = lax.all_to_all(spread, axis_name, axis, axis, tiled=True)]
    all_to_all x5 -> x6, waiting for transfers between devices: 26.9 us -> 34.5 us  [gather_by_exchange(): joined = lax.all_to_all(spread, axis_name, axis, axis, tiled=True)]
    all_to_all x5 -> x6, starting transfers between devices: 25.2 us -> 28.5 us  [gather_by_exchange(): joined = lax.all_to_all(spread, axis_name, axis, axis, tiled=True)]
    ppermute x4, waiting for transfers between devices: 15.9 us -> 13.1 us  [spread_bias(): rightward = lax.ppermute(rightward, 'smp', forward)]
    unnamed x45 -> x79, local copies, waits for them, and re-layouts: 4.69 us -> 6.3 us
  transfers between devices with their start and end apart: 14 -> 15, of which waited for: 9 -> 10; matrix products, arithmetic and copies ran while one was open for 6% -> 8% of each run, Pallas kernels for 0% -> 0%
where the time goes in v11:
time: 258 us; the launch traced here: 256 us
  starting transfers between devices  69 us (27%)
  blocking collectives  67.6 us (26%)
  waiting for transfers between devices  57.9 us (22%)
  local copies, waits for them, and re-layouts  22.2 us (9%)
  matrix products  20.3 us (8%)
  other arithmetic  11.8 us (5%)
  between operations  7.01 us (3%)
    all_to_all x3, blocking collectives, scatter_sum_rows(): arrived = lax.all_to_all(pieces, axis_name, 1, 1, tiled=True)  40.8 us
    all_to_all x6, waiting for transfers between devices, gather_by_exchange(): joined = lax.all_to_all(spread, axis_name, axis, axis, tiled=True)  34.5 us
    all_to_all x6, starting transfers between devices, gather_by_exchange(): joined = lax.all_to_all(spread, axis_name, axis, axis, tiled=True)  28.5 us
    all_to_all x2, blocking collectives, gather_by_exchange(): joined = lax.all_to_all(spread, axis_name, axis, axis, tiled=True)  26.7 us
    ppermute x3, starting transfers between devices, spread_bias(): leftward = lax.ppermute(leftward, 'smp', backward)  18.9 us
    ppermute x4, waiting for transfers between devices, spread_bias(): rightward = lax.ppermute(rightward, 'smp', forward)  13.1 us
    all_to_all x1, waiting for transfers between devices, scatter_sum_rows(): arrived = lax.all_to_all(pieces, axis_name, 1, 1, tiled=True)  10.3 us
    ppermute x4, starting transfers between devices, spread_bias(): rightward = lax.ppermute(rightward, 'smp', forward)  9.36 us
  transfers between devices with their start and end apart: 15, of which 10 were waited for; matrix products, arithmetic and copies ran while one was open for 8% of the time, Pallas kernels for 0%

profile of v11, /device:TPU:8, one launch (start us, length us, event | category | flops | bytes accessed | tf_op | source)
XLA Modules:
  0.0 255.9 jit_solution(14412203473216163601)
XLA Ops:
  6.8 6.2 %all-to-all-start = ((bf16[4,8,2,128,1,16]{3,5,2,0,4,1:T(8,128)(2,1)}), bf16[4,8,2,128,1,16]{3,5,2,0,4,1:T(8,128)(2,1)S(1)}, u32[]{:S(2)}, u32[]{:S(2)}) async-start(bf16[4,8,2,128,1,16]{3,5,2,0,4,1:T(8,128)(2,1)} %copy.65), calls=%async_computation | async-start | bytes 524288 | tf_op jit(solution)/shard_map/all_to_all | solution.py:69
  19.0 2.6 %copy.62 = f32[3,8192]{0,1:T(8,128)} copy(f32[3,8192]{1,0:T(4,128)S(1)} %copy-done.16) | data formatting | bytes 196608 | tf_op args[2]
  21.6 2.8 %gather_fusion = f32[128,3]{1,0:T(8,128)S(1)} fusion(f32[3,8192]{0,1:T(8,128)} %copy.62, s32[1024]{0:T(1024)S(1)} %pad_clamp_fusion), kind=kCustom, calls=%fused_computation | custom fusion | bytes 3584 | tf_op jit(solution)/shard_map/jit(_take)/gather | solution.py:46
  28.5 6.4 %all-to-all-start.1 = ((bf16[8,128,1,2,104]{1,4,3,2,0:T(8,128)(2,1)}), bf16[8,128,1,2,104]{1,4,3,2,0:T(8,128)(2,1)S(1)}, u32[]{:S(2)}, u32[]{:S(2)}) async-start(bf16[8,128,1,2,104]{1,4,3,2,0:T(8,128)(2,1)} %broadcast_in_dim.58), calls=%async_computation.1 | async-start | bytes 851968 | tf_op jit(solution)/shard_map/all_to_all | solution.py:151
  34.9 3.6 %collective-permute-start = (bf16[4,1,2,128,8,16]{3,5,4,2,0,1:T(8,128)(2,1)S(1)}, bf16[4,1,2,128,8,16]{3,5,4,2,0,1:T(8,128)(2,1)S(1)}, u32[]{:S(2)}, u32[]{:S(2)}) collective-permute-start(bf16[4,1,2,128,8,16]{3,5,4,2,0,1:T(8,128)(2,1)S(1)} %bitcast.338), channel_id=1, source_target_pairs={{0,1},{1,2},{2,3},{3,4},{4,5},{5,6},{6,7},{7,0},{8,9},{9,10},{10,1... | collective-permute-start | bytes 786440 | tf_op jit(solution)/shard_map/ppermute | solution.py:80
  38.5 8.6 %collective-permute-start.4 = (bf16[4,1,2,128,8,16]{3,5,4,2,0,1:T(8,128)(2,1)S(1)}, bf16[4,1,2,128,8,16]{3,5,4,2,0,1:T(8,128)(2,1)S(1)}, u32[]{:S(2)}, u32[]{:S(2)}) collective-permute-start(bf16[4,1,2,128,8,16]{3,5,4,2,0,1:T(8,128)(2,1)S(1)} %bitcast.339), channel_id=1, source_target_pairs={{0,7},{1,0},{2,1},{3,2},{4,3},{5,4},{6,5},{7,6},{8,15},{9,8},{10,9... | collective-permute-start | bytes 786440 | tf_op jit(solution)/shard_map/ppermute | solution.py:83
  49.0 2.6 %collective-permute-done = bf16[4,1,2,128,8,16]{3,5,4,2,0,1:T(8,128)(2,1)S(1)} collective-permute-done((bf16[4,1,2,128,8,16]{3,5,4,2,0,1:T(8,128)(2,1)S(1)}, bf16[4,1,2,128,8,16]{3,5,4,2,0,1:T(8,128)(2,1)S(1)}, u32[]{:S(2)}, u32[]{:S(2)}) %collective-permute-start) | collective-permute-done | bytes 262176 | tf_op jit(solution)/shard_map/ppermute | solution.py:80
  51.6 1.9 collective-permute-start.1
  53.5 5.1 %collective-permute-start.5 = (bf16[4,1,2,128,8,16]{3,5,4,2,0,1:T(8,128)(2,1)S(1)}, bf16[4,1,2,128,8,16]{3,5,4,2,0,1:T(8,128)(2,1)S(1)}, u32[]{:S(2)}, u32[]{:S(2)}) collective-permute-start(bf16[4,1,2,128,8,16]{3,5,4,2,0,1:T(8,128)(2,1)S(1)} %collective-permute-done.4), channel_id=1, source_target_pairs={{0,7},{1,0},{2,1},{3,2},{4,3},{5,4},{6,5},{7,6},{8,15},{9,8},{10,9... | collective-permute-start | bytes 786440 | tf_op jit(solution)/shard_map/ppermute | solution.py:83
  62.3 1.9 collective-permute-start.2
  64.3 5.1 %collective-permute-start.6 = (bf16[4,1,2,128,8,16]{3,5,4,2,0,1:T(8,128)(2,1)S(1)}, bf16[4,1,2,128,8,16]{3,5,4,2,0,1:T(8,128)(2,1)S(1)}, u32[]{:S(2)}, u32[]{:S(2)}) collective-permute-start(bf16[4,1,2,128,8,16]{3,5,4,2,0,1:T(8,128)(2,1)S(1)} %collective-permute-done.5), channel_id=1, source_target_pairs={{0,7},{1,0},{2,1},{3,2},{4,3},{5,4},{6,5},{7,6},{8,15},{9,8},{10,9... | collective-permute-start | bytes 786440 | tf_op jit(solution)/shard_map/ppermute | solution.py:83
  69.6 2.5 collective-permute-done.2
  72.1 1.9 collective-permute-start.3
  75.3 6.3 %collective-permute-done.3 = bf16[4,1,2,128,8,16]{3,5,4,2,0,1:T(8,128)(2,1)S(1)} collective-permute-done((bf16[4,1,2,128,8,16]{3,5,4,2,0,1:T(8,128)(2,1)S(1)}, bf16[4,1,2,128,8,16]{3,5,4,2,0,1:T(8,128)(2,1)S(1)}, u32[]{:S(2)}, u32[]{:S(2)}) %collective-permute-start.3) | collective-permute-done | bytes 262176 | tf_op jit(solution)/shard_map/ppermute | solution.py:80
  86.5 1.8 convolution_convert_fusion.4
  88.3 6.1 %all-to-all-start.2 = ((bf16[1,8,16,768]{3,2,0,1:T(8,128)(2,1)}), bf16[1,8,16,768]{3,2,0,1:T(8,128)(2,1)S(1)}, u32[]{:S(2)}, u32[]{:S(2)}) async-start(bf16[1,8,16,768]{3,2,0,1:T(8,128)(2,1)} %bitcast.76), calls=%async_computation.2 | async-start | bytes 393216 | tf_op jit(solution)/shard_map/all_to_all | solution.py:159
  94.4 10.3 %all-to-all-done.2 = bf16[1,8,16,768]{3,2,0,1:T(8,128)(2,1)S(1)} async-done(((bf16[1,8,16,768]{3,2,0,1:T(8,128)(2,1)}), bf16[1,8,16,768]{3,2,0,1:T(8,128)(2,1)S(1)}, u32[]{:S(2)}, u32[]{:S(2)}) %all-to-all-start.2) | async-done | bytes 196640 | tf_op jit(solution)/shard_map/all_to_all | solution.py:159
  105.5 14.1 %all_to_all.78 = bf16[1,8,16,768]{3,2,0,1:T(8,128)(2,1)S(1)} all-to-all(bf16[1,8,16,768]{3,2,0,1:T(8,128)(2,1)S(1)} %broadcast_in_dim.61), channel_id=1, replica_groups=mesh['row'=8,'col'=8,'smp'=8] {'col'}, dimensions={1} | all-to-all | bytes 393216 | tf_op jit(solution)/shard_map/all_to_all | solution.py:151
  121.6 5.6 %all-to-all-start.4 = ((bf16[8,128,1,2,96]{1,4,3,2,0:T(8,128)(2,1)}), bf16[8,128,1,2,96]{1,4,3,2,0:T(8,128)(2,1)S(1)}, u32[]{:S(2)}, u32[]{:S(2)}) async-start(bf16[8,128,1,2,96]{1,4,3,2,0:T(8,128)(2,1)} %broadcast_in_dim.62), calls=%async_computation.4 | async-start | bytes 786432 | tf_op jit(solution)/shard_map/all_to_all | solution.py:151
  129.5 4.5 %all-to-all-done.4 = bf16[8,128,1,2,96]{1,4,3,2,0:T(8,128)(2,1)S(1)} async-done(((bf16[8,128,1,2,96]{1,4,3,2,0:T(8,128)(2,1)}), bf16[8,128,1,2,96]{1,4,3,2,0:T(8,128)(2,1)S(1)}, u32[]{:S(2)}, u32[]{:S(2)}) %all-to-all-start.4) | async-done | bytes 393248 | tf_op jit(solution)/shard_map/all_to_all | solution.py:151
  136.7 13.6 %all_to_all.79 = bf16[1,8,16,768]{3,2,0,1:T(8,128)(2,1)S(1)} all-to-all(bf16[1,8,16,768]{3,2,0,1:T(8,128)(2,1)S(1)} %bitcast.325), channel_id=1, replica_groups=mesh['row'=8,'col'=8,'smp'=8] {'col'}, dimensions={1} | all-to-all | bytes 393216 | tf_op jit(solution)/shard_map/all_to_all | solution.py:159
  151.5 3.4 %all-to-all-start.6 = ((bf16[1,8,16,768]{3,2,0,1:T(8,128)(2,1)}), bf16[1,8,16,768]{3,2,0,1:T(8,128)(2,1)S(1)}, u32[]{:S(2)}, u32[]{:S(2)}) async-start(bf16[1,8,16,768]{3,2,0,1:T(8,128)(2,1)} %broadcast_in_dim.63), calls=%async_computation.6 | async-start | bytes 393216 | tf_op jit(solution)/shard_map/all_to_all | solution.py:151
  155.5 10.1 %all-to-all-done.6 = bf16[1,8,16,768]{3,2,0,1:T(8,128)(2,1)S(1)} async-done(((bf16[1,8,16,768]{3,2,0,1:T(8,128)(2,1)}), bf16[1,8,16,768]{3,2,0,1:T(8,128)(2,1)S(1)}, u32[]{:S(2)}, u32[]{:S(2)}) %all-to-all-start.6) | async-done | bytes 196640 | tf_op jit(solution)/shard_map/all_to_all | solution.py:151
  167.7 4.5 %all-to-all-start.7 = ((bf16[8,128,1,2,96]{1,4,3,2,0:T(8,128)(2,1)}), bf16[8,128,1,2,96]{1,4,3,2,0:T(8,128)(2,1)S(1)}, u32[]{:S(2)}, u32[]{:S(2)}) async-start(bf16[8,128,1,2,96]{1,4,3,2,0:T(8,128)(2,1)} %broadcast_in_dim.64), calls=%async_computation.7 | async-start | bytes 786432 | tf_op jit(solution)/shard_map/all_to_all | solution.py:151
  174.5 4.6 %all-to-all-done.7 = bf16[8,128,1,2,96]{1,4,3,2,0:T(8,128)(2,1)S(1)} async-done(((bf16[8,128,1,2,96]{1,4,3,2,0:T(8,128)(2,1)}), bf16[8,128,1,2,96]{1,4,3,2,0:T(8,128)(2,1)S(1)}, u32[]{:S(2)}, u32[]{:S(2)}) %all-to-all-start.7) | async-done | bytes 393248 | tf_op jit(solution)/shard_map/all_to_all | solution.py:151
  181.6 13.6 %all_to_all.80 = bf16[1,8,16,768]{3,2,0,1:T(8,128)(2,1)S(1)} all-to-all(bf16[1,8,16,768]{3,2,0,1:T(8,128)(2,1)S(1)} %bitcast.326), channel_id=1, replica_groups=mesh['row'=8,'col'=8,'smp'=8] {'col'}, dimensions={1} | all-to-all | bytes 393216 | tf_op jit(solution)/shard_map/all_to_all | solution.py:159
  196.1 12.7 %all_to_all.81 = bf16[1,8,16,768]{3,2,0,1:T(8,128)(2,1)S(1)} all-to-all(bf16[1,8,16,768]{3,2,0,1:T(8,128)(2,1)S(1)} %broadcast_in_dim.65), channel_id=1, replica_groups=mesh['row'=8,'col'=8,'smp'=8] {'col'}, dimensions={1} | all-to-all | bytes 393216 | tf_op jit(solution)/shard_map/all_to_all | solution.py:151
  210.8 5.1 %all-to-all-start.10 = ((bf16[8,128,1,2,96]{1,4,3,2,0:T(8,128)(2,1)}), bf16[8,128,1,2,96]{1,4,3,2,0:T(8,128)(2,1)S(1)}, u32[]{:S(2)}, u32[]{:S(2)}) async-start(bf16[8,128,1,2,96]{1,4,3,2,0:T(8,128)(2,1)} %broadcast_in_dim.66), calls=%async_computation.10 | async-start | bytes 786432 | tf_op jit(solution)/shard_map/all_to_all | solution.py:151
  218.2 4.6 %all-to-all-done.10 = bf16[8,128,1,2,96]{1,4,3,2,0:T(8,128)(2,1)S(1)} async-done(((bf16[8,128,1,2,96]{1,4,3,2,0:T(8,128)(2,1)}), bf16[8,128,1,2,96]{1,4,3,2,0:T(8,128)(2,1)S(1)}, u32[]{:S(2)}, u32[]{:S(2)}) %all-to-all-start.10) | async-done | bytes 393248 | tf_op jit(solution)/shard_map/all_to_all | solution.py:151
  225.3 13.6 %all_to_all.82 = bf16[1,8,16,768]{3,2,0,1:T(8,128)(2,1)S(1)} all-to-all(bf16[1,8,16,768]{3,2,0,1:T(8,128)(2,1)S(1)} %bitcast.327), channel_id=1, replica_groups=mesh['row'=8,'col'=8,'smp'=8] {'col'}, dimensions={1} | all-to-all | bytes 393216 | tf_op jit(solution)/shard_map/all_to_all | solution.py:159
  239.7 3.4 %all-to-all-start.12 = ((bf16[1,8,16,768]{3,2,0,1:T(8,128)(2,1)}), bf16[1,8,16,768]{3,2,0,1:T(8,128)(2,1)S(1)}, u32[]{:S(2)}, u32[]{:S(2)}) async-start(bf16[1,8,16,768]{3,2,0,1:T(8,128)(2,1)} %broadcast_in_dim.67), calls=%async_computation.12 | async-start | bytes 393216 | tf_op jit(solution)/shard_map/all_to_all | solution.py:151
  243.1 10.7 %all-to-all-done.12 = bf16[1,8,16,768]{3,2,0,1:T(8,128)(2,1)S(1)} async-done(((bf16[1,8,16,768]{3,2,0,1:T(8,128)(2,1)}), bf16[1,8,16,768]{3,2,0,1:T(8,128)(2,1)S(1)}, u32[]{:S(2)}, u32[]{:S(2)}) %all-to-all-start.12) | async-done | bytes 196640 | tf_op jit(solution)/shard_map/all_to_all | solution.py:151
  (209 shorter events, 48.8 us)
Async XLA Ops:
  2.0 11.7 %copy-start.33 = (s32[128]{0:T(128)S(1)}, s32[128]{0:T(128)}, u32[]{:S(2)}) copy-start(s32[128]{0:T(128)} %param.20) | copy-start | bytes 1540
  2.0 11.7 %copy-start.23 = (f32[1,3]{1,0:T(1,128)S(1)}, f32[1,3]{1,0:T(1,128)}, u32[]{:S(2)}) copy-start(f32[1,3]{1,0:T(1,128)} %param.23) | copy-start | bytes 40
  2.1 16.8 %copy-start.16 = (f32[3,8192]{1,0:T(4,128)S(1)}, f32[3,8192]{1,0:T(4,128)}, u32[]{:S(2)}) copy-start(f32[3,8192]{1,0:T(4,128)} %param.19) | copy-start | bytes 294916
  6.8 20.9 %all-to-all-start = ((bf16[4,8,2,128,1,16]{3,5,2,0,4,1:T(8,128)(2,1)}), bf16[4,8,2,128,1,16]{3,5,2,0,4,1:T(8,128)(2,1)S(1)}, u32[]{:S(2)}, u32[]{:S(2)}) async-start(bf16[4,8,2,128,1,16]{3,5,2,0,4,1:T(8,128)(2,1)} %copy.65), calls=%async_computation | async-start | bytes 524288 | tf_op jit(solution)/shard_map/all_to_all | solution.py:69
  18.9 7.4 %copy-start.24 = (s32[128]{0:T(128)S(1)}, s32[128]{0:T(128)}, u32[]{:S(2)}) copy-start(s32[128]{0:T(128)} %param.21) | copy-start | bytes 1540
  18.9 7.4 %copy-start.32 = (s32[128]{0:T(128)S(1)}, s32[128]{0:T(128)}, u32[]{:S(2)}) copy-start(s32[128]{0:T(128)} %param.22) | copy-start | bytes 1540
  25.1 23.3 %copy-start.25 = (f32[4,16]{1,0:T(4,128)S(1)}, f32[4,16]{1,0:T(4,128)}, u32[]{:S(2)}) copy-start(f32[4,16]{1,0:T(4,128)} %param.28) | copy-start | bytes 772
  28.5 40.9 %all-to-all-start.1 = ((bf16[8,128,1,2,104]{1,4,3,2,0:T(8,128)(2,1)}), bf16[8,128,1,2,104]{1,4,3,2,0:T(8,128)(2,1)S(1)}, u32[]{:S(2)}, u32[]{:S(2)}) async-start(bf16[8,128,1,2,104]{1,4,3,2,0:T(8,128)(2,1)} %broadcast_in_dim.58), calls=%async_computation.1 | async-start | bytes 851968 | tf_op jit(solution)/shard_map/all_to_all | solution.py:151
  34.9 16.7 %collective-permute-start = (bf16[4,1,2,128,8,16]{3,5,4,2,0,1:T(8,128)(2,1)S(1)}, bf16[4,1,2,128,8,16]{3,5,4,2,0,1:T(8,128)(2,1)S(1)}, u32[]{:S(2)}, u32[]{:S(2)}) collective-permute-start(bf16[4,1,2,128,8,16]{3,5,4,2,0,1:T(8,128)(2,1)S(1)} %bitcast.338), channel_id=1, source_target_pairs={{0,1},{1,2},{2,3},{3,4},{4,5},{5,6},{6,7},{7,0},{8,9},{9,10},{10,1... | collective-permute-start | bytes 786440 | tf_op jit(solution)/shard_map/ppermute | solution.py:80
  38.5 15.0 %collective-permute-start.4 = (bf16[4,1,2,128,8,16]{3,5,4,2,0,1:T(8,128)(2,1)S(1)}, bf16[4,1,2,128,8,16]{3,5,4,2,0,1:T(8,128)(2,1)S(1)}, u32[]{:S(2)}, u32[]{:S(2)}) collective-permute-start(bf16[4,1,2,128,8,16]{3,5,4,2,0,1:T(8,128)(2,1)S(1)} %bitcast.339), channel_id=1, source_target_pairs={{0,7},{1,0},{2,1},{3,2},{4,3},{5,4},{6,5},{7,6},{8,15},{9,8},{10,9... | collective-permute-start | bytes 786440 | tf_op jit(solution)/shard_map/ppermute | solution.py:83
  51.6 10.7 %collective-permute-start.1 = (bf16[4,1,2,128,8,16]{3,5,4,2,0,1:T(8,128)(2,1)S(1)}, bf16[4,1,2,128,8,16]{3,5,4,2,0,1:T(8,128)(2,1)S(1)}, u32[]{:S(2)}, u32[]{:S(2)}) collective-permute-start(bf16[4,1,2,128,8,16]{3,5,4,2,0,1:T(8,128)(2,1)S(1)} %collective-permute-done), channel_id=1, source_target_pairs={{0,1},{1,2},{2,3},{3,4},{4,5},{5,6},{6,7},{7,0},{8,9},{9,10},{10,1... | collective-permute-start | bytes 786440 | tf_op jit(solution)/shard_map/ppermute | solution.py:80
  53.5 10.7 %collective-permute-start.5 = (bf16[4,1,2,128,8,16]{3,5,4,2,0,1:T(8,128)(2,1)S(1)}, bf16[4,1,2,128,8,16]{3,5,4,2,0,1:T(8,128)(2,1)S(1)}, u32[]{:S(2)}, u32[]{:S(2)}) collective-permute-start(bf16[4,1,2,128,8,16]{3,5,4,2,0,1:T(8,128)(2,1)S(1)} %collective-permute-done.4), channel_id=1, source_target_pairs={{0,7},{1,0},{2,1},{3,2},{4,3},{5,4},{6,5},{7,6},{8,15},{9,8},{10,9... | collective-permute-start | bytes 786440 | tf_op jit(solution)/shard_map/ppermute | solution.py:83
  62.3 9.8 %collective-permute-start.2 = (bf16[4,1,2,128,8,16]{3,5,4,2,0,1:T(8,128)(2,1)S(1)}, bf16[4,1,2,128,8,16]{3,5,4,2,0,1:T(8,128)(2,1)S(1)}, u32[]{:S(2)}, u32[]{:S(2)}) collective-permute-start(bf16[4,1,2,128,8,16]{3,5,4,2,0,1:T(8,128)(2,1)S(1)} %collective-permute-done.1), channel_id=1, source_target_pairs={{0,1},{1,2},{2,3},{3,4},{4,5},{5,6},{6,7},{7,0},{8,9},{9,10},{10,1... | collective-permute-start | bytes 786440 | tf_op jit(solution)/shard_map/ppermute | solution.py:80
  64.3 17.7 %collective-permute-start.6 = (bf16[4,1,2,128,8,16]{3,5,4,2,0,1:T(8,128)(2,1)S(1)}, bf16[4,1,2,128,8,16]{3,5,4,2,0,1:T(8,128)(2,1)S(1)}, u32[]{:S(2)}, u32[]{:S(2)}) collective-permute-start(bf16[4,1,2,128,8,16]{3,5,4,2,0,1:T(8,128)(2,1)S(1)} %collective-permute-done.5), channel_id=1, source_target_pairs={{0,7},{1,0},{2,1},{3,2},{4,3},{5,4},{6,5},{7,6},{8,15},{9,8},{10,9... | collective-permute-start | bytes 786440 | tf_op jit(solution)/shard_map/ppermute | solution.py:83
  72.1 9.5 %collective-permute-start.3 = (bf16[4,1,2,128,8,16]{3,5,4,2,0,1:T(8,128)(2,1)S(1)}, bf16[4,1,2,128,8,16]{3,5,4,2,0,1:T(8,128)(2,1)S(1)}, u32[]{:S(2)}, u32[]{:S(2)}) collective-permute-start(bf16[4,1,2,128,8,16]{3,5,4,2,0,1:T(8,128)(2,1)S(1)} %collective-permute-done.2), channel_id=1, source_target_pairs={{0,1},{1,2},{2,3},{3,4},{4,5},{5,6},{6,7},{7,0},{8,9},{9,10},{10,1... | collective-permute-start | bytes 786440 | tf_op jit(solution)/shard_map/ppermute | solution.py:80
  88.3 16.4 %all-to-all-start.2 = ((bf16[1,8,16,768]{3,2,0,1:T(8,128)(2,1)}), bf16[1,8,16,768]{3,2,0,1:T(8,128)(2,1)S(1)}, u32[]{:S(2)}, u32[]{:S(2)}) async-start(bf16[1,8,16,768]{3,2,0,1:T(8,128)(2,1)} %bitcast.76), calls=%async_computation.2 | async-start | bytes 393216 | tf_op jit(solution)/shard_map/all_to_all | solution.py:159
  119.6 7.7 %copy-start.4 = (bf16[1,8,16,768]{3,2,0,1:T(8,128)(2,1)}, bf16[1,8,16,768]{3,2,0,1:T(8,128)(2,1)S(1)}, u32[]{:S(2)}) copy-start(bf16[1,8,16,768]{3,2,0,1:T(8,128)(2,1)S(1)} %all_to_all.78) | copy-start | bytes 589828
  121.6 12.4 %all-to-all-start.4 = ((bf16[8,128,1,2,96]{1,4,3,2,0:T(8,128)(2,1)}), bf16[8,128,1,2,96]{1,4,3,2,0:T(8,128)(2,1)S(1)}, u32[]{:S(2)}, u32[]{:S(2)}) async-start(bf16[8,128,1,2,96]{1,4,3,2,0:T(8,128)(2,1)} %broadcast_in_dim.62), calls=%async_computation.4 | async-start | bytes 786432 | tf_op jit(solution)/shard_map/all_to_all | solution.py:151
  134.7 15.6 %copy-start.11 = (bf16[16,768]{1,0:T(8,128)(2,1)S(1)}, bf16[16,768]{1,0:T(8,128)(2,1)}, u32[]{:S(2)}) copy-start(bf16[16,768]{1,0:T(8,128)(2,1)} %copy-done.10) | copy-start | bytes 73732
  134.7 20.1 %copy-start.26 = (f32[1,16]{1,0:T(1,128)S(1)}, f32[1,16]{1,0:T(1,128)}, u32[]{:S(2)}) copy-start(f32[1,16]{1,0:T(1,128)} %get-tuple-element.45) | copy-start | bytes 196
  134.7 20.1 %copy-start.27 = (f32[1,16]{1,0:T(1,128)S(1)}, f32[1,16]{1,0:T(1,128)}, u32[]{:S(2)}) copy-start(f32[1,16]{1,0:T(1,128)} %get-tuple-element.48) | copy-start | bytes 196
  135.4 36.8 %copy-start.1 = (bf16[2,128,8,8,16]{1,4,3,2,0:T(8,128)(2,1)S(1)}, bf16[2,128,8,8,16]{1,4,3,2,0:T(8,128)(2,1)}, u32[]{:S(2)}) copy-start(bf16[2,128,8,8,16]{1,4,3,2,0:T(8,128)(2,1)} %get-tuple-element.33) | copy-start | bytes 1572868
  135.4 36.8 %copy-start.2 = (bf16[2,128,8,8,16]{1,4,3,2,0:T(8,128)(2,1)S(1)}, bf16[2,128,8,8,16]{1,4,3,2,0:T(8,128)(2,1)}, u32[]{:S(2)}) copy-start(bf16[2,128,8,8,16]{1,4,3,2,0:T(8,128)(2,1)} %get-tuple-element.34) | copy-start | bytes 1572868
  151.5 14.2 %all-to-all-start.6 = ((bf16[1,8,16,768]{3,2,0,1:T(8,128)(2,1)}), bf16[1,8,16,768]{3,2,0,1:T(8,128)(2,1)S(1)}, u32[]{:S(2)}, u32[]{:S(2)}) async-start(bf16[1,8,16,768]{3,2,0,1:T(8,128)(2,1)} %broadcast_in_dim.63), calls=%async_computation.6 | async-start | bytes 393216 | tf_op jit(solution)/shard_map/all_to_all | solution.py:151
  167.7 11.4 %all-to-all-start.7 = ((bf16[8,128,1,2,96]{1,4,3,2,0:T(8,128)(2,1)}), bf16[8,128,1,2,96]{1,4,3,2,0:T(8,128)(2,1)S(1)}, u32[]{:S(2)}, u32[]{:S(2)}) async-start(bf16[8,128,1,2,96]{1,4,3,2,0:T(8,128)(2,1)} %broadcast_in_dim.64), calls=%async_computation.7 | async-start | bytes 786432 | tf_op jit(solution)/shard_map/all_to_all | solution.py:151
  179.7 15.5 %copy-start.9 = (bf16[16,768]{1,0:T(8,128)(2,1)S(1)}, bf16[16,768]{1,0:T(8,128)(2,1)}, u32[]{:S(2)}) copy-start(bf16[16,768]{1,0:T(8,128)(2,1)} %copy-done.8) | copy-start | bytes 73732
  208.8 7.2 %copy-start.6 = (bf16[1,8,16,768]{3,2,0,1:T(8,128)(2,1)}, bf16[1,8,16,768]{3,2,0,1:T(8,128)(2,1)S(1)}, u32[]{:S(2)}) copy-start(bf16[1,8,16,768]{3,2,0,1:T(8,128)(2,1)S(1)} %all_to_all.81) | copy-start | bytes 589828
  210.8 12.0 %all-to-all-start.10 = ((bf16[8,128,1,2,96]{1,4,3,2,0:T(8,128)(2,1)}), bf16[8,128,1,2,96]{1,4,3,2,0:T(8,128)(2,1)S(1)}, u32[]{:S(2)}, u32[]{:S(2)}) async-start(bf16[8,128,1,2,96]{1,4,3,2,0:T(8,128)(2,1)} %broadcast_in_dim.66), calls=%async_computation.10 | async-start | bytes 786432 | tf_op jit(solution)/shard_map/all_to_all | solution.py:151
  223.4 15.5 %copy-start.13 = (bf16[16,768]{1,0:T(8,128)(2,1)S(1)}, bf16[16,768]{1,0:T(8,128)(2,1)}, u32[]{:S(2)}) copy-start(bf16[16,768]{1,0:T(8,128)(2,1)} %copy-done.12) | copy-start | bytes 73732
  223.7 30.7 %copy-start.21 = (f32[1,3,128]{2,1,0:T(4,128)S(1)}, f32[1,3,128]{2,1,0:T(4,128)}, u32[]{:S(2)}) copy-start(f32[1,3,128]{2,1,0:T(4,128)} %get-tuple-element.32) | copy-start | bytes 4612
  223.8 30.7 %copy-start.22 = (bf16[3,768]{1,0:T(4,128)(2,1)S(1)}, bf16[3,768]{1,0:T(4,128)(2,1)}, u32[]{:S(2)}) copy-start(bf16[3,768]{1,0:T(4,128)(2,1)} %param.31) | copy-start | bytes 13828
  239.7 14.2 %all-to-all-start.12 = ((bf16[1,8,16,768]{3,2,0,1:T(8,128)(2,1)}), bf16[1,8,16,768]{3,2,0,1:T(8,128)(2,1)S(1)}, u32[]{:S(2)}, u32[]{:S(2)}) async-start(bf16[1,8,16,768]{3,2,0,1:T(8,128)(2,1)} %broadcast_in_dim.67), calls=%async_computation.12 | async-start | bytes 393216 | tf_op jit(solution)/shard_map/all_to_all | solution.py:151
  (17 other events, 77.0 us)
